TPU v7x, 32 devices: a whole 2x2x4 slice. The times are simulated.
32 devices in a mesh: grp: 4 (over y, x), sta: 8 (over z, core).
Axes of the slice: x: 2, y: 2, z: 4, core: 2. Of those that a mesh axis runs over, the one named last changes fastest.
Arguments:
- spectra: float32 [256, 2, 18432], P(('grp', 'sta')), may hold values from -61 to 61
- stacks: float32 [3072, 1601], P(('grp', 'sta')), may hold values from -6 to 6
- pair_sta: int32 [2, 3072], P(None, ('grp', 'sta')), may hold values from 0 to 63
- pair_valid: int32 [3072], P(('grp', 'sta')), may hold values 0 or 1
- owner: int32 [3072, 1], P(('grp', 'sta')), may hold values from 0 to 31; in each aligned block of 96 rows (0 to 95, 96 to 191, ...) at most 4 rows name the same one
- slot: int32 [3072], P(('grp', 'sta')), may hold values from 0 to 95
Outputs:
- stacks_new: float32 [3072, 1601], P(('grp', 'sta'))
Inputs may be any that keep to these rules, and one draw needn't show every extreme that they name: Among the 96 rows of one device no owner is named more than 4 times.
All inputs are finite; a program needn't handle non-finite values. No bound on the sum of `pair_valid` on one device may be relied on, other than what follows from the above.
Results may differ from a plain program's by a relative error of at most 0.0041.
Values may be sent and summed in bfloat16 or wider, within the bound.
No kernel may reach another device: no remote copies, remote signals or barrier semaphores. Data moves between devices by JAX's collectives and lax.ppermute only.
A program may use at most 128 MiB of HBM per device.

v0:
```python
import math

import jax
import jax.numpy as jnp
from jax import lax
from jax.sharding import PartitionSpec as P

BAND = 64


def whiten(spectra):
    shape = spectra.shape
    split = spectra.reshape(shape[0], 2, shape[2] // BAND, BAND)
    power = jnp.mean(split * split, axis=(1, 3), keepdims=True)
    return (split * lax.rsqrt(power + 1e-06)).reshape(shape).astype(jnp.bfloat16)


def table_block(start, width, lag_count, total_bins):
    freqs = start + lax.iota(jnp.int32, width)
    shifts = lax.iota(jnp.int32, lag_count) - (lag_count - 1) // 2
    angle_ids = jnp.mod(freqs[:, None] * shifts[None, :], 2 * total_bins)
    theta = angle_ids.astype(jnp.float32) * jnp.float32(math.pi / total_bins)
    return (jnp.cos(theta).astype(jnp.bfloat16), (-jnp.sin(theta)).astype(jnp.bfloat16))


def local(spectra, stacks, pair_sta, pair_valid, owner, slot):
    total_bins = spectra.shape[2]
    lag_count = stacks.shape[1]
    stack_rows = stacks.shape[0]
    pair_count = pair_sta.shape[1]
    groups = lax.axis_size("grp")
    members = lax.axis_size("sta")
    devices = groups * members
    capacity = max(2, (4 * pair_count + 3 * devices - 1) // (3 * devices))
    whitened = whiten(spectra)
    gathered = lax.all_gather(whitened, "sta", axis=0, tiled=True)
    first = jnp.take(gathered, pair_sta[0], axis=0)
    second = jnp.take(gathered, pair_sta[1], axis=0)
    fblock = 2048

    def add_block(index, total):
        start = index * fblock
        left = lax.dynamic_slice_in_dim(first, start, fblock, 2).astype(jnp.float32)
        right = lax.dynamic_slice_in_dim(second, start, fblock, 2).astype(jnp.float32)
        real_part = (left[:, 0] * right[:, 0] + left[:, 1] * right[:, 1]).astype(jnp.bfloat16)
        imag_part = (left[:, 1] * right[:, 0] - left[:, 0] * right[:, 1]).astype(jnp.bfloat16)
        cosines, sines = table_block(start, fblock, lag_count, total_bins)
        total = total + jnp.dot(real_part, cosines, preferred_element_type=jnp.float32)
        return total + jnp.dot(imag_part, sines, preferred_element_type=jnp.float32)

    corr = lax.fori_loop(
        0, total_bins // fblock, add_block, jnp.zeros((pair_count, lag_count), jnp.float32)
    )
    corr = corr * jnp.float32(total_bins ** (-0.5)) * pair_valid.astype(jnp.float32)[:, None]
    dest = owner[:, 0]
    dest_hot = (dest[:, None] == lax.iota(jnp.int32, devices)[None, :]).astype(jnp.int32)
    before = jnp.cumsum(dest_hot, axis=0) - dest_hot
    position = jnp.sum(before * dest_hot, axis=1)
    flat = dest * capacity + position
    placing = (flat[:, None] == lax.iota(jnp.int32, devices * capacity)[None, :]).astype(
        jnp.float32
    )
    send_rows = jnp.dot(placing.T, corr, precision=lax.Precision.HIGHEST)
    send_slots = jnp.dot(
        placing.T, slot.astype(jnp.float32)[:, None], precision=lax.Precision.HIGHEST
    )[:, 0]
    got_rows, got_slots = (
        lax.all_to_all(
            send_rows.reshape(devices, capacity, lag_count),
            ("grp", "sta"),
            split_axis=0,
            concat_axis=0,
            tiled=True,
        ),
        lax.all_to_all(
            send_slots.reshape(devices, capacity),
            ("grp", "sta"),
            split_axis=0,
            concat_axis=0,
            tiled=True,
        ),
    )
    got_rows = got_rows.reshape(devices * capacity, lag_count)
    got_slots = got_slots.reshape(devices * capacity)
    adding = (
        got_slots[None, :] == lax.iota(jnp.int32, stack_rows).astype(jnp.float32)[:, None]
    ).astype(jnp.float32)
    return stacks + jnp.dot(adding, got_rows, precision=lax.Precision.HIGHEST)


def solution(mesh):
    return jax.shard_map(
        local,
        mesh=mesh,
        in_specs=(
            P(("grp", "sta"), None, None),
            P(("grp", "sta"), None),
            P(None, ("grp", "sta")),
            P(("grp", "sta")),
            P(("grp", "sta"), None),
            P(("grp", "sta")),
        ),
        out_specs=P(("grp", "sta"), None),
        check_vma=False,
    )
```

profile of v0, /device:TPU:0, one launch (start us, length us, event | category | flops | bytes accessed | tf_op | source)
XLA Modules:
  0.0 1176.4 jit_solution(17567279320542674453)
XLA Ops:
  21.6 45.2 %all-gather.2.cloned.1.call-done = bf16[64,2,18432]{2,1,0:T(2,128)(2,1)} async-done(((bf16[8,2,18432]{2,1,0:T(2,128)(2,1)}), bf16[64,2,18432]{2,1,0:T(2,128)(2,1)}) %all-gather.2.cloned.1.call-update) | async-done | bytes 4718608 | tf_op jit(solution)/shard_map/all_gather | solution.py:36
  66.8 19.2 %gather_fusion = bf16[96,2,18432]{2,1,0:T(2,128)(2,1)} fusion(bf16[64,2,18432]{2,1,0:T(2,128)(2,1)} %all-gather.2.cloned.1.call-done, s32[1024]{0:T(1024)S(1)} %pad_clamp_fusion.1), kind=kCustom, calls=%fused_computation.clone | custom fusion | bytes 14156160 | tf_op jit(solution)/shard_map/jit(_take)/gather | solution.py:37
  86.0 19.3 %gather_fusion.1 = bf16[96,2,18432]{2,1,0:T(2,128)(2,1)} fusion(bf16[64,2,18432]{2,1,0:T(2,128)(2,1)} %all-gather.2.cloned.1.call-done, s32[1024]{0:T(1024)S(1)} %pad_clamp_fusion), kind=kCustom, calls=%fused_computation.1.clone | custom fusion | bytes 14156160 | tf_op jit(solution)/shard_map/jit(_take)/gather | solution.py:38
  105.3 16.3 %broadcast_select_fusion = (bf16[96,2,18432]{2,1,0:T(2,128)(2,1)}, bf16[96,2,18432]{2,1,0:T(2,128)(2,1)}) fusion(bf16[96,2,18432]{2,1,0:T(2,128)(2,1)} %gather_fusion.1, pred[96]{0:T(512)(128)(4,1)S(1)} %get-tuple-element.150, bf16[96,2,18432]{2,1,0:T(2,128)(2,1)} %gather_fusion, pred[96]{0:T(512)(128)(4,1)S(1)} %get-tuple-element.156), kind=kLoop, calls=%fused_computation.31 | loop fusion | flops 7077888 | bytes 28311744 | tf_op jit(solution)/shard_map/jit(_take)/select_n | solution.py:38
  121.6 1016.4 %while.16 = (s32[]{:T(128)}, f32[96,1601]{1,0:T(8,128)}, bf16[96,2,18432]{2,1,0:T(2,128)(2,1)}, bf16[96,2,18432]{2,1,0:T(2,128)(2,1)}, s32[]{:T(128)}, /*index=5*/s32[]{:T(128)}, s32[]{:T(128)}, s32[]{:T(128)}) while((s32[]{:T(128)}, f32[96,1601]{1,0:T(8,128)}, bf16[96,2,18432]{2,1,0:T(2,128)(2,1)}, ...), condition=%wide.region_5.7_spmd.clone, body=%wide.region_4.6_spmd.clone.sunk | while | flops 1330757632 | bytes 16658849 | solution.py:51
  145.6 52.5 %fusion.43 = f32[96,1601]{1,0:T(8,128)S(1)} fusion(s32[1601]{0:T(1024)S(1)} %iota_add_fusion.4, s32[2048]{0:T(1024)S(1)} %iota_add_fusion.5, f32[96,1601]{1,0:T(8,128)} %get-tuple-element.198, f32[96,2,2048]{2,0,1:T(8,128)S(1)} %copy_convert_fusion.4, f32[96,2,2048]{2,0,1:T(8,128)S(1)} %copy_convert_fusion.5, pred[]{:T(512)S(6)} %compare.3), kind=kOutput, calls=%fused_computation.14.clone.3 | convolution fusion | flops 663421184 | bytes 4389893 | tf_op jit(solution)/shard_map/while/body/eval_jaxpr/dot_general | solution.py:48
  198.1 54.1 %fusion.44 = f32[96,1601]{1,0:T(8,128)} fusion(f32[96,1601]{1,0:T(8,128)S(1)} %fusion.43, s32[1601]{0:T(1024)S(1)} %iota_add_fusion.4, s32[2048]{0:T(1024)S(1)} %iota_add_fusion.5, f32[96,2,2048]{2,0,1:T(8,128)S(1)} %copy_convert_fusion.4, f32[96,2,2048]{2,0,1:T(8,128)S(1)} %copy_convert_fusion.5), kind=kOutput, calls=%fused_computation.13.clone.3 | convolution fusion | flops 666546304 | bytes 4389892 | tf_op jit(solution)/shard_map/while/body/eval_jaxpr/dot_general | solution.py:49
  255.3 53.6 %fusion.43 = f32[96,1601]{1,0:T(8,128)S(1)} fusion(s32[1601]{0:T(1024)S(1)} %iota_add_fusion.4, s32[2048]{0:T(1024)S(1)} %iota_add_fusion.5, f32[96,1601]{1,0:T(8,128)} %get-tuple-element.198, f32[96,2,2048]{2,0,1:T(8,128)S(1)} %copy_convert_fusion.4, f32[96,2,2048]{2,0,1:T(8,128)S(1)} %copy_convert_fusion.5, pred[]{:T(512)S(6)} %compare.3), kind=kOutput, calls=%fused_computation.14.clone.3 | convolution fusion | flops 663421184 | bytes 4389893 | tf_op jit(solution)/shard_map/while/body/eval_jaxpr/dot_general | solution.py:48
  308.8 54.1 %fusion.44 = f32[96,1601]{1,0:T(8,128)} fusion(f32[96,1601]{1,0:T(8,128)S(1)} %fusion.43, s32[1601]{0:T(1024)S(1)} %iota_add_fusion.4, s32[2048]{0:T(1024)S(1)} %iota_add_fusion.5, f32[96,2,2048]{2,0,1:T(8,128)S(1)} %copy_convert_fusion.4, f32[96,2,2048]{2,0,1:T(8,128)S(1)} %copy_convert_fusion.5), kind=kOutput, calls=%fused_computation.13.clone.3 | convolution fusion | flops 666546304 | bytes 4389892 | tf_op jit(solution)/shard_map/while/body/eval_jaxpr/dot_general | solution.py:49
  366.0 53.6 %fusion.43 = f32[96,1601]{1,0:T(8,128)S(1)} fusion(s32[1601]{0:T(1024)S(1)} %iota_add_fusion.4, s32[2048]{0:T(1024)S(1)} %iota_add_fusion.5, f32[96,1601]{1,0:T(8,128)} %get-tuple-element.198, f32[96,2,2048]{2,0,1:T(8,128)S(1)} %copy_convert_fusion.4, f32[96,2,2048]{2,0,1:T(8,128)S(1)} %copy_convert_fusion.5, pred[]{:T(512)S(6)} %compare.3), kind=kOutput, calls=%fused_computation.14.clone.3 | convolution fusion | flops 663421184 | bytes 4389893 | tf_op jit(solution)/shard_map/while/body/eval_jaxpr/dot_general | solution.py:48
  419.5 54.1 %fusion.44 = f32[96,1601]{1,0:T(8,128)} fusion(f32[96,1601]{1,0:T(8,128)S(1)} %fusion.43, s32[1601]{0:T(1024)S(1)} %iota_add_fusion.4, s32[2048]{0:T(1024)S(1)} %iota_add_fusion.5, f32[96,2,2048]{2,0,1:T(8,128)S(1)} %copy_convert_fusion.4, f32[96,2,2048]{2,0,1:T(8,128)S(1)} %copy_convert_fusion.5), kind=kOutput, calls=%fused_computation.13.clone.3 | convolution fusion | flops 666546304 | bytes 4389892 | tf_op jit(solution)/shard_map/while/body/eval_jaxpr/dot_general | solution.py:49
  476.7 53.6 %fusion.43 = f32[96,1601]{1,0:T(8,128)S(1)} fusion(s32[1601]{0:T(1024)S(1)} %iota_add_fusion.4, s32[2048]{0:T(1024)S(1)} %iota_add_fusion.5, f32[96,1601]{1,0:T(8,128)} %get-tuple-element.198, f32[96,2,2048]{2,0,1:T(8,128)S(1)} %copy_convert_fusion.4, f32[96,2,2048]{2,0,1:T(8,128)S(1)} %copy_convert_fusion.5, pred[]{:T(512)S(6)} %compare.3), kind=kOutput, calls=%fused_computation.14.clone.3 | convolution fusion | flops 663421184 | bytes 4389893 | tf_op jit(solution)/shard_map/while/body/eval_jaxpr/dot_general | solution.py:48
  530.2 54.1 %fusion.44 = f32[96,1601]{1,0:T(8,128)} fusion(f32[96,1601]{1,0:T(8,128)S(1)} %fusion.43, s32[1601]{0:T(1024)S(1)} %iota_add_fusion.4, s32[2048]{0:T(1024)S(1)} %iota_add_fusion.5, f32[96,2,2048]{2,0,1:T(8,128)S(1)} %copy_convert_fusion.4, f32[96,2,2048]{2,0,1:T(8,128)S(1)} %copy_convert_fusion.5), kind=kOutput, calls=%fused_computation.13.clone.3 | convolution fusion | flops 666546304 | bytes 4389892 | tf_op jit(solution)/shard_map/while/body/eval_jaxpr/dot_general | solution.py:49
  587.4 53.6 %fusion.43 = f32[96,1601]{1,0:T(8,128)S(1)} fusion(s32[1601]{0:T(1024)S(1)} %iota_add_fusion.4, s32[2048]{0:T(1024)S(1)} %iota_add_fusion.5, f32[96,1601]{1,0:T(8,128)} %get-tuple-element.198, f32[96,2,2048]{2,0,1:T(8,128)S(1)} %copy_convert_fusion.4, f32[96,2,2048]{2,0,1:T(8,128)S(1)} %copy_convert_fusion.5, pred[]{:T(512)S(6)} %compare.3), kind=kOutput, calls=%fused_computation.14.clone.3 | convolution fusion | flops 663421184 | bytes 4389893 | tf_op jit(solution)/shard_map/while/body/eval_jaxpr/dot_general | solution.py:48
  641.0 54.1 %fusion.44 = f32[96,1601]{1,0:T(8,128)} fusion(f32[96,1601]{1,0:T(8,128)S(1)} %fusion.43, s32[1601]{0:T(1024)S(1)} %iota_add_fusion.4, s32[2048]{0:T(1024)S(1)} %iota_add_fusion.5, f32[96,2,2048]{2,0,1:T(8,128)S(1)} %copy_convert_fusion.4, f32[96,2,2048]{2,0,1:T(8,128)S(1)} %copy_convert_fusion.5), kind=kOutput, calls=%fused_computation.13.clone.3 | convolution fusion | flops 666546304 | bytes 4389892 | tf_op jit(solution)/shard_map/while/body/eval_jaxpr/dot_general | solution.py:49
  698.1 53.6 %fusion.43 = f32[96,1601]{1,0:T(8,128)S(1)} fusion(s32[1601]{0:T(1024)S(1)} %iota_add_fusion.4, s32[2048]{0:T(1024)S(1)} %iota_add_fusion.5, f32[96,1601]{1,0:T(8,128)} %get-tuple-element.198, f32[96,2,2048]{2,0,1:T(8,128)S(1)} %copy_convert_fusion.4, f32[96,2,2048]{2,0,1:T(8,128)S(1)} %copy_convert_fusion.5, pred[]{:T(512)S(6)} %compare.3), kind=kOutput, calls=%fused_computation.14.clone.3 | convolution fusion | flops 663421184 | bytes 4389893 | tf_op jit(solution)/shard_map/while/body/eval_jaxpr/dot_general | solution.py:48
  751.7 54.1 %fusion.44 = f32[96,1601]{1,0:T(8,128)} fusion(f32[96,1601]{1,0:T(8,128)S(1)} %fusion.43, s32[1601]{0:T(1024)S(1)} %iota_add_fusion.4, s32[2048]{0:T(1024)S(1)} %iota_add_fusion.5, f32[96,2,2048]{2,0,1:T(8,128)S(1)} %copy_convert_fusion.4, f32[96,2,2048]{2,0,1:T(8,128)S(1)} %copy_convert_fusion.5), kind=kOutput, calls=%fused_computation.13.clone.3 | convolution fusion | flops 666546304 | bytes 4389892 | tf_op jit(solution)/shard_map/while/body/eval_jaxpr/dot_general | solution.py:49
  808.8 53.6 %fusion.43 = f32[96,1601]{1,0:T(8,128)S(1)} fusion(s32[1601]{0:T(1024)S(1)} %iota_add_fusion.4, s32[2048]{0:T(1024)S(1)} %iota_add_fusion.5, f32[96,1601]{1,0:T(8,128)} %get-tuple-element.198, f32[96,2,2048]{2,0,1:T(8,128)S(1)} %copy_convert_fusion.4, f32[96,2,2048]{2,0,1:T(8,128)S(1)} %copy_convert_fusion.5, pred[]{:T(512)S(6)} %compare.3), kind=kOutput, calls=%fused_computation.14.clone.3 | convolution fusion | flops 663421184 | bytes 4389893 | tf_op jit(solution)/shard_map/while/body/eval_jaxpr/dot_general | solution.py:48
  862.4 54.1 %fusion.44 = f32[96,1601]{1,0:T(8,128)} fusion(f32[96,1601]{1,0:T(8,128)S(1)} %fusion.43, s32[1601]{0:T(1024)S(1)} %iota_add_fusion.4, s32[2048]{0:T(1024)S(1)} %iota_add_fusion.5, f32[96,2,2048]{2,0,1:T(8,128)S(1)} %copy_convert_fusion.4, f32[96,2,2048]{2,0,1:T(8,128)S(1)} %copy_convert_fusion.5), kind=kOutput, calls=%fused_computation.13.clone.3 | convolution fusion | flops 666546304 | bytes 4389892 | tf_op jit(solution)/shard_map/while/body/eval_jaxpr/dot_general | solution.py:49
  919.5 53.6 %fusion.43 = f32[96,1601]{1,0:T(8,128)S(1)} fusion(s32[1601]{0:T(1024)S(1)} %iota_add_fusion.4, s32[2048]{0:T(1024)S(1)} %iota_add_fusion.5, f32[96,1601]{1,0:T(8,128)} %get-tuple-element.198, f32[96,2,2048]{2,0,1:T(8,128)S(1)} %copy_convert_fusion.4, f32[96,2,2048]{2,0,1:T(8,128)S(1)} %copy_convert_fusion.5, pred[]{:T(512)S(6)} %compare.3), kind=kOutput, calls=%fused_computation.14.clone.3 | convolution fusion | flops 663421184 | bytes 4389893 | tf_op jit(solution)/shard_map/while/body/eval_jaxpr/dot_general | solution.py:48
  973.1 54.1 %fusion.44 = f32[96,1601]{1,0:T(8,128)} fusion(f32[96,1601]{1,0:T(8,128)S(1)} %fusion.43, s32[1601]{0:T(1024)S(1)} %iota_add_fusion.4, s32[2048]{0:T(1024)S(1)} %iota_add_fusion.5, f32[96,2,2048]{2,0,1:T(8,128)S(1)} %copy_convert_fusion.4, f32[96,2,2048]{2,0,1:T(8,128)S(1)} %copy_convert_fusion.5), kind=kOutput, calls=%fused_computation.13.clone.3 | convolution fusion | flops 666546304 | bytes 4389892 | tf_op jit(solution)/shard_map/while/body/eval_jaxpr/dot_general | solution.py:49
  1030.2 53.6 %fusion.43 = f32[96,1601]{1,0:T(8,128)S(1)} fusion(s32[1601]{0:T(1024)S(1)} %iota_add_fusion.4, s32[2048]{0:T(1024)S(1)} %iota_add_fusion.5, f32[96,1601]{1,0:T(8,128)} %get-tuple-element.198, f32[96,2,2048]{2,0,1:T(8,128)S(1)} %copy_convert_fusion.4, f32[96,2,2048]{2,0,1:T(8,128)S(1)} %copy_convert_fusion.5, pred[]{:T(512)S(6)} %compare.3), kind=kOutput, calls=%fused_computation.14.clone.3 | convolution fusion | flops 663421184 | bytes 4389893 | tf_op jit(solution)/shard_map/while/body/eval_jaxpr/dot_general | solution.py:48
  1083.8 54.1 %fusion.44 = f32[96,1601]{1,0:T(8,128)} fusion(f32[96,1601]{1,0:T(8,128)S(1)} %fusion.43, s32[1601]{0:T(1024)S(1)} %iota_add_fusion.4, s32[2048]{0:T(1024)S(1)} %iota_add_fusion.5, f32[96,2,2048]{2,0,1:T(8,128)S(1)} %copy_convert_fusion.4, f32[96,2,2048]{2,0,1:T(8,128)S(1)} %copy_convert_fusion.5), kind=kOutput, calls=%fused_computation.13.clone.3 | convolution fusion | flops 666546304 | bytes 4389892 | tf_op jit(solution)/shard_map/while/body/eval_jaxpr/dot_general | solution.py:49
  1145.6 21.9 %all-to-all-done.1 = f32[32,4,1601]{2,1,0:T(4,128)S(1)} async-done(((f32[32,4,1601]{2,1,0:T(4,128)}), f32[32,4,1601]{2,1,0:T(4,128)S(1)}, u32[]{:S(2)}, u32[]{:S(2)}) %all-to-all-start.1) | async-done | bytes 819744 | tf_op jit(solution)/shard_map/all_to_all | solution.py:68
  (90 shorter events, 51.2 us)
Async XLA Ops:
  6.5 4.7 copy-start
  6.5 6.1 copy-start.2
  6.5 6.7 copy-start.4
  6.5 15.0 %copy-start.3 = (s32[2,96]{1,0:T(2,128)S(1)}, s32[2,96]{1,0:T(2,128)}, u32[]{:S(2)}) copy-start(s32[2,96]{1,0:T(2,128)} %param.12) | copy-start | bytes 2308
  6.5 15.0 %copy-start.5 = (s32[96]{0:T(128)S(1)}, s32[96]{0:T(128)}, u32[]{:S(2)}) copy-start(s32[96]{0:T(128)} %param.13) | copy-start | bytes 1156
  6.5 60.2 %all-gather.2.cloned.1.call-start = ((), (), s32[]{:S(2)}) async-start(), calls=%async_computation.2 | async-start | bytes 5308416 | tf_op jit(solution)/shard_map/all_gather | solution.py:36
  14.2 1126.7 %all-to-all-start = ((f32[32,1,4]{2,1,0:T(1,128)}), f32[32,1,4]{2,1,0:T(1,128)S(1)}, u32[]{:S(2)}, u32[]{:S(2)}) async-start(f32[32,1,4]{2,1,0:T(1,128)} %copy.14), calls=%async_computation | async-start | bytes 32768 | tf_op jit(solution)/shard_map/all_to_all | solution.py:75
  1137.9 29.9 %copy-start.1 = (f32[96,1601]{1,0:T(8,128)S(1)}, f32[96,1601]{1,0:T(8,128)}, u32[]{:S(2)}) copy-start(f32[96,1601]{1,0:T(8,128)} %param.11) | copy-start | bytes 1844356
  1140.9 26.6 %all-to-all-start.1 = ((f32[32,4,1601]{2,1,0:T(4,128)}), f32[32,4,1601]{2,1,0:T(4,128)S(1)}, u32[]{:S(2)}, u32[]{:S(2)}) async-start(f32[32,4,1601]{2,1,0:T(4,128)} %reshape.68), calls=%async_computation.1 | async-start | bytes 1703936 | tf_op jit(solution)/shard_map/all_to_all | solution.py:68
Sparse Core Ops, SparseCore 0:
  12.8 53.9 all-gather.1
where the time goes:
time: 1190 us; the launch traced here: 1180 us
  matrix products  971 us (82%)
  waiting for transfers between devices  67.1 us (6%)
  local copies, waits for them, and re-layouts  64.7 us (5%)
  other arithmetic  27.2 us (2%)
  loops' own time  21.4 us (2%)
  between operations  14 us (1%)
    dot_general x9, matrix products, add_block(): return total + jnp.dot(imag_part, sines, preferred_element_type=jnp.float32)  487 us
    dot_general x9, matrix products, add_block(): jnp.dot(real_part, cosines, preferred_element_type=jnp.float32)  481 us
    all_gather x1, waiting for transfers between devices, local(): gathered = lax.all_gather(whitened, 'sta', axis=0, tiled=True)  45.2 us
  transfers between devices with their start and end apart: 3, of which 2 were waited for; matrix products, arithmetic and copies ran while one was open for 90% of the time, Pallas kernels for 0%

commit v1 on v0

--- a/solution.py
+++ b/solution.py
@@ -15,12 +15,11 @@
     return (split * lax.rsqrt(power + 1e-06)).reshape(shape).astype(jnp.bfloat16)
 
 
-def table_block(start, width, lag_count, total_bins):
-    freqs = start + lax.iota(jnp.int32, width)
+def angle_table(freqs, lag_count, total_bins):
     shifts = lax.iota(jnp.int32, lag_count) - (lag_count - 1) // 2
     angle_ids = jnp.mod(freqs[:, None] * shifts[None, :], 2 * total_bins)
     theta = angle_ids.astype(jnp.float32) * jnp.float32(math.pi / total_bins)
-    return (jnp.cos(theta).astype(jnp.bfloat16), (-jnp.sin(theta)).astype(jnp.bfloat16))
+    return jnp.cos(theta), jnp.sin(theta)
 
 
 def local(spectra, stacks, pair_sta, pair_valid, owner, slot):
@@ -34,19 +33,33 @@
     capacity = max(2, (4 * pair_count + 3 * devices - 1) // (3 * devices))
     whitened = whiten(spectra)
     gathered = lax.all_gather(whitened, "sta", axis=0, tiled=True)
-    first = jnp.take(gathered, pair_sta[0], axis=0)
-    second = jnp.take(gathered, pair_sta[1], axis=0)
+    group_sta = gathered.shape[0]
+    flat = gathered.reshape(group_sta, 2 * total_bins)
+    sta_ids = lax.iota(jnp.int32, group_sta)[None, :]
+    pick0 = (pair_sta[0][:, None] == sta_ids).astype(jnp.bfloat16)
+    pick1 = (pair_sta[1][:, None] == sta_ids).astype(jnp.bfloat16)
+    first = jnp.dot(pick0, flat, preferred_element_type=jnp.float32).reshape(pair_count, 2, total_bins)
+    second = jnp.dot(pick1, flat, preferred_element_type=jnp.float32).reshape(pair_count, 2, total_bins)
+    real_all = (first[:, 0] * second[:, 0] + first[:, 1] * second[:, 1]).astype(jnp.bfloat16)
+    imag_all = (first[:, 1] * second[:, 0] - first[:, 0] * second[:, 1]).astype(jnp.bfloat16)
+
+    low = 64
     fblock = 2048
+    assert total_bins % fblock == 0 and fblock % low == 0
+    hi_count = fblock // low
+    cos_hi, sin_hi = angle_table(lax.iota(jnp.int32, total_bins // low) * low, lag_count, total_bins)
+    cos_lo, sin_lo = angle_table(lax.iota(jnp.int32, low), lag_count, total_bins)
 
     def add_block(index, total):
         start = index * fblock
-        left = lax.dynamic_slice_in_dim(first, start, fblock, 2).astype(jnp.float32)
-        right = lax.dynamic_slice_in_dim(second, start, fblock, 2).astype(jnp.float32)
-        real_part = (left[:, 0] * right[:, 0] + left[:, 1] * right[:, 1]).astype(jnp.bfloat16)
-        imag_part = (left[:, 1] * right[:, 0] - left[:, 0] * right[:, 1]).astype(jnp.bfloat16)
-        cosines, sines = table_block(start, fblock, lag_count, total_bins)
-        total = total + jnp.dot(real_part, cosines, preferred_element_type=jnp.float32)
-        return total + jnp.dot(imag_part, sines, preferred_element_type=jnp.float32)
+        left = lax.dynamic_slice_in_dim(real_all, start, fblock, 1)
+        right = lax.dynamic_slice_in_dim(imag_all, start, fblock, 1)
+        ch = lax.dynamic_slice_in_dim(cos_hi, index * hi_count, hi_count, 0)[:, None, :]
+        sh = lax.dynamic_slice_in_dim(sin_hi, index * hi_count, hi_count, 0)[:, None, :]
+        cosines = (ch * cos_lo[None] - sh * sin_lo[None]).reshape(fblock, lag_count)
+        sines = (-(sh * cos_lo[None] + ch * sin_lo[None])).reshape(fblock, lag_count)
+        total = total + jnp.dot(left, cosines.astype(jnp.bfloat16), preferred_element_type=jnp.float32)
+        return total + jnp.dot(right, sines.astype(jnp.bfloat16), preferred_element_type=jnp.float32)
 
     corr = lax.fori_loop(
         0, total_bins // fblock, add_block, jnp.zeros((pair_count, lag_count), jnp.float32)

time: 1190 us -> 303 us (0.25); the launches traced: 1180 us -> 302 us
  matrix products: 971 us -> 77 us
  other arithmetic: 27.2 us -> 125 us
  local copies, waits for them, and re-layouts: 64.7 us -> 17.7 us
  loops' own time: 21.4 us -> 0.35 us
    dot_general x18 -> x20, matrix products: 968 us -> 74.8 us  [the longest x9 39.9 us: add_block(): jnp.dot(left, cosines.astype(jnp.bfloat16), preferred_element_type=jnp.fl...]
    convert_element_type x18 -> x10, other arithmetic: 4.81 us -> 94.4 us  [the longest x9 86.4 us: add_block(): sines.astype(jnp.bfloat16)]
    gather x2 -> x0, local copies, waits for them, and re-layouts: 38.5 us -> none  [the longest x1 19.3 us: local(): second = jnp.take(gathered, pair_sta[1], axis=0)]
    another operation x1, loops' own time: 21.4 us -> 0.35 us  [local(): lax.fori_loop(0, total_bins // fblock, add_block, jnp.zeros((pair_count,...]
    select_n x1 -> x0, other arithmetic: 16.3 us -> none  [local(): second = jnp.take(gathered, pair_sta[1], axis=0)]
    cos x0 -> x9, other arithmetic: none -> 15.4 us  [angle_table(): return (jnp.cos(theta), jnp.sin(theta))]
    dynamic_slice x9, local copies, waits for them, and re-layouts: 22.1 us -> 8.7 us  [add_block(): lax.dynamic_slice_in_dim(sin_hi, index * hi_count, hi_count, 0)[:, None, :]]
  transfers between devices with their start and end apart: 3 -> 3, of which waited for: 2 -> 2; matrix products, arithmetic and copies ran while one was open for 90% -> 68% of each run, Pallas kernels for 0% -> 0%
where the time goes in v1:
time: 303 us; the launch traced here: 302 us
  other arithmetic  125 us (41%)
  matrix products  77 us (25%)
  waiting for transfers between devices  58 us (19%)
  local copies, waits for them, and re-layouts  17.7 us (6%)
  between operations  13.6 us (4%)
  starting transfers between devices  10.9 us (4%)
    convert_element_type x9, other arithmetic, add_block(): sines.astype(jnp.bfloat16)  86.4 us
    dot_general x9, matrix products, add_block(): jnp.dot(left, cosines.astype(jnp.bfloat16), preferred_element_type=jnp.fl...  39.9 us
    all_gather x1, waiting for transfers between devices, local(): gathered = lax.all_gather(whitened, 'sta', axis=0, tiled=True)  36 us
    all_to_all x1, waiting for transfers between devices, local(): lax.all_to_all(send_rows.reshape(devices, capacity, lag_count), ('grp', '...  21.9 us
    dot_general x9, matrix products, add_block(): jnp.dot(right, sines.astype(jnp.bfloat16), preferred_element_type=jnp.flo...  20 us
    cos x9, other arithmetic, angle_table(): return (jnp.cos(theta), jnp.sin(theta))  15.4 us
    sin x1, other arithmetic, angle_table(): return (jnp.cos(theta), jnp.sin(theta))  8.97 us
    dot_general x1, matrix products, local(): jnp.dot(pick0, flat, preferred_element_type=jnp.float32)  8.76 us
  transfers between devices with their start and end apart: 3, of which 2 were waited for; matrix products, arithmetic and copies ran while one was open for 68% of the time, Pallas kernels for 0%

profile of v1, /device:TPU:0, one launch (start us, length us, event | category | flops | bytes accessed | tf_op | source)
XLA Modules:
  0.0 302.4 jit_solution(13132071680303862116)
XLA Ops:
  14.2 7.5 %all-to-all-start = ((f32[32,1,4]{2,1,0:T(1,128)}), f32[32,1,4]{2,1,0:T(1,128)S(1)}, u32[]{:S(2)}, u32[]{:S(2)}) async-start(f32[32,1,4]{2,1,0:T(1,128)} %copy.12), calls=%async_computation | async-start | bytes 32768 | tf_op jit(solution)/shard_map/all_to_all | solution.py:88
  21.8 9.0 %fusion.27 = (f32[288,1601]{1,0:T(8,128)S(1)}, f32[288,1601]{1,0:T(8,128)}) fusion(s32[1601]{0:T(1024)S(1)} %iota_add_fusion, s32[288]{0:T(512)S(1)} %iota_multiply_fusion), kind=kLoop, calls=%fused_computation.38 | loop fusion | flops 4149792 | bytes 3696260 | tf_op jit(solution)/shard_map/sin | solution.py:22
  30.7 36.0 %all-gather.2.cloned.1.call-done = bf16[64,2,18432]{2,1,0:T(2,128)(2,1)} async-done(((bf16[8,2,18432]{2,1,0:T(2,128)(2,1)}), bf16[64,2,18432]{2,1,0:T(2,128)(2,1)}) %all-gather.2.cloned.1.call-update) | async-done | bytes 4718608 | tf_op jit(solution)/shard_map/all_gather | solution.py:35
  66.8 6.1 %fusion.15 = f32[96,2,18432]{2,0,1:T(8,128)S(1)} fusion(s32[96]{0:T(128)S(1)} %get-tuple-element.271, bf16[8,8,2,18432]{3,2,1,0:T(2,128)(2,1)} %bitcast.58), kind=kOutput, calls=%fused_computation.23 | convolution fusion | flops 452990976 | bytes 18874752 | tf_op jit(solution)/shard_map/dot_general | solution.py:42
  72.9 8.8 %fusion.17 = f32[96,2,18432]{2,0,1:T(8,128)} fusion(s32[96]{0:T(128)S(1)} %get-tuple-element.270, bf16[8,8,2,18432]{3,2,1,0:T(2,128)(2,1)S(1)} %bitcast.59), kind=kOutput, calls=%fused_computation.25 | convolution fusion | flops 452990976 | bytes 18874752 | tf_op jit(solution)/shard_map/dot_general | solution.py:41
  81.7 7.9 %fusion.22 = (bf16[96,18432]{1,0:T(8,128)(2,1)}, bf16[96,18432]{1,0:T(8,128)(2,1)}) fusion(f32[96,2,18432]{2,0,1:T(8,128)S(1)} %fusion.15, f32[96,2,18432]{2,0,1:T(8,128)} %fusion.17), kind=kLoop, calls=%fused_computation.30 | loop fusion | flops 14155776 | bytes 35389440 | tf_op jit(solution)/shard_map/convert_element_type | solution.py:44
  89.6 175.8 %while.17 = (s32[]{:T(128)}, f32[96,1601]{1,0:T(8,128)S(1)}, bf16[96,18432]{1,0:T(8,128)(2,1)}, f32[288,1601]{1,0:T(8,128)}, f32[288,1601]{1,0:T(8,128)S(1)}, /*...) while((s32[]{:T(128)}, f32[96,1601]{1,0:T(8,128)S(1)}, ...), condition=%wide.region_5.6_spmd.clone.clone.clone.clone, body=%wide.region_4.5_spmd.clone.clone.clone.clone.sunk | while | flops 1289970688 | bytes 58840844 | solution.py:64
  92.3 9.6 %negate_convert_fusion.2 = (bf16[32,64,1601]{2,1,0:T(8,128)(2,1)}, bf16[32,64,1601]{2,1,0:T(8,128)(2,1)}) fusion(f32[64,1601]{1,0:T(8,128)S(1)} %get-tuple-element.321, f32[32,1601]{1,0:T(8,128)S(1)} %get-tuple-element.322, f32[64,1601]{1,0:T(8,128)S(1)} %get-tuple-element.323, f32[32,1601]{1,0:T(8,128)S(1)} %get-tuple-element.324), kind=kLoop, calls=%fused_computation.2.clone.1 | loop fusion | flops 29509632 | bytes 14344960 | tf_op jit(solution)/shard_map/while/body/eval_jaxpr/convert_element_type | solution.py:62
  111.8 9.6 %negate_convert_fusion.2 = (bf16[32,64,1601]{2,1,0:T(8,128)(2,1)}, bf16[32,64,1601]{2,1,0:T(8,128)(2,1)}) fusion(f32[64,1601]{1,0:T(8,128)S(1)} %get-tuple-element.321, f32[32,1601]{1,0:T(8,128)S(1)} %get-tuple-element.322, f32[64,1601]{1,0:T(8,128)S(1)} %get-tuple-element.323, f32[32,1601]{1,0:T(8,128)S(1)} %get-tuple-element.324), kind=kLoop, calls=%fused_computation.2.clone.1 | loop fusion | flops 29509632 | bytes 14344960 | tf_op jit(solution)/shard_map/while/body/eval_jaxpr/convert_element_type | solution.py:62
  121.4 4.4 %convolution_add_fusion.5 = f32[96,1601]{1,0:T(8,128)S(1)} fusion(bf16[2048,1601]{1,0:T(8,128)(2,1)} %bitcast.56, f32[96,1601]{1,0:T(8,128)S(1)} %get-tuple-element.341, bf16[96,18432]{1,0:T(8,128)(2,1)} %get-tuple-element.355, s32[]{:T(128)S(6)} %select_n.82, pred[]{:T(512)S(6)} %compare.5), kind=kOutput, calls=%fused_computation.5.clone.1 | convolution fusion | flops 629846272 | bytes 8438533 | tf_op jit(solution)/shard_map/while/body/eval_jaxpr/dot_general | solution.py:61
  131.4 9.6 %negate_convert_fusion.2 = (bf16[32,64,1601]{2,1,0:T(8,128)(2,1)}, bf16[32,64,1601]{2,1,0:T(8,128)(2,1)}) fusion(f32[64,1601]{1,0:T(8,128)S(1)} %get-tuple-element.321, f32[32,1601]{1,0:T(8,128)S(1)} %get-tuple-element.322, f32[64,1601]{1,0:T(8,128)S(1)} %get-tuple-element.323, f32[32,1601]{1,0:T(8,128)S(1)} %get-tuple-element.324), kind=kLoop, calls=%fused_computation.2.clone.1 | loop fusion | flops 29509632 | bytes 14344960 | tf_op jit(solution)/shard_map/while/body/eval_jaxpr/convert_element_type | solution.py:62
  141.0 4.4 %convolution_add_fusion.5 = f32[96,1601]{1,0:T(8,128)S(1)} fusion(bf16[2048,1601]{1,0:T(8,128)(2,1)} %bitcast.56, f32[96,1601]{1,0:T(8,128)S(1)} %get-tuple-element.341, bf16[96,18432]{1,0:T(8,128)(2,1)} %get-tuple-element.355, s32[]{:T(128)S(6)} %select_n.82, pred[]{:T(512)S(6)} %compare.5), kind=kOutput, calls=%fused_computation.5.clone.1 | convolution fusion | flops 629846272 | bytes 8438533 | tf_op jit(solution)/shard_map/while/body/eval_jaxpr/dot_general | solution.py:61
  150.9 9.6 %negate_convert_fusion.2 = (bf16[32,64,1601]{2,1,0:T(8,128)(2,1)}, bf16[32,64,1601]{2,1,0:T(8,128)(2,1)}) fusion(f32[64,1601]{1,0:T(8,128)S(1)} %get-tuple-element.321, f32[32,1601]{1,0:T(8,128)S(1)} %get-tuple-element.322, f32[64,1601]{1,0:T(8,128)S(1)} %get-tuple-element.323, f32[32,1601]{1,0:T(8,128)S(1)} %get-tuple-element.324), kind=kLoop, calls=%fused_computation.2.clone.1 | loop fusion | flops 29509632 | bytes 14344960 | tf_op jit(solution)/shard_map/while/body/eval_jaxpr/convert_element_type | solution.py:62
  160.5 4.4 %convolution_add_fusion.5 = f32[96,1601]{1,0:T(8,128)S(1)} fusion(bf16[2048,1601]{1,0:T(8,128)(2,1)} %bitcast.56, f32[96,1601]{1,0:T(8,128)S(1)} %get-tuple-element.341, bf16[96,18432]{1,0:T(8,128)(2,1)} %get-tuple-element.355, s32[]{:T(128)S(6)} %select_n.82, pred[]{:T(512)S(6)} %compare.5), kind=kOutput, calls=%fused_computation.5.clone.1 | convolution fusion | flops 629846272 | bytes 8438533 | tf_op jit(solution)/shard_map/while/body/eval_jaxpr/dot_general | solution.py:61
  170.4 9.6 %negate_convert_fusion.2 = (bf16[32,64,1601]{2,1,0:T(8,128)(2,1)}, bf16[32,64,1601]{2,1,0:T(8,128)(2,1)}) fusion(f32[64,1601]{1,0:T(8,128)S(1)} %get-tuple-element.321, f32[32,1601]{1,0:T(8,128)S(1)} %get-tuple-element.322, f32[64,1601]{1,0:T(8,128)S(1)} %get-tuple-element.323, f32[32,1601]{1,0:T(8,128)S(1)} %get-tuple-element.324), kind=kLoop, calls=%fused_computation.2.clone.1 | loop fusion | flops 29509632 | bytes 14344960 | tf_op jit(solution)/shard_map/while/body/eval_jaxpr/convert_element_type | solution.py:62
  180.0 4.4 %convolution_add_fusion.5 = f32[96,1601]{1,0:T(8,128)S(1)} fusion(bf16[2048,1601]{1,0:T(8,128)(2,1)} %bitcast.56, f32[96,1601]{1,0:T(8,128)S(1)} %get-tuple-element.341, bf16[96,18432]{1,0:T(8,128)(2,1)} %get-tuple-element.355, s32[]{:T(128)S(6)} %select_n.82, pred[]{:T(512)S(6)} %compare.5), kind=kOutput, calls=%fused_computation.5.clone.1 | convolution fusion | flops 629846272 | bytes 8438533 | tf_op jit(solution)/shard_map/while/body/eval_jaxpr/dot_general | solution.py:61
  190.0 9.6 %negate_convert_fusion.2 = (bf16[32,64,1601]{2,1,0:T(8,128)(2,1)}, bf16[32,64,1601]{2,1,0:T(8,128)(2,1)}) fusion(f32[64,1601]{1,0:T(8,128)S(1)} %get-tuple-element.321, f32[32,1601]{1,0:T(8,128)S(1)} %get-tuple-element.322, f32[64,1601]{1,0:T(8,128)S(1)} %get-tuple-element.323, f32[32,1601]{1,0:T(8,128)S(1)} %get-tuple-element.324), kind=kLoop, calls=%fused_computation.2.clone.1 | loop fusion | flops 29509632 | bytes 14344960 | tf_op jit(solution)/shard_map/while/body/eval_jaxpr/convert_element_type | solution.py:62
  199.6 4.4 %convolution_add_fusion.5 = f32[96,1601]{1,0:T(8,128)S(1)} fusion(bf16[2048,1601]{1,0:T(8,128)(2,1)} %bitcast.56, f32[96,1601]{1,0:T(8,128)S(1)} %get-tuple-element.341, bf16[96,18432]{1,0:T(8,128)(2,1)} %get-tuple-element.355, s32[]{:T(128)S(6)} %select_n.82, pred[]{:T(512)S(6)} %compare.5), kind=kOutput, calls=%fused_computation.5.clone.1 | convolution fusion | flops 629846272 | bytes 8438533 | tf_op jit(solution)/shard_map/while/body/eval_jaxpr/dot_general | solution.py:61
  209.5 9.6 %negate_convert_fusion.2 = (bf16[32,64,1601]{2,1,0:T(8,128)(2,1)}, bf16[32,64,1601]{2,1,0:T(8,128)(2,1)}) fusion(f32[64,1601]{1,0:T(8,128)S(1)} %get-tuple-element.321, f32[32,1601]{1,0:T(8,128)S(1)} %get-tuple-element.322, f32[64,1601]{1,0:T(8,128)S(1)} %get-tuple-element.323, f32[32,1601]{1,0:T(8,128)S(1)} %get-tuple-element.324), kind=kLoop, calls=%fused_computation.2.clone.1 | loop fusion | flops 29509632 | bytes 14344960 | tf_op jit(solution)/shard_map/while/body/eval_jaxpr/convert_element_type | solution.py:62
  229.0 9.6 %negate_convert_fusion.2 = (bf16[32,64,1601]{2,1,0:T(8,128)(2,1)}, bf16[32,64,1601]{2,1,0:T(8,128)(2,1)}) fusion(f32[64,1601]{1,0:T(8,128)S(1)} %get-tuple-element.321, f32[32,1601]{1,0:T(8,128)S(1)} %get-tuple-element.322, f32[64,1601]{1,0:T(8,128)S(1)} %get-tuple-element.323, f32[32,1601]{1,0:T(8,128)S(1)} %get-tuple-element.324), kind=kLoop, calls=%fused_computation.2.clone.1 | loop fusion | flops 29509632 | bytes 14344960 | tf_op jit(solution)/shard_map/while/body/eval_jaxpr/convert_element_type | solution.py:62
  238.7 4.4 %convolution_add_fusion.5 = f32[96,1601]{1,0:T(8,128)S(1)} fusion(bf16[2048,1601]{1,0:T(8,128)(2,1)} %bitcast.56, f32[96,1601]{1,0:T(8,128)S(1)} %get-tuple-element.341, bf16[96,18432]{1,0:T(8,128)(2,1)} %get-tuple-element.355, s32[]{:T(128)S(6)} %select_n.82, pred[]{:T(512)S(6)} %compare.5), kind=kOutput, calls=%fused_computation.5.clone.1 | convolution fusion | flops 629846272 | bytes 8438533 | tf_op jit(solution)/shard_map/while/body/eval_jaxpr/dot_general | solution.py:61
  248.6 9.6 %negate_convert_fusion.2 = (bf16[32,64,1601]{2,1,0:T(8,128)(2,1)}, bf16[32,64,1601]{2,1,0:T(8,128)(2,1)}) fusion(f32[64,1601]{1,0:T(8,128)S(1)} %get-tuple-element.321, f32[32,1601]{1,0:T(8,128)S(1)} %get-tuple-element.322, f32[64,1601]{1,0:T(8,128)S(1)} %get-tuple-element.323, f32[32,1601]{1,0:T(8,128)S(1)} %get-tuple-element.324), kind=kLoop, calls=%fused_computation.2.clone.1 | loop fusion | flops 29509632 | bytes 14344960 | tf_op jit(solution)/shard_map/while/body/eval_jaxpr/convert_element_type | solution.py:62
  258.2 4.4 %convolution_add_fusion.5 = f32[96,1601]{1,0:T(8,128)S(1)} fusion(bf16[2048,1601]{1,0:T(8,128)(2,1)} %bitcast.56, f32[96,1601]{1,0:T(8,128)S(1)} %get-tuple-element.341, bf16[96,18432]{1,0:T(8,128)(2,1)} %get-tuple-element.355, s32[]{:T(128)S(6)} %select_n.82, pred[]{:T(512)S(6)} %compare.5), kind=kOutput, calls=%fused_computation.5.clone.1 | convolution fusion | flops 629846272 | bytes 8438533 | tf_op jit(solution)/shard_map/while/body/eval_jaxpr/dot_general | solution.py:61
  271.9 21.9 %all-to-all-done.1 = f32[32,4,1601]{2,1,0:T(4,128)S(1)} async-done(((f32[32,4,1601]{2,1,0:T(4,128)}), f32[32,4,1601]{2,1,0:T(4,128)S(1)}, u32[]{:S(2)}, u32[]{:S(2)}) %all-to-all-start.1) | async-done | bytes 819744 | tf_op jit(solution)/shard_map/all_to_all | solution.py:81
  (93 shorter events, 73.7 us)
Async XLA Ops:
  6.5 4.7 %copy-start.2 = (f32[8,2,18432]{2,1,0:T(2,128)S(1)}, f32[8,2,18432]{2,1,0:T(2,128)}, u32[]{:S(2)}) copy-start(f32[8,2,18432]{2,1,0:T(2,128)} %param.8) | copy-start | bytes 3538948
  6.5 60.2 %all-gather.2.cloned.1.call-start = ((), (), s32[]{:S(2)}) async-start(), calls=%async_computation.2 | async-start | bytes 5308416 | tf_op jit(solution)/shard_map/all_gather | solution.py:35
  9.4 3.2 %copy-start.4 = (s32[96,1]{0,1:T(1,128)S(1)}, s32[96,1]{0,1:T(1,128)}, u32[]{:S(2)}) copy-start(s32[96,1]{0,1:T(1,128)} %param.12) | copy-start | bytes 1156
  9.5 3.8 %copy-start.6 = (s32[96]{0:T(128)S(1)}, s32[96]{0:T(128)}, u32[]{:S(2)}) copy-start(s32[96]{0:T(128)} %param.13) | copy-start | bytes 1156
  9.5 12.3 %copy-start.7 = (s32[96]{0:T(128)S(1)}, s32[96]{0:T(128)}, u32[]{:S(2)}) copy-start(s32[96]{0:T(128)} %param.11) | copy-start | bytes 1156
  9.5 12.3 %copy-start.5 = (s32[2,96]{1,0:T(2,128)S(1)}, s32[2,96]{1,0:T(2,128)}, u32[]{:S(2)}) copy-start(s32[2,96]{1,0:T(2,128)} %param.10) | copy-start | bytes 2308
  14.2 253.0 %all-to-all-start = ((f32[32,1,4]{2,1,0:T(1,128)}), f32[32,1,4]{2,1,0:T(1,128)S(1)}, u32[]{:S(2)}, u32[]{:S(2)}) async-start(f32[32,1,4]{2,1,0:T(1,128)} %copy.12), calls=%async_computation | async-start | bytes 32768 | tf_op jit(solution)/shard_map/all_to_all | solution.py:88
  66.8 6.1 %copy-start.1 = (bf16[64,2,18432]{2,1,0:T(2,128)(2,1)S(1)}, bf16[64,2,18432]{2,1,0:T(2,128)(2,1)}, u32[]{:S(2)}) copy-start(bf16[64,2,18432]{2,1,0:T(2,128)(2,1)} %all-gather.2.cloned.1.call-done) | copy-start | bytes 14155780
  101.9 5.0 %copy-start = (bf16[32,64,1601]{2,1,0:T(8,128)(2,1)S(1)}, bf16[32,64,1601]{2,1,0:T(8,128)(2,1)}, u32[]{:S(2)}) copy-start(bf16[32,64,1601]{2,1,0:T(8,128)(2,1)} %get-tuple-element.326) | copy-start | bytes 19673092 | tf_op jit(solution)/shard_map/while
  121.4 5.0 %copy-start = (bf16[32,64,1601]{2,1,0:T(8,128)(2,1)S(1)}, bf16[32,64,1601]{2,1,0:T(8,128)(2,1)}, u32[]{:S(2)}) copy-start(bf16[32,64,1601]{2,1,0:T(8,128)(2,1)} %get-tuple-element.326) | copy-start | bytes 19673092 | tf_op jit(solution)/shard_map/while
  141.0 5.0 %copy-start = (bf16[32,64,1601]{2,1,0:T(8,128)(2,1)S(1)}, bf16[32,64,1601]{2,1,0:T(8,128)(2,1)}, u32[]{:S(2)}) copy-start(bf16[32,64,1601]{2,1,0:T(8,128)(2,1)} %get-tuple-element.326) | copy-start | bytes 19673092 | tf_op jit(solution)/shard_map/while
  160.5 5.0 %copy-start = (bf16[32,64,1601]{2,1,0:T(8,128)(2,1)S(1)}, bf16[32,64,1601]{2,1,0:T(8,128)(2,1)}, u32[]{:S(2)}) copy-start(bf16[32,64,1601]{2,1,0:T(8,128)(2,1)} %get-tuple-element.326) | copy-start | bytes 19673092 | tf_op jit(solution)/shard_map/while
  180.0 5.0 %copy-start = (bf16[32,64,1601]{2,1,0:T(8,128)(2,1)S(1)}, bf16[32,64,1601]{2,1,0:T(8,128)(2,1)}, u32[]{:S(2)}) copy-start(bf16[32,64,1601]{2,1,0:T(8,128)(2,1)} %get-tuple-element.326) | copy-start | bytes 19673092 | tf_op jit(solution)/shard_map/while
  199.6 5.0 %copy-start = (bf16[32,64,1601]{2,1,0:T(8,128)(2,1)S(1)}, bf16[32,64,1601]{2,1,0:T(8,128)(2,1)}, u32[]{:S(2)}) copy-start(bf16[32,64,1601]{2,1,0:T(8,128)(2,1)} %get-tuple-element.326) | copy-start | bytes 19673092 | tf_op jit(solution)/shard_map/while
  219.1 5.0 %copy-start = (bf16[32,64,1601]{2,1,0:T(8,128)(2,1)S(1)}, bf16[32,64,1601]{2,1,0:T(8,128)(2,1)}, u32[]{:S(2)}) copy-start(bf16[32,64,1601]{2,1,0:T(8,128)(2,1)} %get-tuple-element.326) | copy-start | bytes 19673092 | tf_op jit(solution)/shard_map/while
  238.7 5.0 %copy-start = (bf16[32,64,1601]{2,1,0:T(8,128)(2,1)S(1)}, bf16[32,64,1601]{2,1,0:T(8,128)(2,1)}, u32[]{:S(2)}) copy-start(bf16[32,64,1601]{2,1,0:T(8,128)(2,1)} %get-tuple-element.326) | copy-start | bytes 19673092 | tf_op jit(solution)/shard_map/while
  258.2 5.0 %copy-start = (bf16[32,64,1601]{2,1,0:T(8,128)(2,1)S(1)}, bf16[32,64,1601]{2,1,0:T(8,128)(2,1)}, u32[]{:S(2)}) copy-start(bf16[32,64,1601]{2,1,0:T(8,128)(2,1)} %get-tuple-element.326) | copy-start | bytes 19673092 | tf_op jit(solution)/shard_map/while
  265.4 28.7 %copy-start.3 = (f32[96,1601]{1,0:T(8,128)S(1)}, f32[96,1601]{1,0:T(8,128)}, u32[]{:S(2)}) copy-start(f32[96,1601]{1,0:T(8,128)} %param.9) | copy-start | bytes 1844356
  267.2 26.6 %all-to-all-start.1 = ((f32[32,4,1601]{2,1,0:T(4,128)}), f32[32,4,1601]{2,1,0:T(4,128)S(1)}, u32[]{:S(2)}, u32[]{:S(2)}) async-start(f32[32,4,1601]{2,1,0:T(4,128)} %reshape.116), calls=%async_computation.1 | async-start | bytes 1703936 | tf_op jit(solution)/shard_map/all_to_all | solution.py:81
Sparse Core Ops, SparseCore 0:
  12.8 53.9 all-gather.1

commit v2 on v1

--- a/solution.py
+++ b/solution.py
@@ -3,6 +3,8 @@
 import jax
 import jax.numpy as jnp
 from jax import lax
+from jax.experimental import pallas as pl
+from jax.experimental.pallas import tpu as pltpu
 from jax.sharding import PartitionSpec as P
 
 BAND = 64
@@ -15,11 +17,67 @@
     return (split * lax.rsqrt(power + 1e-06)).reshape(shape).astype(jnp.bfloat16)
 
 
-def angle_table(freqs, lag_count, total_bins):
-    shifts = lax.iota(jnp.int32, lag_count) - (lag_count - 1) // 2
+def angle_table(freqs, lag_pad, lag_count, total_bins):
+    shifts = lax.iota(jnp.int32, lag_pad) - (lag_count - 1) // 2
     angle_ids = jnp.mod(freqs[:, None] * shifts[None, :], 2 * total_bins)
     theta = angle_ids.astype(jnp.float32) * jnp.float32(math.pi / total_bins)
     return jnp.cos(theta), jnp.sin(theta)
+
+
+LOW = 64
+FBLOCK = 1024
+
+
+def table_kernel(real_ref, imag_ref, chi_ref, shi_ref, clo_ref, slo_ref, out_ref, ctab, stab):
+    @pl.when(pl.program_id(0) == 0)
+    def _():
+        out_ref[...] = jnp.zeros_like(out_ref)
+
+    def fill(j, carry):
+        clo = clo_ref[...]
+        slo = slo_ref[...]
+        ch = chi_ref[pl.ds(j, 1), :]
+        sh = shi_ref[pl.ds(j, 1), :]
+        rows = pl.ds(pl.multiple_of(j * LOW, LOW), LOW)
+        ctab[rows, :] = (ch * clo - sh * slo).astype(jnp.bfloat16)
+        stab[rows, :] = (-(sh * clo + ch * slo)).astype(jnp.bfloat16)
+        return carry
+
+    lax.fori_loop(0, FBLOCK // LOW, fill, 0)
+    out_ref[...] += jnp.dot(real_ref[...], ctab[...], preferred_element_type=jnp.float32) + jnp.dot(
+        imag_ref[...], stab[...], preferred_element_type=jnp.float32
+    )
+
+
+def correlate(real_all, imag_all, lag_count, total_bins):
+    pair_count = real_all.shape[0]
+    lag_pad = -(-lag_count // 128) * 128
+    cos_hi, sin_hi = angle_table(lax.iota(jnp.int32, total_bins // LOW) * LOW, lag_pad, lag_count, total_bins)
+    cos_lo, sin_lo = angle_table(lax.iota(jnp.int32, LOW), lag_pad, lag_count, total_bins)
+    hi_rows = FBLOCK // LOW
+    assert total_bins % FBLOCK == 0
+    out = pl.pallas_call(
+        table_kernel,
+        grid=(total_bins // FBLOCK,),
+        in_specs=[
+            pl.BlockSpec((pair_count, FBLOCK), lambda i: (0, i)),
+            pl.BlockSpec((pair_count, FBLOCK), lambda i: (0, i)),
+            pl.BlockSpec((hi_rows, lag_pad), lambda i: (i, 0)),
+            pl.BlockSpec((hi_rows, lag_pad), lambda i: (i, 0)),
+            pl.BlockSpec((LOW, lag_pad), lambda i: (0, 0)),
+            pl.BlockSpec((LOW, lag_pad), lambda i: (0, 0)),
+        ],
+        out_specs=pl.BlockSpec((pair_count, lag_pad), lambda i: (0, 0)),
+        out_shape=jax.ShapeDtypeStruct((pair_count, lag_pad), jnp.float32),
+        scratch_shapes=[
+            pltpu.VMEM((FBLOCK, lag_pad), jnp.bfloat16),
+            pltpu.VMEM((FBLOCK, lag_pad), jnp.bfloat16),
+        ],
+        compiler_params=pltpu.CompilerParams(
+            dimension_semantics=("arbitrary",), vmem_limit_bytes=48 * 1024 * 1024
+        ),
+    )(real_all, imag_all, cos_hi, sin_hi, cos_lo, sin_lo)
+    return out[:, :lag_count]
 
 
 def local(spectra, stacks, pair_sta, pair_valid, owner, slot):
@@ -38,32 +96,14 @@
     sta_ids = lax.iota(jnp.int32, group_sta)[None, :]
     pick0 = (pair_sta[0][:, None] == sta_ids).astype(jnp.bfloat16)
     pick1 = (pair_sta[1][:, None] == sta_ids).astype(jnp.bfloat16)
-    first = jnp.dot(pick0, flat, preferred_element_type=jnp.float32).reshape(pair_count, 2, total_bins)
-    second = jnp.dot(pick1, flat, preferred_element_type=jnp.float32).reshape(pair_count, 2, total_bins)
+    first = jnp.dot(pick0, flat, preferred_element_type=jnp.bfloat16).reshape(pair_count, 2, total_bins)
+    second = jnp.dot(pick1, flat, preferred_element_type=jnp.bfloat16).reshape(pair_count, 2, total_bins)
+    first = first.astype(jnp.float32)
+    second = second.astype(jnp.float32)
     real_all = (first[:, 0] * second[:, 0] + first[:, 1] * second[:, 1]).astype(jnp.bfloat16)
     imag_all = (first[:, 1] * second[:, 0] - first[:, 0] * second[:, 1]).astype(jnp.bfloat16)
 
-    low = 64
-    fblock = 2048
-    assert total_bins % fblock == 0 and fblock % low == 0
-    hi_count = fblock // low
-    cos_hi, sin_hi = angle_table(lax.iota(jnp.int32, total_bins // low) * low, lag_count, total_bins)
-    cos_lo, sin_lo = angle_table(lax.iota(jnp.int32, low), lag_count, total_bins)
-
-    def add_block(index, total):
-        start = index * fblock
-        left = lax.dynamic_slice_in_dim(real_all, start, fblock, 1)
-        right = lax.dynamic_slice_in_dim(imag_all, start, fblock, 1)
-        ch = lax.dynamic_slice_in_dim(cos_hi, index * hi_count, hi_count, 0)[:, None, :]
-        sh = lax.dynamic_slice_in_dim(sin_hi, index * hi_count, hi_count, 0)[:, None, :]
-        cosines = (ch * cos_lo[None] - sh * sin_lo[None]).reshape(fblock, lag_count)
-        sines = (-(sh * cos_lo[None] + ch * sin_lo[None])).reshape(fblock, lag_count)
-        total = total + jnp.dot(left, cosines.astype(jnp.bfloat16), preferred_element_type=jnp.float32)
-        return total + jnp.dot(right, sines.astype(jnp.bfloat16), preferred_element_type=jnp.float32)
-
-    corr = lax.fori_loop(
-        0, total_bins // fblock, add_block, jnp.zeros((pair_count, lag_count), jnp.float32)
-    )
+    corr = correlate(real_all, imag_all, lag_count, total_bins)
     corr = corr * jnp.float32(total_bins ** (-0.5)) * pair_valid.astype(jnp.float32)[:, None]
     dest = owner[:, 0]
     dest_hot = (dest[:, None] == lax.iota(jnp.int32, devices)[None, :]).astype(jnp.int32)

time: 303 us -> 196 us (0.65)
  other arithmetic: 125 us -> 29.9 us
  Pallas kernels: 0 us -> 59.1 us
  matrix products: 77 us -> 22.2 us
  local copies, waits for them, and re-layouts: 17.7 us -> 4.04 us
    convert_element_type x9 -> x0, other arithmetic: 86.4 us -> none  [add_block(): sines.astype(jnp.bfloat16)]
    pallas_call x0 -> x1, Pallas kernels: none -> 59.1 us  [correlate(): pl.pallas_call(table_kernel, grid=(total_bins // FBLOCK,), in_specs=[pl.B...]
    dot_general x20 -> x2, matrix products: 74.8 us -> 20 us  [the longest x1 11.2 us: local(): jnp.dot(pick1, flat, preferred_element_type=jnp.bfloat16)]
    cos x9 -> x0, other arithmetic: 15.4 us -> none  [angle_table(): return (jnp.cos(theta), jnp.sin(theta))]
    dynamic_slice x9 -> x0, local copies, waits for them, and re-layouts: 8.7 us -> none  [add_block(): lax.dynamic_slice_in_dim(sin_hi, index * hi_count, hi_count, 0)[:, None, :]]
    convert_element_type x1, other arithmetic: 7.95 us -> 13.1 us  [local(): (first[:, 1] * second[:, 0] - first[:, 0] * second[:, 1]).astype(jnp.bflo...]
    while x18 -> x0, local copies, waits for them, and re-layouts: 4.96 us -> none
    sin x1 -> x2, other arithmetic: 8.97 us -> 10.7 us  [angle_table(): return (jnp.cos(theta), jnp.sin(theta))]
  transfers between devices with their start and end apart: 3 -> 3, of which waited for: 2 -> 2; matrix products, arithmetic and copies ran while one was open for 68% -> 25% of each run, Pallas kernels for 0% -> 30%
where the time goes in v2:
time: 196 us
  Pallas kernels  59.1 us (30%)
  waiting for transfers between devices  56.3 us (29%)
  other arithmetic  29.9 us (15%)
  matrix products  22.2 us (11%)
  between operations  13.6 us (7%)
  starting transfers between devices  10.9 us (6%)
  local copies, waits for them, and re-layouts  4.04 us (2%)
    pallas_call x1, Pallas kernels, correlate(): pl.pallas_call(table_kernel, grid=(total_bins // FBLOCK,), in_specs=[pl.B...  59.1 us
    all_gather x1, waiting for transfers between devices, local(): gathered = lax.all_gather(whitened, 'sta', axis=0, tiled=True)  34.3 us
    all_to_all x1, waiting for transfers between devices, local(): lax.all_to_all(send_rows.reshape(devices, capacity, lag_count), ('grp', '...  21.9 us
    convert_element_type x1, other arithmetic, local(): (first[:, 1] * second[:, 0] - first[:, 0] * second[:, 1]).astype(jnp.bflo...  13.1 us
    dot_general x1, matrix products, local(): jnp.dot(pick1, flat, preferred_element_type=jnp.bfloat16)  11.2 us
    sin x2, other arithmetic, angle_table(): return (jnp.cos(theta), jnp.sin(theta))  10.7 us
    dot_general x1, matrix products, local(): jnp.dot(pick0, flat, preferred_element_type=jnp.bfloat16)  8.84 us
    all_to_all x1, starting transfers between devices, local(): lax.all_to_all(send_slots.reshape(devices, capacity), ('grp', 'sta'), spl...  7.51 us
  transfers between devices with their start and end apart: 3, of which 2 were waited for; matrix products, arithmetic and copies ran while one was open for 25% of the time, Pallas kernels for 30%

profile of v2, /device:TPU:0, one launch (start us, length us, event | category | flops | bytes accessed | tf_op | source)
XLA Modules:
  0.0 196.0 jit_solution(15431936940595730726)
XLA Ops:
  6.5 2.9 %multiply_reduce_fusion = f32[8,18432]{1,0:T(8,128)S(1)} fusion(f32[8,2,18432]{2,1,0:T(2,128)} %param.6), kind=kLoop, calls=%fused_computation.21 | loop fusion | flops 442368 | bytes 1769472 | tf_op jit(solution)/shard_map/reduce_sum | solution.py:16
  9.5 0.5 reduce_sum.30
  10.0 0.5 reduce_sum.31
  10.5 0.4 mul.127
  10.8 0.4 mul.128
  11.2 1.4 multiply_convert_fusion
  13.2 0.2 fusion.22
  13.5 0.7 copy.12
  14.2 7.5 %all-to-all-start = ((f32[32,1,4]{2,1,0:T(1,128)}), f32[32,1,4]{2,1,0:T(1,128)S(1)}, u32[]{:S(2)}, u32[]{:S(2)}) async-start(f32[32,1,4]{2,1,0:T(1,128)} %copy.12), calls=%async_computation | async-start | bytes 32768 | tf_op jit(solution)/shard_map/all_to_all | solution.py:128
  21.8 1.7 fusion.18
  23.5 9.0 %fusion.10 = (f32[288,1664]{1,0:T(8,128)S(1)}, f32[288,1664]{1,0:T(8,128)}) fusion(s32[1664]{0:T(1024)S(1)} %iota_add_fusion, s32[288]{0:T(512)S(1)} %iota_multiply_fusion), kind=kLoop, calls=%fused_computation.17 | loop fusion | flops 4313088 | bytes 3841664 | tf_op jit(solution)/shard_map/sin | solution.py:24
  32.5 34.3 %all-gather.2.cloned.1.call-done = bf16[64,2,18432]{2,1,0:T(2,128)(2,1)} async-done(((bf16[8,2,18432]{2,1,0:T(2,128)(2,1)}), bf16[64,2,18432]{2,1,0:T(2,128)(2,1)}) %all-gather.2.cloned.1.call-update) | async-done | bytes 4718608 | tf_op jit(solution)/shard_map/all_gather | solution.py:93
  66.8 11.2 %convolution_convert_fusion = f32[96,2,18432]{2,0,1:T(8,128)} fusion(s32[96]{0:T(128)S(1)} %get-tuple-element.12, bf16[8,8,2,18432]{3,2,1,0:T(2,128)(2,1)} %bitcast.44), kind=kOutput, calls=%fused_computation | convolution fusion | flops 456529920 | bytes 18874752 | tf_op jit(solution)/shard_map/dot_general | solution.py:100
  78.0 8.8 %convolution_convert_fusion.1 = f32[96,2,18432]{2,0,1:T(8,128)} fusion(s32[96]{0:T(128)S(1)} %get-tuple-element.11, bf16[8,8,2,18432]{3,2,1,0:T(2,128)(2,1)S(1)} %bitcast.45), kind=kOutput, calls=%fused_computation.1 | convolution fusion | flops 456529920 | bytes 18874752 | tf_op jit(solution)/shard_map/dot_general | solution.py:99
  86.8 13.1 %fusion.5 = (bf16[96,18432]{1,0:T(8,128)(2,1)}, bf16[96,18432]{1,0:T(8,128)(2,1)}) fusion(f32[96,2,18432]{2,0,1:T(8,128)} %convolution_convert_fusion, f32[96,2,18432]{2,0,1:T(8,128)} %convolution_convert_fusion.1), kind=kLoop, calls=%fused_computation.9 | loop fusion | flops 14155776 | bytes 35389440 | tf_op jit(solution)/shard_map/convert_element_type | solution.py:104
  99.9 59.1 %shard_map.64 = f32[96,1664]{1,0:T(8,128)S(1)} custom-call(bf16[96,18432]{1,0:T(8,128)(2,1)} %get-tuple-element.6.real_ref, bf16[96,18432]{1,0:T(8,128)(2,1)} %get-tuple-element.5.imag_ref, f32[288,1664]{1,0:T(8,128)S(1)} %copy-done, f32[288,1664]{1,0:T(8,128)S(1)} %get-tuple-element.7.shi_ref, f32[64,1664]{1,0:T(8,128)S(1)} %get-tuple-element.10.clo_ref, ...), custom_call_target="tpu_custom_call" | custom-call | tf_op jit(solution)/shard_map/pallas_call | solution.py:59
  159.1 0.6 fusion.13
  159.7 1.2 reshape.73
  160.9 3.4 %all-to-all-start.1 = ((f32[32,4,1601]{2,1,0:T(4,128)}), f32[32,4,1601]{2,1,0:T(4,128)S(1)}, u32[]{:S(2)}, u32[]{:S(2)}) async-start(f32[32,4,1601]{2,1,0:T(4,128)} %reshape.73), calls=%async_computation.1 | async-start | bytes 1703936 | tf_op jit(solution)/shard_map/all_to_all | solution.py:121
  164.3 0.5 broadcast.54
  164.8 0.7 reduce.5
  165.6 21.9 %all-to-all-done.1 = f32[32,4,1601]{2,1,0:T(4,128)S(1)} async-done(((f32[32,4,1601]{2,1,0:T(4,128)}), f32[32,4,1601]{2,1,0:T(4,128)S(1)}, u32[]{:S(2)}, u32[]{:S(2)}) %all-to-all-start.1) | async-done | bytes 819744 | tf_op jit(solution)/shard_map/all_to_all | solution.py:121
  187.5 0.3 reshape.74
  187.8 1.4 convolution_add_fusion
  (32 shorter events, 0.7 us)
Async XLA Ops:
  6.5 4.7 %copy-start.2 = (f32[8,2,18432]{2,1,0:T(2,128)S(1)}, f32[8,2,18432]{2,1,0:T(2,128)}, u32[]{:S(2)}) copy-start(f32[8,2,18432]{2,1,0:T(2,128)} %param.6) | copy-start | bytes 3538948
  6.5 60.2 %all-gather.2.cloned.1.call-start = ((), (), s32[]{:S(2)}) async-start(), calls=%async_computation.2 | async-start | bytes 5308416 | tf_op jit(solution)/shard_map/all_gather | solution.py:93
  9.4 3.2 %copy-start.4 = (s32[96,1]{0,1:T(1,128)S(1)}, s32[96,1]{0,1:T(1,128)}, u32[]{:S(2)}) copy-start(s32[96,1]{0,1:T(1,128)} %param.10) | copy-start | bytes 1156
  9.5 3.8 %copy-start.6 = (s32[96]{0:T(128)S(1)}, s32[96]{0:T(128)}, u32[]{:S(2)}) copy-start(s32[96]{0:T(128)} %param.11) | copy-start | bytes 1156
  9.5 12.2 %copy-start.7 = (s32[96]{0:T(128)S(1)}, s32[96]{0:T(128)}, u32[]{:S(2)}) copy-start(s32[96]{0:T(128)} %param.9) | copy-start | bytes 1156
  9.5 12.3 %copy-start.5 = (s32[2,96]{1,0:T(2,128)S(1)}, s32[2,96]{1,0:T(2,128)}, u32[]{:S(2)}) copy-start(s32[2,96]{1,0:T(2,128)} %param.8) | copy-start | bytes 2308
  14.2 146.7 %all-to-all-start = ((f32[32,1,4]{2,1,0:T(1,128)}), f32[32,1,4]{2,1,0:T(1,128)S(1)}, u32[]{:S(2)}, u32[]{:S(2)}) async-start(f32[32,1,4]{2,1,0:T(1,128)} %copy.12), calls=%async_computation | async-start | bytes 32768 | tf_op jit(solution)/shard_map/all_to_all | solution.py:128
  66.8 11.2 %copy-start.1 = (bf16[64,2,18432]{2,1,0:T(2,128)(2,1)S(1)}, bf16[64,2,18432]{2,1,0:T(2,128)(2,1)}, u32[]{:S(2)}) copy-start(bf16[64,2,18432]{2,1,0:T(2,128)(2,1)} %all-gather.2.cloned.1.call-done) | copy-start | bytes 14155780
  86.8 13.1 %copy-start = (f32[288,1664]{1,0:T(8,128)S(1)}, f32[288,1664]{1,0:T(8,128)}, u32[]{:S(2)}) copy-start(f32[288,1664]{1,0:T(8,128)} %get-tuple-element.8.chi_ref) | copy-start | bytes 5750788
  159.1 28.7 %copy-start.3 = (f32[96,1601]{1,0:T(8,128)S(1)}, f32[96,1601]{1,0:T(8,128)}, u32[]{:S(2)}) copy-start(f32[96,1601]{1,0:T(8,128)} %param.7) | copy-start | bytes 1844356
  160.9 26.6 %all-to-all-start.1 = ((f32[32,4,1601]{2,1,0:T(4,128)}), f32[32,4,1601]{2,1,0:T(4,128)S(1)}, u32[]{:S(2)}, u32[]{:S(2)}) async-start(f32[32,4,1601]{2,1,0:T(4,128)} %reshape.73), calls=%async_computation.1 | async-start | bytes 1703936 | tf_op jit(solution)/shard_map/all_to_all | solution.py:121
Sparse Core Ops, SparseCore 0:
  12.8 53.9 all-gather.1

commit v3 on v2

--- a/solution.py
+++ b/solution.py
@@ -28,10 +28,17 @@
 FBLOCK = 1024
 
 
-def table_kernel(real_ref, imag_ref, chi_ref, shi_ref, clo_ref, slo_ref, out_ref, ctab, stab):
+def table_kernel(a0_ref, a1_ref, b0_ref, b1_ref, chi_ref, shi_ref, clo_ref, slo_ref, out_ref, ctab, stab):
     @pl.when(pl.program_id(0) == 0)
     def _():
         out_ref[...] = jnp.zeros_like(out_ref)
+
+    a0 = a0_ref[...].astype(jnp.float32)
+    a1 = a1_ref[...].astype(jnp.float32)
+    b0 = b0_ref[...].astype(jnp.float32)
+    b1 = b1_ref[...].astype(jnp.float32)
+    real = (a0 * b0 + a1 * b1).astype(jnp.bfloat16)
+    imag = (a1 * b0 - a0 * b1).astype(jnp.bfloat16)
 
     def fill(j, carry):
         clo = clo_ref[...]
@@ -44,24 +51,27 @@
         return carry
 
     lax.fori_loop(0, FBLOCK // LOW, fill, 0)
-    out_ref[...] += jnp.dot(real_ref[...], ctab[...], preferred_element_type=jnp.float32) + jnp.dot(
-        imag_ref[...], stab[...], preferred_element_type=jnp.float32
+    out_ref[...] += jnp.dot(real, ctab[...], preferred_element_type=jnp.float32) + jnp.dot(
+        imag, stab[...], preferred_element_type=jnp.float32
     )
 
 
-def correlate(real_all, imag_all, lag_count, total_bins):
-    pair_count = real_all.shape[0]
-    lag_pad = -(-lag_count // 128) * 128
+def correlate(first, second, lag_count, total_bins):
+    pair_count = first.shape[0]
+    lag_pad = -(-(lag_count + 1) // 128) * 128
     cos_hi, sin_hi = angle_table(lax.iota(jnp.int32, total_bins // LOW) * LOW, lag_pad, lag_count, total_bins)
     cos_lo, sin_lo = angle_table(lax.iota(jnp.int32, LOW), lag_pad, lag_count, total_bins)
     hi_rows = FBLOCK // LOW
     assert total_bins % FBLOCK == 0
+    blocks = total_bins // FBLOCK
     out = pl.pallas_call(
         table_kernel,
         grid=(total_bins // FBLOCK,),
         in_specs=[
             pl.BlockSpec((pair_count, FBLOCK), lambda i: (0, i)),
+            pl.BlockSpec((pair_count, FBLOCK), lambda i: (0, i + blocks)),
             pl.BlockSpec((pair_count, FBLOCK), lambda i: (0, i)),
+            pl.BlockSpec((pair_count, FBLOCK), lambda i: (0, i + blocks)),
             pl.BlockSpec((hi_rows, lag_pad), lambda i: (i, 0)),
             pl.BlockSpec((hi_rows, lag_pad), lambda i: (i, 0)),
             pl.BlockSpec((LOW, lag_pad), lambda i: (0, 0)),
@@ -76,8 +86,8 @@
         compiler_params=pltpu.CompilerParams(
             dimension_semantics=("arbitrary",), vmem_limit_bytes=48 * 1024 * 1024
         ),
-    )(real_all, imag_all, cos_hi, sin_hi, cos_lo, sin_lo)
-    return out[:, :lag_count]
+    )(first, first, second, second, cos_hi, sin_hi, cos_lo, sin_lo)
+    return out
 
 
 def local(spectra, stacks, pair_sta, pair_valid, owner, slot):
@@ -96,15 +106,13 @@
     sta_ids = lax.iota(jnp.int32, group_sta)[None, :]
     pick0 = (pair_sta[0][:, None] == sta_ids).astype(jnp.bfloat16)
     pick1 = (pair_sta[1][:, None] == sta_ids).astype(jnp.bfloat16)
-    first = jnp.dot(pick0, flat, preferred_element_type=jnp.bfloat16).reshape(pair_count, 2, total_bins)
-    second = jnp.dot(pick1, flat, preferred_element_type=jnp.bfloat16).reshape(pair_count, 2, total_bins)
-    first = first.astype(jnp.float32)
-    second = second.astype(jnp.float32)
-    real_all = (first[:, 0] * second[:, 0] + first[:, 1] * second[:, 1]).astype(jnp.bfloat16)
-    imag_all = (first[:, 1] * second[:, 0] - first[:, 0] * second[:, 1]).astype(jnp.bfloat16)
+    first = jnp.dot(pick0, flat, preferred_element_type=jnp.bfloat16)
+    second = jnp.dot(pick1, flat, preferred_element_type=jnp.bfloat16)
 
-    corr = correlate(real_all, imag_all, lag_count, total_bins)
+    corr = correlate(first, second, lag_count, total_bins)
     corr = corr * jnp.float32(total_bins ** (-0.5)) * pair_valid.astype(jnp.float32)[:, None]
+    column = lax.iota(jnp.int32, corr.shape[1])[None, :]
+    corr = jnp.where(column == lag_count, slot.astype(jnp.float32)[:, None], corr)
     dest = owner[:, 0]
     dest_hot = (dest[:, None] == lax.iota(jnp.int32, devices)[None, :]).astype(jnp.int32)
     before = jnp.cumsum(dest_hot, axis=0) - dest_hot
@@ -114,27 +122,15 @@
         jnp.float32
     )
     send_rows = jnp.dot(placing.T, corr, precision=lax.Precision.HIGHEST)
-    send_slots = jnp.dot(
-        placing.T, slot.astype(jnp.float32)[:, None], precision=lax.Precision.HIGHEST
-    )[:, 0]
-    got_rows, got_slots = (
-        lax.all_to_all(
-            send_rows.reshape(devices, capacity, lag_count),
-            ("grp", "sta"),
-            split_axis=0,
-            concat_axis=0,
-            tiled=True,
-        ),
-        lax.all_to_all(
-            send_slots.reshape(devices, capacity),
-            ("grp", "sta"),
-            split_axis=0,
-            concat_axis=0,
-            tiled=True,
-        ),
-    )
-    got_rows = got_rows.reshape(devices * capacity, lag_count)
-    got_slots = got_slots.reshape(devices * capacity)
+    got = lax.all_to_all(
+        send_rows.reshape(devices, capacity, corr.shape[1]),
+        ("grp", "sta"),
+        split_axis=0,
+        concat_axis=0,
+        tiled=True,
+    ).reshape(devices * capacity, corr.shape[1])
+    got_rows = got[:, :lag_count]
+    got_slots = got[:, lag_count]
     adding = (
         got_slots[None, :] == lax.iota(jnp.int32, stack_rows).astype(jnp.float32)[:, None]
     ).astype(jnp.float32)

time: 196 us -> 184 us (0.939)
  other arithmetic: 29.9 us -> 16 us
  matrix products: 22.2 us -> 11.9 us
  waiting for transfers between devices: 56.3 us -> 66 us
  starting transfers between devices: 10.9 us -> 3.36 us
  Pallas kernels: 59.1 us -> 66 us
  local copies, waits for them, and re-layouts: 4.04 us -> 6.67 us
    convert_element_type x1, other arithmetic: 13.1 us -> 0.01 us  [local(): slot.astype(jnp.float32)[:, None]]
    dot_general x3 -> x2, matrix products: 20.2 us -> 9.92 us  [the longest x1 4.99 us: local(): second = jnp.dot(pick1, flat, preferred_element_type=jnp.bfloat16)]
    all_gather x1, waiting for transfers between devices: 34.3 us -> 42.7 us  [local(): gathered = lax.all_gather(whitened, 'sta', axis=0, tiled=True)]
    all_to_all x2 -> x1, starting transfers between devices: 10.9 us -> 3.36 us  [local(): lax.all_to_all(send_rows.reshape(devices, capacity, corr.shape[1]), ('grp...]
    pallas_call x1, Pallas kernels: 59.1 us -> 66 us  [correlate(): pl.pallas_call(table_kernel, grid=(total_bins // FBLOCK,), in_specs=[pl.B...]
    unnamed x16 -> x15, local copies, waits for them, and re-layouts: 0.04 us -> 3.82 us
    all_to_all x2 -> x1, waiting for transfers between devices: 21.9 us -> 23.2 us  [local(): lax.all_to_all(send_rows.reshape(devices, capacity, corr.shape[1]), ('grp...]
  transfers between devices with their start and end apart: 3 -> 2, of which waited for: 2 -> 2; matrix products, arithmetic and copies ran while one was open for 25% -> 6% of each run, Pallas kernels for 30% -> 0%
where the time goes in v3:
time: 184 us
  waiting for transfers between devices  66 us (36%)
  Pallas kernels  66 us (36%)
  other arithmetic  16 us (9%)
  between operations  13.6 us (7%)
  matrix products  11.9 us (6%)
  local copies, waits for them, and re-layouts  6.67 us (4%)
  starting transfers between devices  3.36 us (2%)
    pallas_call x1, Pallas kernels, correlate(): pl.pallas_call(table_kernel, grid=(total_bins // FBLOCK,), in_specs=[pl.B...  66 us
    all_gather x1, waiting for transfers between devices, local(): gathered = lax.all_gather(whitened, 'sta', axis=0, tiled=True)  42.7 us
    all_to_all x1, waiting for transfers between devices, local(): lax.all_to_all(send_rows.reshape(devices, capacity, corr.shape[1]), ('grp...  23.2 us
    sin x2, other arithmetic, angle_table(): return (jnp.cos(theta), jnp.sin(theta))  10.9 us
    dot_general x1, matrix products, local(): second = jnp.dot(pick1, flat, preferred_element_type=jnp.bfloat16)  4.99 us
    dot_general x1, matrix products, local(): first = jnp.dot(pick0, flat, preferred_element_type=jnp.bfloat16)  4.94 us
    unnamed x15, local copies, waits for them, and re-layouts  3.82 us
  transfers between devices with their start and end apart: 2, of which 2 were waited for; matrix products, arithmetic and copies ran while one was open for 6% of the time, Pallas kernels for 0%

profile of v3, /device:TPU:0, one launch (start us, length us, event | category | flops | bytes accessed | tf_op | source)
XLA Modules:
  0.0 183.5 jit_solution(5658979884186591058)
XLA Ops:
  6.5 2.8 %multiply_reduce_fusion = f32[8,18432]{1,0:T(8,128)S(1)} fusion(f32[8,2,18432]{2,1,0:T(2,128)} %param.6), kind=kLoop, calls=%fused_computation.11 | loop fusion | flops 442368 | bytes 1769472 | tf_op jit(solution)/shard_map/reduce_sum | solution.py:16
  9.4 0.5 reduce_sum.30
  9.8 0.5 reduce_sum.31
  10.3 0.4 mul.111
  10.7 0.4 mul.112
  11.2 1.4 multiply_convert_fusion
  12.6 0.0 all-gather.2.cloned.1.call-update
  12.6 0.1 fusion.21
  12.7 0.1 reduce_window_sum.11
  12.9 0.2 select_reduce_fusion
  13.1 1.7 fusion.15
  14.8 9.2 %fusion.4 = (f32[288,1664]{1,0:T(8,128)S(1)}, f32[288,1664]{1,0:T(8,128)}) fusion(s32[1664]{0:T(1024)S(1)} %iota_add_fusion, s32[288]{0:T(512)S(1)} %iota_multiply_fusion), kind=kLoop, calls=%fused_computation.7 | loop fusion | flops 4313088 | bytes 3841664 | tf_op jit(solution)/shard_map/sin | solution.py:24
  24.0 42.7 %all-gather.2.cloned.1.call-done = bf16[64,2,18432]{2,1,0:T(2,128)(2,1)} async-done(((bf16[8,2,18432]{2,1,0:T(2,128)(2,1)}), bf16[64,2,18432]{2,1,0:T(2,128)(2,1)}) %all-gather.2.cloned.1.call-update) | async-done | bytes 4718608 | tf_op jit(solution)/shard_map/all_gather | solution.py:103
  66.7 3.8 %copy.8 = bf16[8,8,2,18432]{3,1,2,0:T(8,128)(2,1)S(1)} copy(bf16[8,8,2,18432]{3,2,1,0:T(2,128)(2,1)} %bitcast.17) | data formatting | bytes 9437184
  70.5 4.9 %fusion.22.a0_ref.a1_ref = bf16[96,36864]{1,0:T(8,128)(2,1)} fusion(bf16[64,36864]{1,0:T(8,128)(2,1)S(1)} %bitcast.15, s32[96]{0:T(128)S(1)} %get-tuple-element.10), kind=kOutput, calls=%fused_computation.35 | convolution fusion | flops 452990976 | bytes 11796864 | tf_op jit(solution)/shard_map/dot_general | solution.py:109
  75.4 5.0 %fusion.23.b0_ref.b1_ref = bf16[96,36864]{1,0:T(8,128)(2,1)} fusion(bf16[64,36864]{1,0:T(8,128)(2,1)S(1)} %bitcast.16, s32[96]{0:T(128)S(1)} %get-tuple-element.9), kind=kOutput, calls=%fused_computation.36 | convolution fusion | flops 452990976 | bytes 11796864 | tf_op jit(solution)/shard_map/dot_general | solution.py:110
  80.4 66.0 %shard_map.64 = f32[96,1664]{1,0:T(8,128)S(1)} custom-call(bf16[96,36864]{1,0:T(8,128)(2,1)} %fusion.22.a0_ref.a1_ref, bf16[96,36864]{1,0:T(8,128)(2,1)} %fusion.22.a0_ref.a1_ref, bf16[96,36864]{1,0:T(8,128)(2,1)} %fusion.23.b0_ref.b1_ref, bf16[96,36864]{1,0:T(8,128)(2,1)} %fusion.23.b0_ref.b1_ref, f32[288,1664]{1,0:T(8,128)S(1)} %copy-done, ...), custom_call_target="tpu_custom_call" | custom-call | tf_op jit(solution)/shard_map/pallas_call | solution.py:67
  146.4 0.6 fusion.8
  147.1 1.2 reshape.45
  148.2 3.4 %all-to-all-start = ((f32[32,4,1664]{2,1,0:T(4,128)}), f32[32,4,1664]{2,1,0:T(4,128)S(1)}, u32[]{:S(2)}, u32[]{:S(2)}) async-start(f32[32,4,1664]{2,1,0:T(4,128)} %reshape.45), calls=%async_computation | async-start | bytes 1703936 | tf_op jit(solution)/shard_map/all_to_all | solution.py:125
  151.6 23.2 %all-to-all-done = f32[32,4,1664]{2,1,0:T(4,128)S(1)} async-done(((f32[32,4,1664]{2,1,0:T(4,128)}), f32[32,4,1664]{2,1,0:T(4,128)S(1)}, u32[]{:S(2)}, u32[]{:S(2)}) %all-to-all-start) | async-done | bytes 852000 | tf_op jit(solution)/shard_map/all_to_all | solution.py:125
  174.9 0.3 reshape.46
  175.2 0.2 slice_reduce_fusion
  175.3 1.4 convolution_add_fusion
  (24 shorter events, 0.1 us)
Async XLA Ops:
  6.5 60.2 %all-gather.2.cloned.1.call-start = ((), (), s32[]{:S(2)}) async-start(), calls=%async_computation.1 | async-start | bytes 5308416 | tf_op jit(solution)/shard_map/all_gather | solution.py:103
  9.8 1.3 copy-start.1
  11.1 1.5 copy-start.5
  11.1 1.5 copy-start.3
  11.1 1.9 %copy-start.6 = (s32[96]{0:T(128)S(1)}, s32[96]{0:T(128)}, u32[]{:S(2)}) copy-start(s32[96]{0:T(128)} %param.9) | copy-start | bytes 1156
  11.1 2.0 %copy-start.4 = (s32[2,96]{1,0:T(2,128)S(1)}, s32[2,96]{1,0:T(2,128)}, u32[]{:S(2)}) copy-start(s32[2,96]{1,0:T(2,128)} %param.8) | copy-start | bytes 2308
  75.4 5.0 %copy-start = (f32[288,1664]{1,0:T(8,128)S(1)}, f32[288,1664]{1,0:T(8,128)}, u32[]{:S(2)}) copy-start(f32[288,1664]{1,0:T(8,128)} %get-tuple-element.6.chi_ref) | copy-start | bytes 5750788
  148.2 27.1 %copy-start.2 = (f32[96,1601]{1,0:T(8,128)S(1)}, f32[96,1601]{1,0:T(8,128)}, u32[]{:S(2)}) copy-start(f32[96,1601]{1,0:T(8,128)} %param.7) | copy-start | bytes 1844356
  148.2 26.6 %all-to-all-start = ((f32[32,4,1664]{2,1,0:T(4,128)}), f32[32,4,1664]{2,1,0:T(4,128)S(1)}, u32[]{:S(2)}, u32[]{:S(2)}) async-start(f32[32,4,1664]{2,1,0:T(4,128)} %reshape.45), calls=%async_computation | async-start | bytes 1703936 | tf_op jit(solution)/shard_map/all_to_all | solution.py:125
Sparse Core Ops, SparseCore 0:
  12.7 53.9 all-gather.1

commit v4 on v3

--- a/solution.py
+++ b/solution.py
@@ -26,12 +26,13 @@
 
 LOW = 64
 FBLOCK = 1024
+CHUNKS = 3
 
 
-def table_kernel(a0_ref, a1_ref, b0_ref, b1_ref, chi_ref, shi_ref, clo_ref, slo_ref, out_ref, ctab, stab):
+def table_kernel(a0_ref, a1_ref, b0_ref, b1_ref, chi_ref, shi_ref, clo_ref, slo_ref, acc_ref, out_ref, ctab, stab):
     @pl.when(pl.program_id(0) == 0)
     def _():
-        out_ref[...] = jnp.zeros_like(out_ref)
+        out_ref[...] = acc_ref[...]
 
     a0 = a0_ref[...].astype(jnp.float32)
     a1 = a1_ref[...].astype(jnp.float32)
@@ -56,17 +57,17 @@
     )
 
 
-def correlate(first, second, lag_count, total_bins):
+def correlate(first, second, tables, acc):
+    cos_hi, sin_hi, cos_lo, sin_lo = tables
     pair_count = first.shape[0]
-    lag_pad = -(-(lag_count + 1) // 128) * 128
-    cos_hi, sin_hi = angle_table(lax.iota(jnp.int32, total_bins // LOW) * LOW, lag_pad, lag_count, total_bins)
-    cos_lo, sin_lo = angle_table(lax.iota(jnp.int32, LOW), lag_pad, lag_count, total_bins)
+    lag_pad = cos_lo.shape[1]
+    width = first.shape[1] // 2
     hi_rows = FBLOCK // LOW
-    assert total_bins % FBLOCK == 0
-    blocks = total_bins // FBLOCK
+    assert width % FBLOCK == 0
+    blocks = width // FBLOCK
     out = pl.pallas_call(
         table_kernel,
-        grid=(total_bins // FBLOCK,),
+        grid=(blocks,),
         in_specs=[
             pl.BlockSpec((pair_count, FBLOCK), lambda i: (0, i)),
             pl.BlockSpec((pair_count, FBLOCK), lambda i: (0, i + blocks)),
@@ -76,6 +77,7 @@
             pl.BlockSpec((hi_rows, lag_pad), lambda i: (i, 0)),
             pl.BlockSpec((LOW, lag_pad), lambda i: (0, 0)),
             pl.BlockSpec((LOW, lag_pad), lambda i: (0, 0)),
+            pl.BlockSpec((pair_count, lag_pad), lambda i: (0, 0)),
         ],
         out_specs=pl.BlockSpec((pair_count, lag_pad), lambda i: (0, 0)),
         out_shape=jax.ShapeDtypeStruct((pair_count, lag_pad), jnp.float32),
@@ -86,7 +88,13 @@
         compiler_params=pltpu.CompilerParams(
             dimension_semantics=("arbitrary",), vmem_limit_bytes=48 * 1024 * 1024
         ),
-    )(first, first, second, second, cos_hi, sin_hi, cos_lo, sin_lo)
+        cost_estimate=pl.CostEstimate(
+            flops=2 * 2 * pair_count * width * lag_pad + 10 * width * lag_pad,
+            transcendentals=0,
+            bytes_accessed=4 * pair_count * width * 2 + 4 * pair_count * lag_pad,
+        ),
+        input_output_aliases={8: 0},
+    )(first, first, second, second, cos_hi, sin_hi, cos_lo, sin_lo, acc)
     return out
 
 
@@ -99,17 +107,27 @@
     members = lax.axis_size("sta")
     devices = groups * members
     capacity = max(2, (4 * pair_count + 3 * devices - 1) // (3 * devices))
-    whitened = whiten(spectra)
-    gathered = lax.all_gather(whitened, "sta", axis=0, tiled=True)
-    group_sta = gathered.shape[0]
-    flat = gathered.reshape(group_sta, 2 * total_bins)
+    group_sta = spectra.shape[0] * members
     sta_ids = lax.iota(jnp.int32, group_sta)[None, :]
     pick0 = (pair_sta[0][:, None] == sta_ids).astype(jnp.bfloat16)
     pick1 = (pair_sta[1][:, None] == sta_ids).astype(jnp.bfloat16)
-    first = jnp.dot(pick0, flat, preferred_element_type=jnp.bfloat16)
-    second = jnp.dot(pick1, flat, preferred_element_type=jnp.bfloat16)
-
-    corr = correlate(first, second, lag_count, total_bins)
+    lag_pad = -(-(lag_count + 1) // 128) * 128
+    hi_all = angle_table(lax.iota(jnp.int32, total_bins // LOW) * LOW, lag_pad, lag_count, total_bins)
+    lo_all = angle_table(lax.iota(jnp.int32, LOW), lag_pad, lag_count, total_bins)
+    chunks = CHUNKS if total_bins % (CHUNKS * FBLOCK) == 0 else 1
+    width = total_bins // chunks
+    corr = jnp.zeros((pair_count, lag_pad), jnp.float32)
+    for c in range(chunks):
+        piece = whiten(spectra[:, :, c * width:(c + 1) * width])
+        gathered = lax.all_gather(piece, "sta", axis=0, tiled=True)
+        if c:
+            gathered, corr = lax.optimization_barrier((gathered, corr))
+        flat = gathered.reshape(group_sta, 2 * width)
+        first = jnp.dot(pick0, flat, preferred_element_type=jnp.bfloat16)
+        second = jnp.dot(pick1, flat, preferred_element_type=jnp.bfloat16)
+        rows = slice(c * width // LOW, (c + 1) * width // LOW)
+        tables = (hi_all[0][rows], hi_all[1][rows], lo_all[0], lo_all[1])
+        corr = correlate(first, second, tables, corr)
     corr = corr * jnp.float32(total_bins ** (-0.5)) * pair_valid.astype(jnp.float32)[:, None]
     column = lax.iota(jnp.int32, corr.shape[1])[None, :]
     corr = jnp.where(column == lag_count, slot.astype(jnp.float32)[:, None], corr)

time: 184 us -> 163 us (0.89)
  waiting for transfers between devices: 66 us -> 35.4 us
  local copies, waits for them, and re-layouts: 6.67 us -> 13.5 us
  Pallas kernels: 66 us -> 68.5 us
    all_gather x1 -> x3, waiting for transfers between devices: 42.7 us -> 10.9 us  [local(): gathered = lax.all_gather(piece, 'sta', axis=0, tiled=True)]
    slice x0 -> x1, local copies, waits for them, and re-layouts: none -> 3.41 us  [local(): tables = (hi_all[0][rows], hi_all[1][rows], lo_all[0], lo_all[1])]
    unnamed x15 -> x31, local copies, waits for them, and re-layouts: 3.82 us -> 7.03 us
    dot_general x1 -> x3, matrix products: 4.94 us -> 2.42 us  [local(): first = jnp.dot(pick0, flat, preferred_element_type=jnp.bfloat16)]
    pallas_call x1 -> x3, Pallas kernels: 66 us -> 68.5 us  [correlate(): pl.pallas_call(table_kernel, grid=(blocks,), in_specs=[pl.BlockSpec((pair...]
    dot_general x1 -> x3, matrix products: 4.99 us -> 6.7 us  [local(): second = jnp.dot(pick1, flat, preferred_element_type=jnp.bfloat16)]
  transfers between devices with their start and end apart: 2 -> 4, of which waited for: 2 -> 2; matrix products, arithmetic and copies ran while one was open for 6% -> 16% of each run, Pallas kernels for 0% -> 28%
where the time goes in v4:
time: 163 us
  Pallas kernels  68.5 us (42%)
  waiting for transfers between devices  35.4 us (22%)
  other arithmetic  17 us (10%)
  local copies, waits for them, and re-layouts  13.5 us (8%)
  between operations  13.4 us (8%)
  matrix products  11.1 us (7%)
  starting transfers between devices  3.96 us (2%)
    pallas_call x3, Pallas kernels, correlate(): pl.pallas_call(table_kernel, grid=(blocks,), in_specs=[pl.BlockSpec((pair...  68.5 us
    all_to_all x1, waiting for transfers between devices, local(): lax.all_to_all(send_rows.reshape(devices, capacity, corr.shape[1]), ('grp...  23.2 us
    sin x2, other arithmetic, angle_table(): return (jnp.cos(theta), jnp.sin(theta))  11.9 us
    all_gather x3, waiting for transfers between devices, local(): gathered = lax.all_gather(piece, 'sta', axis=0, tiled=True)  10.9 us
    unnamed x31, local copies, waits for them, and re-layouts  7.03 us
    dot_general x3, matrix products, local(): second = jnp.dot(pick1, flat, preferred_element_type=jnp.bfloat16)  6.7 us
    all_to_all x1, starting transfers between devices, local(): lax.all_to_all(send_rows.reshape(devices, capacity, corr.shape[1]), ('grp...  3.7 us
    slice x1, local copies, waits for them, and re-layouts, local(): tables = (hi_all[0][rows], hi_all[1][rows], lo_all[0], lo_all[1])  3.41 us
  transfers between devices with their start and end apart: 4, of which 2 were waited for; matrix products, arithmetic and copies ran while one was open for 16% of the time, Pallas kernels for 28%

profile of v4, /device:TPU:0, one launch (start us, length us, event | category | flops | bytes accessed | tf_op | source)
XLA Modules:
  0.0 163.0 jit_solution(5489949453126378871)
XLA Ops:
  6.5 2.8 %multiply_reduce_fusion = (f32[8,6144]{1,0:T(8,128)S(1)}, f32[8,6144]{1,0:T(8,128)S(1)}, f32[8,6144]{1,0:T(8,128)S(1)}) fusion(f32[8,2,18432]{2,1,0:T(2,128)} %param.6), kind=kLoop, calls=%fused_computation.24 | loop fusion | flops 442368 | bytes 1769472 | tf_op jit(solution)/shard_map/reduce_sum | solution.py:16
  11.5 1.4 multiply_convert_fusion
  12.9 0.7 all-gather.6.cloned.1.call-update
  14.4 2.5 %fusion.15 = (f32[64,1664]{1,0:T(8,128)}, f32[64,1664]{1,0:T(8,128)}) fusion(s32[1664]{0:T(1024)S(1)} %iota_add_fusion), kind=kLoop, calls=%fused_computation.20 | loop fusion | flops 958464 | bytes 858624 | tf_op jit(solution)/shard_map/sin | solution.py:24
  16.9 9.3 %fusion.4 = (f32[288,1664]{1,0:T(8,128)}, f32[288,1664]{1,0:T(8,128)}) fusion(s32[1664]{0:T(1024)S(1)} %iota_add_fusion, s32[288]{0:T(512)S(1)} %iota_multiply_fusion), kind=kLoop, calls=%fused_computation.7 | loop fusion | flops 4313088 | bytes 3841664 | tf_op jit(solution)/shard_map/sin | solution.py:24
  26.7 3.4 %fusion.39 = (f32[96,1664]{1,0:T(8,128)S(1)}, f32[96,1664]{1,0:T(8,128)S(1)}, f32[96,1664]{1,0:T(8,128)}, f32[96,1664]{1,0:T(8,128)}, f32[96,1664]{1,0:T(8,128)S(1)}, /*index=5*/f32[96,1664]{1,0:T(8,128)S(1)}) fusion(f32[288,1664]{1,0:T(8,128)} %get-tuple-element.25, f32[288,1664]{1,0:T(8,128)} %get-tuple-element.26), kind=kLoop, calls=%fused_computation.67 | loop fusion | bytes 7667712 | tf_op jit(solution)/shard_map/slice | solution.py:129
  30.1 10.9 %all-gather.8.cloned.1.call-done = bf16[64,2,6144]{2,1,0:T(2,128)(2,1)} async-done(((bf16[8,2,6144]{2,1,0:T(2,128)(2,1)}), bf16[64,2,6144]{2,1,0:T(2,128)(2,1)}) %all-gather.8.cloned.1.call-update) | async-done | bytes 1572880 | tf_op jit(solution)/shard_map/all_gather | solution.py:122
  41.0 1.9 %copy.11 = bf16[8,8,2,6144]{3,1,2,0:T(8,128)(2,1)S(1)} copy(bf16[8,8,2,6144]{3,2,1,0:T(2,128)(2,1)} %bitcast.31) | data formatting | bytes 3145728
  42.9 2.2 %fusion.23.b0_ref.b1_ref = bf16[96,12288]{1,0:T(8,128)(2,1)} fusion(bf16[64,12288]{1,0:T(8,128)(2,1)S(1)} %bitcast.25, s32[96]{0:T(128)S(1)} %get-tuple-element.29), kind=kOutput, calls=%fused_computation.36 | convolution fusion | flops 151001088 | bytes 3932544 | tf_op jit(solution)/shard_map/dot_general | solution.py:127
  45.2 0.8 fusion.26.a0_ref.a1_ref
  46.7 22.8 %shard_map.64.acc_ref = f32[96,1664]{1,0:T(8,128)S(1)} custom-call(bf16[96,12288]{1,0:T(8,128)(2,1)S(1)} %fusion.26.a0_ref.a1_ref, bf16[96,12288]{1,0:T(8,128)(2,1)S(1)} %fusion.26.a0_ref.a1_ref, bf16[96,12288]{1,0:T(8,128)(2,1)} %fusion.23.b0_ref.b1_ref, bf16[96,12288]{1,0:T(8,128)(2,1)} %fusion.23.b0_ref.b1_ref, ...), custom_call_target="tpu_custom_call", output_to_operand_aliasing={{}: (8, {})} | custom-call | flops 4028104704 | bytes 5357568 | tf_op jit(solution)/shard_map/pallas_call | solution.py:68
  69.5 1.9 %copy.12 = bf16[8,8,2,6144]{3,1,2,0:T(8,128)(2,1)S(1)} copy(bf16[8,8,2,6144]{3,2,1,0:T(2,128)(2,1)} %bitcast.30) | data formatting | bytes 3145728
  71.4 2.2 %fusion.22.b0_ref.b1_ref = bf16[96,12288]{1,0:T(8,128)(2,1)} fusion(bf16[64,12288]{1,0:T(8,128)(2,1)S(1)} %bitcast.27, s32[96]{0:T(128)S(1)} %get-tuple-element.29), kind=kOutput, calls=%fused_computation.35 | convolution fusion | flops 151001088 | bytes 3932544 | tf_op jit(solution)/shard_map/dot_general | solution.py:127
  73.7 0.8 fusion.25.a0_ref.a1_ref
  74.8 22.8 %shard_map.65.acc_ref = f32[96,1664]{1,0:T(8,128)S(1)} custom-call(bf16[96,12288]{1,0:T(8,128)(2,1)S(1)} %fusion.25.a0_ref.a1_ref, bf16[96,12288]{1,0:T(8,128)(2,1)S(1)} %fusion.25.a0_ref.a1_ref, bf16[96,12288]{1,0:T(8,128)(2,1)} %fusion.22.b0_ref.b1_ref, bf16[96,12288]{1,0:T(8,128)(2,1)} %fusion.22.b0_ref.b1_ref, ...), custom_call_target="tpu_custom_call", output_to_operand_aliasing={{}: (8, {})} | custom-call | flops 4028104704 | bytes 5357568 | tf_op jit(solution)/shard_map/pallas_call | solution.py:68
  97.7 1.9 %copy.13 = bf16[8,8,2,6144]{3,1,2,0:T(8,128)(2,1)S(1)} copy(bf16[8,8,2,6144]{3,2,1,0:T(2,128)(2,1)} %bitcast.29) | data formatting | bytes 3145728
  99.6 2.2 %fusion.21.b0_ref.b1_ref = bf16[96,12288]{1,0:T(8,128)(2,1)} fusion(bf16[64,12288]{1,0:T(8,128)(2,1)S(1)} %bitcast.23, s32[96]{0:T(128)S(1)} %get-tuple-element.29), kind=kOutput, calls=%fused_computation.34 | convolution fusion | flops 151001088 | bytes 3932544 | tf_op jit(solution)/shard_map/dot_general | solution.py:127
  101.8 0.8 fusion.24.a0_ref.a1_ref
  103.0 22.8 %shard_map.66 = f32[96,1664]{1,0:T(8,128)S(1)} custom-call(bf16[96,12288]{1,0:T(8,128)(2,1)S(1)} %fusion.24.a0_ref.a1_ref, bf16[96,12288]{1,0:T(8,128)(2,1)S(1)} %fusion.24.a0_ref.a1_ref, bf16[96,12288]{1,0:T(8,128)(2,1)} %fusion.21.b0_ref.b1_ref, bf16[96,12288]{1,0:T(8,128)(2,1)} %fusion.21.b0_ref.b1_ref, ...), custom_call_target="tpu_custom_call", output_to_operand_aliasing={{}: (8, {})} | custom-call | flops 4028104704 | bytes 5357568 | tf_op jit(solution)/shard_map/pallas_call | solution.py:68
  125.8 0.6 fusion.8
  126.5 1.2 reshape.77
  127.6 3.7 %all-to-all-start = ((f32[32,4,1664]{2,1,0:T(4,128)}), f32[32,4,1664]{2,1,0:T(4,128)S(1)}, u32[]{:S(2)}, u32[]{:S(2)}) async-start(f32[32,4,1664]{2,1,0:T(4,128)} %reshape.77), calls=%async_computation | async-start | bytes 1703936 | tf_op jit(solution)/shard_map/all_to_all | solution.py:143
  131.3 23.2 %all-to-all-done = f32[32,4,1664]{2,1,0:T(4,128)S(1)} async-done(((f32[32,4,1664]{2,1,0:T(4,128)}), f32[32,4,1664]{2,1,0:T(4,128)S(1)}, u32[]{:S(2)}, u32[]{:S(2)}) %all-to-all-start) | async-done | bytes 852000 | tf_op jit(solution)/shard_map/all_to_all | solution.py:143
  155.1 1.4 convolution_add_fusion
  (64 shorter events, 5.1 us)
Async XLA Ops:
  6.5 34.5 %all-gather.8.cloned.1.call-start = ((), (), s32[]{:S(2)}) async-start(), calls=%async_computation.3 | async-start | bytes 1769472 | tf_op jit(solution)/shard_map/all_gather | solution.py:122
  10.0 1.4 copy-start.8
  11.2 3.2 %copy-start.11 = (s32[2,96]{1,0:T(2,128)S(1)}, s32[2,96]{1,0:T(2,128)}, u32[]{:S(2)}) copy-start(s32[2,96]{1,0:T(2,128)} %param.8) | copy-start | bytes 2308
  12.9 56.7 %all-gather.6.cloned.1.call-start = ((), (), s32[]{:S(2)}) async-start(), calls=%async_computation.2 | async-start | bytes 1769472 | tf_op jit(solution)/shard_map/all_gather | solution.py:122
  13.6 84.1 %all-gather.4.cloned.1.call-start = ((), (), s32[]{:S(2)}) async-start(), calls=%async_computation.1 | async-start | bytes 1769472 | tf_op jit(solution)/shard_map/all_gather | solution.py:122
  16.9 9.3 %copy-start.10 = (s32[96,1]{0,1:T(1,128)S(1)}, s32[96,1]{0,1:T(1,128)}, u32[]{:S(2)}) copy-start(s32[96,1]{0,1:T(1,128)} %param.10) | copy-start | bytes 1156
  16.9 9.7 %copy-start.12 = (s32[96]{0:T(128)S(1)}, s32[96]{0:T(128)}, u32[]{:S(2)}) copy-start(s32[96]{0:T(128)} %param.11) | copy-start | bytes 1156
  16.9 9.8 %copy-start.13 = (s32[96]{0:T(128)S(1)}, s32[96]{0:T(128)}, u32[]{:S(2)}) copy-start(s32[96]{0:T(128)} %param.9) | copy-start | bytes 1156
  45.2 1.1 copy-start
  45.2 1.3 copy-start.1
  45.2 1.4 copy-start.2
  45.2 1.5 copy-start.5
  73.7 1.0 copy-start.3
  73.7 1.2 copy-start.6
  101.8 1.0 copy-start.4
  101.8 1.1 copy-start.7
  127.6 27.4 %copy-start.9 = (f32[96,1601]{1,0:T(8,128)S(1)}, f32[96,1601]{1,0:T(8,128)}, u32[]{:S(2)}) copy-start(f32[96,1601]{1,0:T(8,128)} %param.7) | copy-start | bytes 1844356
  127.6 27.0 %all-to-all-start = ((f32[32,4,1664]{2,1,0:T(4,128)}), f32[32,4,1664]{2,1,0:T(4,128)S(1)}, u32[]{:S(2)}, u32[]{:S(2)}) async-start(f32[32,4,1664]{2,1,0:T(4,128)} %reshape.77), calls=%async_computation | async-start | bytes 1703936 | tf_op jit(solution)/shard_map/all_to_all | solution.py:143
Sparse Core Ops, SparseCore 0:
  13.0 27.9 all-gather.7
  42.7 24.4 all-gather.5
  68.8 24.3 all-gather.3

commit v5 on v4

--- a/solution.py
+++ b/solution.py
@@ -17,8 +17,8 @@
     return (split * lax.rsqrt(power + 1e-06)).reshape(shape).astype(jnp.bfloat16)
 
 
-def angle_table(freqs, lag_pad, lag_count, total_bins):
-    shifts = lax.iota(jnp.int32, lag_pad) - (lag_count - 1) // 2
+def angle_table(freqs, lag_pad, total_bins):
+    shifts = lax.iota(jnp.int32, lag_pad)
     angle_ids = jnp.mod(freqs[:, None] * shifts[None, :], 2 * total_bins)
     theta = angle_ids.astype(jnp.float32) * jnp.float32(math.pi / total_bins)
     return jnp.cos(theta), jnp.sin(theta)
@@ -48,13 +48,13 @@
         sh = shi_ref[pl.ds(j, 1), :]
         rows = pl.ds(pl.multiple_of(j * LOW, LOW), LOW)
         ctab[rows, :] = (ch * clo - sh * slo).astype(jnp.bfloat16)
-        stab[rows, :] = (-(sh * clo + ch * slo)).astype(jnp.bfloat16)
+        stab[rows, :] = (sh * clo + ch * slo).astype(jnp.bfloat16)
         return carry
 
     lax.fori_loop(0, FBLOCK // LOW, fill, 0)
-    out_ref[...] += jnp.dot(real, ctab[...], preferred_element_type=jnp.float32) + jnp.dot(
-        imag, stab[...], preferred_element_type=jnp.float32
-    )
+    half = ctab.shape[1]
+    out_ref[:, :half] += jnp.dot(real, ctab[...], preferred_element_type=jnp.float32)
+    out_ref[:, half:] += jnp.dot(imag, stab[...], preferred_element_type=jnp.float32)
 
 
 def correlate(first, second, tables, acc):
@@ -77,10 +77,10 @@
             pl.BlockSpec((hi_rows, lag_pad), lambda i: (i, 0)),
             pl.BlockSpec((LOW, lag_pad), lambda i: (0, 0)),
             pl.BlockSpec((LOW, lag_pad), lambda i: (0, 0)),
-            pl.BlockSpec((pair_count, lag_pad), lambda i: (0, 0)),
+            pl.BlockSpec((pair_count, 2 * lag_pad), lambda i: (0, 0)),
         ],
-        out_specs=pl.BlockSpec((pair_count, lag_pad), lambda i: (0, 0)),
-        out_shape=jax.ShapeDtypeStruct((pair_count, lag_pad), jnp.float32),
+        out_specs=pl.BlockSpec((pair_count, 2 * lag_pad), lambda i: (0, 0)),
+        out_shape=jax.ShapeDtypeStruct((pair_count, 2 * lag_pad), jnp.float32),
         scratch_shapes=[
             pltpu.VMEM((FBLOCK, lag_pad), jnp.bfloat16),
             pltpu.VMEM((FBLOCK, lag_pad), jnp.bfloat16),
@@ -111,12 +111,14 @@
     sta_ids = lax.iota(jnp.int32, group_sta)[None, :]
     pick0 = (pair_sta[0][:, None] == sta_ids).astype(jnp.bfloat16)
     pick1 = (pair_sta[1][:, None] == sta_ids).astype(jnp.bfloat16)
-    lag_pad = -(-(lag_count + 1) // 128) * 128
-    hi_all = angle_table(lax.iota(jnp.int32, total_bins // LOW) * LOW, lag_pad, lag_count, total_bins)
-    lo_all = angle_table(lax.iota(jnp.int32, LOW), lag_pad, lag_count, total_bins)
+    assert lag_count % 2 == 1
+    side = (lag_count - 1) // 2
+    lag_pad = -(-(side + 1) // 128) * 128
+    hi_all = angle_table(lax.iota(jnp.int32, total_bins // LOW) * LOW, lag_pad, total_bins)
+    lo_all = angle_table(lax.iota(jnp.int32, LOW), lag_pad, total_bins)
     chunks = CHUNKS if total_bins % (CHUNKS * FBLOCK) == 0 else 1
     width = total_bins // chunks
-    corr = jnp.zeros((pair_count, lag_pad), jnp.float32)
+    corr = jnp.zeros((pair_count, 2 * lag_pad), jnp.float32)
     for c in range(chunks):
         piece = whiten(spectra[:, :, c * width:(c + 1) * width])
         gathered = lax.all_gather(piece, "sta", axis=0, tiled=True)
@@ -128,9 +130,15 @@
         rows = slice(c * width // LOW, (c + 1) * width // LOW)
         tables = (hi_all[0][rows], hi_all[1][rows], lo_all[0], lo_all[1])
         corr = correlate(first, second, tables, corr)
+    even = corr[:, : side + 1]
+    odd = corr[:, lag_pad : lag_pad + side + 1]
+    corr = jnp.concatenate([(even + odd)[:, :0:-1], even - odd], axis=1)
     corr = corr * jnp.float32(total_bins ** (-0.5)) * pair_valid.astype(jnp.float32)[:, None]
-    column = lax.iota(jnp.int32, corr.shape[1])[None, :]
-    corr = jnp.where(column == lag_count, slot.astype(jnp.float32)[:, None], corr)
+    lag_ext = -(-(lag_count + 1) // 128) * 128
+    corr = jnp.concatenate(
+        [corr, slot.astype(jnp.float32)[:, None], jnp.zeros((pair_count, lag_ext - lag_count - 1), jnp.float32)],
+        axis=1,
+    )
     dest = owner[:, 0]
     dest_hot = (dest[:, None] == lax.iota(jnp.int32, devices)[None, :]).astype(jnp.int32)
     before = jnp.cumsum(dest_hot, axis=0) - dest_hot

time: 163 us -> 152 us (0.933)
  Pallas kernels: 68.5 us -> 43.9 us
  waiting for transfers between devices: 35.4 us -> 58 us
  other arithmetic: 17 us -> 10.8 us
  local copies, waits for them, and re-layouts: 13.5 us -> 10.1 us
    pallas_call x3, Pallas kernels: 68.5 us -> 43.9 us  [correlate(): pl.pallas_call(table_kernel, grid=(blocks,), in_specs=[pl.BlockSpec((pair...]
    all_gather x3, waiting for transfers between devices: 10.9 us -> 33.6 us  [local(): gathered = lax.all_gather(piece, 'sta', axis=0, tiled=True)]
    sin x2, other arithmetic: 11.9 us -> 5.17 us  [angle_table(): return (jnp.cos(theta), jnp.sin(theta))]
    slice x1, local copies, waits for them, and re-layouts: 3.41 us -> 0.14 us  [local(): tables = (hi_all[0][rows], hi_all[1][rows], lo_all[0], lo_all[1])]
    unnamed x31 -> x17, local copies, waits for them, and re-layouts: 7.03 us -> 6.68 us
  transfers between devices with their start and end apart: 4 -> 4, of which waited for: 2 -> 4; matrix products, arithmetic and copies ran while one was open for 16% -> 10% of each run, Pallas kernels for 28% -> 19%
where the time goes in v5:
time: 152 us; the launch traced here: 151 us
  waiting for transfers between devices  58 us (38%)
  Pallas kernels  43.9 us (29%)
  between operations  13.4 us (9%)
  matrix products  11.1 us (7%)
  other arithmetic  10.8 us (7%)
  local copies, waits for them, and re-layouts  10.1 us (7%)
  starting transfers between devices  3.99 us (3%)
    pallas_call x3, Pallas kernels, correlate(): pl.pallas_call(table_kernel, grid=(blocks,), in_specs=[pl.BlockSpec((pair...  43.9 us
    all_gather x3, waiting for transfers between devices, local(): gathered = lax.all_gather(piece, 'sta', axis=0, tiled=True)  33.6 us
    all_to_all x1, waiting for transfers between devices, local(): lax.all_to_all(send_rows.reshape(devices, capacity, corr.shape[1]), ('grp...  23.2 us
    dot_general x3, matrix products, local(): second = jnp.dot(pick1, flat, preferred_element_type=jnp.bfloat16)  6.68 us
    unnamed x17, local copies, waits for them, and re-layouts  6.68 us
    sin x2, other arithmetic, angle_table(): return (jnp.cos(theta), jnp.sin(theta))  5.17 us
    all_to_all x1, starting transfers between devices, local(): lax.all_to_all(send_rows.reshape(devices, capacity, corr.shape[1]), ('grp...  3.73 us
    reduce_sum x4, other arithmetic, whiten(): power = jnp.mean(split * split, axis=(1, 3), keepdims=True)  3.41 us
  transfers between devices with their start and end apart: 4, of which 4 were waited for; matrix products, arithmetic and copies ran while one was open for 10% of the time, Pallas kernels for 19%

profile of v5, /device:TPU:0, one launch (start us, length us, event | category | flops | bytes accessed | tf_op | source)
XLA Modules:
  0.0 151.4 jit_solution(3817075447330742819)
XLA Ops:
  6.5 2.8 %multiply_reduce_fusion = (f32[8,6144]{1,0:T(8,128)S(1)}, f32[8,6144]{1,0:T(8,128)S(1)}, f32[8,6144]{1,0:T(8,128)S(1)}) fusion(f32[8,2,18432]{2,1,0:T(2,128)} %param.6), kind=kLoop, calls=%fused_computation.13 | loop fusion | flops 442368 | bytes 1769472 | tf_op jit(solution)/shard_map/reduce_sum | solution.py:16
  11.7 1.4 multiply_convert_fusion
  13.1 0.7 all-gather.6.cloned.1.call-update
  14.6 0.9 fusion.12
  16.1 4.2 %fusion.4 = (f32[288,896]{1,0:T(8,128)S(1)}, f32[288,896]{1,0:T(8,128)S(1)}) fusion(s32[288]{0:T(512)S(1)} %iota_multiply_fusion), kind=kLoop, calls=%fused_computation.7 | loop fusion | flops 2322432 | bytes 2065536 | tf_op jit(solution)/shard_map/sin | solution.py:24
  20.5 20.7 %all-gather.8.cloned.1.call-done = bf16[64,2,6144]{2,1,0:T(2,128)(2,1)} async-done(((bf16[8,2,6144]{2,1,0:T(2,128)(2,1)}), bf16[64,2,6144]{2,1,0:T(2,128)(2,1)}) %all-gather.8.cloned.1.call-update) | async-done | bytes 1572880 | tf_op jit(solution)/shard_map/all_gather | solution.py:124
  41.2 1.9 %copy.15 = bf16[8,8,2,6144]{3,1,2,0:T(8,128)(2,1)S(1)} copy(bf16[8,8,2,6144]{3,2,1,0:T(2,128)(2,1)} %bitcast.35) | data formatting | bytes 3145728
  43.1 2.2 %fusion.17.b0_ref.b1_ref = bf16[96,12288]{1,0:T(8,128)(2,1)} fusion(bf16[64,12288]{1,0:T(8,128)(2,1)S(1)} %bitcast.29, s32[96]{0:T(128)S(1)} %get-tuple-element.30), kind=kOutput, calls=%fused_computation.32 | convolution fusion | flops 151001088 | bytes 3932544 | tf_op jit(solution)/shard_map/dot_general | solution.py:129
  45.4 0.8 fusion.20.a0_ref.a1_ref
  46.2 14.8 %shard_map.64.acc_ref = f32[96,1792]{1,0:T(8,128)S(1)} custom-call(bf16[96,12288]{1,0:T(8,128)(2,1)S(1)} %fusion.20.a0_ref.a1_ref, bf16[96,12288]{1,0:T(8,128)(2,1)S(1)} %fusion.20.a0_ref.a1_ref, bf16[96,12288]{1,0:T(8,128)(2,1)} %fusion.17.b0_ref.b1_ref, bf16[96,12288]{1,0:T(8,128)(2,1)} %fusion.17.b0_ref.b1_ref, ...), custom_call_target="tpu_custom_call", output_to_operand_aliasing={{}: (8, {})} | custom-call | flops 2168979456 | bytes 5062656 | tf_op jit(solution)/shard_map/pallas_call | solution.py:68
  61.0 6.3 %all-gather.6.cloned.1.call-done = bf16[64,2,6144]{2,1,0:T(2,128)(2,1)} async-done(((bf16[8,2,6144]{2,1,0:T(2,128)(2,1)}), bf16[64,2,6144]{2,1,0:T(2,128)(2,1)}) %all-gather.6.cloned.1.call-update) | async-done | bytes 1572880 | tf_op jit(solution)/shard_map/all_gather | solution.py:124
  67.3 1.9 %copy.16 = bf16[8,8,2,6144]{3,1,2,0:T(8,128)(2,1)S(1)} copy(bf16[8,8,2,6144]{3,2,1,0:T(2,128)(2,1)} %bitcast.34) | data formatting | bytes 3145728
  69.2 2.2 %fusion.16.b0_ref.b1_ref = bf16[96,12288]{1,0:T(8,128)(2,1)} fusion(bf16[64,12288]{1,0:T(8,128)(2,1)S(1)} %bitcast.31, s32[96]{0:T(128)S(1)} %get-tuple-element.30), kind=kOutput, calls=%fused_computation.31 | convolution fusion | flops 151001088 | bytes 3932544 | tf_op jit(solution)/shard_map/dot_general | solution.py:129
  71.4 0.8 fusion.19.a0_ref.a1_ref
  72.2 14.6 %shard_map.65.acc_ref = f32[96,1792]{1,0:T(8,128)S(1)} custom-call(bf16[96,12288]{1,0:T(8,128)(2,1)S(1)} %fusion.19.a0_ref.a1_ref, bf16[96,12288]{1,0:T(8,128)(2,1)S(1)} %fusion.19.a0_ref.a1_ref, bf16[96,12288]{1,0:T(8,128)(2,1)} %fusion.16.b0_ref.b1_ref, bf16[96,12288]{1,0:T(8,128)(2,1)} %fusion.16.b0_ref.b1_ref, ...), custom_call_target="tpu_custom_call", output_to_operand_aliasing={{}: (8, {})} | custom-call | flops 2168979456 | bytes 5062656 | tf_op jit(solution)/shard_map/pallas_call | solution.py:68
  86.8 6.6 %all-gather.4.cloned.1.call-done = bf16[64,2,6144]{2,1,0:T(2,128)(2,1)} async-done(((bf16[8,2,6144]{2,1,0:T(2,128)(2,1)}), bf16[64,2,6144]{2,1,0:T(2,128)(2,1)}) %all-gather.4.cloned.1.call-update) | async-done | bytes 1572880 | tf_op jit(solution)/shard_map/all_gather | solution.py:124
  93.4 1.9 %copy.17 = bf16[8,8,2,6144]{3,1,2,0:T(8,128)(2,1)S(1)} copy(bf16[8,8,2,6144]{3,2,1,0:T(2,128)(2,1)} %bitcast.33) | data formatting | bytes 3145728
  95.3 2.2 %fusion.15.b0_ref.b1_ref = bf16[96,12288]{1,0:T(8,128)(2,1)} fusion(bf16[64,12288]{1,0:T(8,128)(2,1)S(1)} %bitcast.27, s32[96]{0:T(128)S(1)} %get-tuple-element.30), kind=kOutput, calls=%fused_computation.30 | convolution fusion | flops 151001088 | bytes 3932544 | tf_op jit(solution)/shard_map/dot_general | solution.py:129
  97.5 0.8 fusion.18.a0_ref.a1_ref
  98.3 14.6 %shard_map.66 = f32[96,1792]{1,0:T(8,128)S(1)} custom-call(bf16[96,12288]{1,0:T(8,128)(2,1)S(1)} %fusion.18.a0_ref.a1_ref, bf16[96,12288]{1,0:T(8,128)(2,1)S(1)} %fusion.18.a0_ref.a1_ref, bf16[96,12288]{1,0:T(8,128)(2,1)} %fusion.15.b0_ref.b1_ref, bf16[96,12288]{1,0:T(8,128)(2,1)} %fusion.15.b0_ref.b1_ref, ...), custom_call_target="tpu_custom_call", output_to_operand_aliasing={{}: (8, {})} | custom-call | flops 2168979456 | bytes 5062656 | tf_op jit(solution)/shard_map/pallas_call | solution.py:68
  114.9 1.2 reshape.67
  116.1 3.7 %all-to-all-start = ((f32[32,4,1664]{2,1,0:T(4,128)}), f32[32,4,1664]{2,1,0:T(4,128)S(1)}, u32[]{:S(2)}, u32[]{:S(2)}) async-start(f32[32,4,1664]{2,1,0:T(4,128)} %reshape.67), calls=%async_computation | async-start | bytes 1703936 | tf_op jit(solution)/shard_map/all_to_all | solution.py:151
  119.8 23.2 %all-to-all-done = f32[32,4,1664]{2,1,0:T(4,128)S(1)} async-done(((f32[32,4,1664]{2,1,0:T(4,128)}), f32[32,4,1664]{2,1,0:T(4,128)S(1)}, u32[]{:S(2)}, u32[]{:S(2)}) %all-to-all-start) | async-done | bytes 852000 | tf_op jit(solution)/shard_map/all_to_all | solution.py:151
  143.5 1.4 convolution_add_fusion
  (54 shorter events, 6.2 us)
Async XLA Ops:
  6.5 34.7 %all-gather.8.cloned.1.call-start = ((), (), s32[]{:S(2)}) async-start(), calls=%async_computation.3 | async-start | bytes 1769472 | tf_op jit(solution)/shard_map/all_gather | solution.py:124
  10.4 1.3 copy-start
  11.7 3.8 %copy-start.4 = (s32[96]{0:T(128)S(1)}, s32[96]{0:T(128)}, u32[]{:S(2)}) copy-start(s32[96]{0:T(128)} %param.9) | copy-start | bytes 1156
  11.7 3.8 %copy-start.5 = (s32[96]{0:T(128)S(1)}, s32[96]{0:T(128)}, u32[]{:S(2)}) copy-start(s32[96]{0:T(128)} %param.11) | copy-start | bytes 1156
  11.7 3.9 %copy-start.2 = (s32[96,1]{0,1:T(1,128)S(1)}, s32[96,1]{0,1:T(1,128)}, u32[]{:S(2)}) copy-start(s32[96,1]{0,1:T(1,128)} %param.10) | copy-start | bytes 1156
  11.7 4.4 %copy-start.3 = (s32[2,96]{1,0:T(2,128)S(1)}, s32[2,96]{1,0:T(2,128)}, u32[]{:S(2)}) copy-start(s32[2,96]{1,0:T(2,128)} %param.8) | copy-start | bytes 2308
  13.1 54.2 %all-gather.6.cloned.1.call-start = ((), (), s32[]{:S(2)}) async-start(), calls=%async_computation.2 | async-start | bytes 1769472 | tf_op jit(solution)/shard_map/all_gather | solution.py:124
  13.8 79.5 %all-gather.4.cloned.1.call-start = ((), (), s32[]{:S(2)}) async-start(), calls=%async_computation.1 | async-start | bytes 1769472 | tf_op jit(solution)/shard_map/all_gather | solution.py:124
  116.1 27.5 %copy-start.1 = (f32[96,1601]{1,0:T(8,128)S(1)}, f32[96,1601]{1,0:T(8,128)}, u32[]{:S(2)}) copy-start(f32[96,1601]{1,0:T(8,128)} %param.7) | copy-start | bytes 1844356
  116.1 27.0 %all-to-all-start = ((f32[32,4,1664]{2,1,0:T(4,128)}), f32[32,4,1664]{2,1,0:T(4,128)S(1)}, u32[]{:S(2)}, u32[]{:S(2)}) async-start(f32[32,4,1664]{2,1,0:T(4,128)} %reshape.67), calls=%async_computation | async-start | bytes 1703936 | tf_op jit(solution)/shard_map/all_to_all | solution.py:151
Sparse Core Ops, SparseCore 0:
  13.2 27.9 all-gather.7
  42.9 24.3 all-gather.5
  68.9 24.3 all-gather.3

commit v6 on v5

--- a/solution.py
+++ b/solution.py
@@ -26,7 +26,6 @@
 
 LOW = 64
 FBLOCK = 1024
-CHUNKS = 3
 
 
 def table_kernel(a0_ref, a1_ref, b0_ref, b1_ref, chi_ref, shi_ref, clo_ref, slo_ref, acc_ref, out_ref, ctab, stab):
@@ -116,18 +115,22 @@
     lag_pad = -(-(side + 1) // 128) * 128
     hi_all = angle_table(lax.iota(jnp.int32, total_bins // LOW) * LOW, lag_pad, total_bins)
     lo_all = angle_table(lax.iota(jnp.int32, LOW), lag_pad, total_bins)
-    chunks = CHUNKS if total_bins % (CHUNKS * FBLOCK) == 0 else 1
-    width = total_bins // chunks
+    blocks = total_bins // FBLOCK
+    assert total_bins % FBLOCK == 0
+    lead = max(1, min(blocks - 1, (blocks * 31 + 25) // 50))
+    bounds = [0, lead * FBLOCK, total_bins] if blocks > 1 else [0, total_bins]
     corr = jnp.zeros((pair_count, 2 * lag_pad), jnp.float32)
-    for c in range(chunks):
-        piece = whiten(spectra[:, :, c * width:(c + 1) * width])
+    for c in range(len(bounds) - 1):
+        begin, end = bounds[c], bounds[c + 1]
+        width = end - begin
+        piece = whiten(spectra[:, :, begin:end])
         gathered = lax.all_gather(piece, "sta", axis=0, tiled=True)
         if c:
             gathered, corr = lax.optimization_barrier((gathered, corr))
         flat = gathered.reshape(group_sta, 2 * width)
         first = jnp.dot(pick0, flat, preferred_element_type=jnp.bfloat16)
         second = jnp.dot(pick1, flat, preferred_element_type=jnp.bfloat16)
-        rows = slice(c * width // LOW, (c + 1) * width // LOW)
+        rows = slice(begin // LOW, end // LOW)
         tables = (hi_all[0][rows], hi_all[1][rows], lo_all[0], lo_all[1])
         corr = correlate(first, second, tables, corr)
     even = corr[:, : side + 1]

time: 152 us -> 146 us (0.961)
  waiting for transfers between devices: 58 us -> 53.6 us
  local copies, waits for them, and re-layouts: 10.1 us -> 8.19 us
    all_gather x3 -> x2, waiting for transfers between devices: 33.6 us -> 30.4 us  [local(): gathered = lax.all_gather(piece, 'sta', axis=0, tiled=True)]
    dot_general x3 -> x2, matrix products: 2.42 us -> 4.21 us  [local(): first = jnp.dot(pick0, flat, preferred_element_type=jnp.bfloat16)]
    unnamed x17 -> x16, local copies, waits for them, and re-layouts: 6.68 us -> 5.04 us
    pallas_call x3 -> x2, Pallas kernels: 43.9 us -> 42.7 us  [correlate(): pl.pallas_call(table_kernel, grid=(blocks,), in_specs=[pl.BlockSpec((pair...]
    dot_general x3 -> x2, matrix products: 6.68 us -> 5.79 us  [local(): second = jnp.dot(pick1, flat, preferred_element_type=jnp.bfloat16)]
  transfers between devices with their start and end apart: 4 -> 3, of which waited for: 4 -> 2; matrix products, arithmetic and copies ran while one was open for 10% -> 12% of each run, Pallas kernels for 19% -> 18%
where the time goes in v6:
time: 146 us
  waiting for transfers between devices  53.6 us (37%)
  Pallas kernels  42.7 us (29%)
  between operations  13.7 us (9%)
  matrix products  12 us (8%)
  other arithmetic  11.4 us (8%)
  local copies, waits for them, and re-layouts  8.19 us (6%)
  starting transfers between devices  4.01 us (3%)
    pallas_call x2, Pallas kernels, correlate(): pl.pallas_call(table_kernel, grid=(blocks,), in_specs=[pl.BlockSpec((pair...  42.7 us
    all_gather x2, waiting for transfers between devices, local(): gathered = lax.all_gather(piece, 'sta', axis=0, tiled=True)  30.4 us
    all_to_all x1, waiting for transfers between devices, local(): lax.all_to_all(send_rows.reshape(devices, capacity, corr.shape[1]), ('grp...  23.2 us
    dot_general x2, matrix products, local(): second = jnp.dot(pick1, flat, preferred_element_type=jnp.bfloat16)  5.79 us
    sin x2, other arithmetic, angle_table(): return (jnp.cos(theta), jnp.sin(theta))  5.18 us
    unnamed x16, local copies, waits for them, and re-layouts  5.04 us
    dot_general x2, matrix products, local(): first = jnp.dot(pick0, flat, preferred_element_type=jnp.bfloat16)  4.21 us
    all_to_all x1, starting transfers between devices, local(): lax.all_to_all(send_rows.reshape(devices, capacity, corr.shape[1]), ('grp...  3.78 us
  transfers between devices with their start and end apart: 3, of which 2 were waited for; matrix products, arithmetic and copies ran while one was open for 12% of the time, Pallas kernels for 18%

profile of v6, /device:TPU:0, one launch (start us, length us, event | category | flops | bytes accessed | tf_op | source)
XLA Modules:
  0.0 145.7 jit_solution(14428782770008991335)
XLA Ops:
  6.5 2.1 %multiply_reduce_fusion = f32[8,11264]{1,0:T(8,128)S(1)} fusion(f32[8,2,18432]{2,1,0:T(2,128)} %param.6), kind=kLoop, calls=%fused_computation.12 | loop fusion | flops 270336 | bytes 1081344 | tf_op jit(solution)/shard_map/reduce_sum | solution.py:16
  8.9 0.3 reduce_sum.50
  9.2 0.3 mul.169
  9.7 1.1 multiply_convert_fusion
  11.1 0.6 multiply_reduce_fusion.1
  12.4 0.9 multiply_convert_fusion.1
  13.4 4.2 %fusion.4 = (f32[288,896]{1,0:T(8,128)S(1)}, f32[288,896]{1,0:T(8,128)S(1)}) fusion(s32[288]{0:T(512)S(1)} %iota_multiply_fusion), kind=kLoop, calls=%fused_computation.7 | loop fusion | flops 2322432 | bytes 2065536 | tf_op jit(solution)/shard_map/sin | solution.py:24
  18.4 0.9 fusion.12
  19.4 30.3 %all-gather.5.cloned.1.call-done = bf16[64,2,11264]{2,1,0:T(2,128)(2,1)} async-done(((bf16[8,2,11264]{2,1,0:T(2,128)(2,1)}), bf16[64,2,11264]{2,1,0:T(2,128)(2,1)}) %all-gather.5.cloned.1.call-update) | async-done | bytes 2883600 | tf_op jit(solution)/shard_map/all_gather | solution.py:127
  49.7 2.4 %copy.14 = bf16[8,8,2,11264]{3,1,2,0:T(8,128)(2,1)S(1)} copy(bf16[8,8,2,11264]{3,2,1,0:T(2,128)(2,1)} %bitcast.27) | data formatting | bytes 5767168
  52.1 3.3 %fusion.16.b0_ref.b1_ref = bf16[96,22528]{1,0:T(8,128)(2,1)} fusion(bf16[64,22528]{1,0:T(8,128)(2,1)S(1)} %bitcast.23, s32[96]{0:T(128)S(1)} %get-tuple-element.14), kind=kOutput, calls=%fused_computation.29 | convolution fusion | flops 276830208 | bytes 7209344 | tf_op jit(solution)/shard_map/dot_general | solution.py:132
  55.4 3.3 %fusion.18.a0_ref.a1_ref = bf16[96,22528]{1,0:T(8,128)(2,1)} fusion(bf16[64,22528]{1,0:T(8,128)(2,1)S(1)} %bitcast.24, s32[96]{0:T(128)S(1)} %get-tuple-element.15), kind=kOutput, calls=%fused_computation.32 | convolution fusion | flops 276830208 | bytes 7209344 | tf_op jit(solution)/shard_map/dot_general | solution.py:131
  58.8 25.9 %shard_map.64.acc_ref = f32[96,1792]{1,0:T(8,128)S(1)} custom-call(bf16[96,22528]{1,0:T(8,128)(2,1)} %fusion.18.a0_ref.a1_ref, bf16[96,22528]{1,0:T(8,128)(2,1)} %fusion.18.a0_ref.a1_ref, bf16[96,22528]{1,0:T(8,128)(2,1)} %fusion.16.b0_ref.b1_ref, bf16[96,22528]{1,0:T(8,128)(2,1)} %fusion.16.b0_ref.b1_ref, ...), custom_call_target="tpu_custom_call", output_to_operand_aliasing={{}: (8, {})} | custom-call | flops 3976462336 | bytes 8994816 | tf_op jit(solution)/shard_map/pallas_call | solution.py:67
  84.7 1.9 %copy.15 = bf16[8,8,2,7168]{3,1,2,0:T(8,128)(2,1)S(1)} copy(bf16[8,8,2,7168]{3,2,1,0:T(2,128)(2,1)} %bitcast.28) | data formatting | bytes 3670016
  86.6 2.5 %fusion.15.b0_ref.b1_ref = bf16[96,14336]{1,0:T(8,128)(2,1)} fusion(bf16[64,14336]{1,0:T(8,128)(2,1)S(1)} %bitcast.25, s32[96]{0:T(128)S(1)} %get-tuple-element.14), kind=kOutput, calls=%fused_computation.28 | convolution fusion | flops 176166912 | bytes 4587904 | tf_op jit(solution)/shard_map/dot_general | solution.py:132
  89.1 0.9 fusion.17.a0_ref.a1_ref
  90.0 16.8 %shard_map.65 = f32[96,1792]{1,0:T(8,128)S(1)} custom-call(bf16[96,14336]{1,0:T(8,128)(2,1)S(1)} %fusion.17.a0_ref.a1_ref, bf16[96,14336]{1,0:T(8,128)(2,1)S(1)} %fusion.17.a0_ref.a1_ref, bf16[96,14336]{1,0:T(8,128)(2,1)} %fusion.15.b0_ref.b1_ref, bf16[96,14336]{1,0:T(8,128)(2,1)} %fusion.15.b0_ref.b1_ref, ...), custom_call_target="tpu_custom_call", output_to_operand_aliasing={{}: (8, {})} | custom-call | flops 2530476032 | bytes 5849088 | tf_op jit(solution)/shard_map/pallas_call | solution.py:67
  107.1 0.6 reverse
  108.2 0.6 fusion.20
  108.8 1.2 reshape.51
  110.0 3.8 %all-to-all-start = ((f32[32,4,1664]{2,1,0:T(4,128)}), f32[32,4,1664]{2,1,0:T(4,128)S(1)}, u32[]{:S(2)}, u32[]{:S(2)}) async-start(f32[32,4,1664]{2,1,0:T(4,128)} %reshape.51), calls=%async_computation | async-start | bytes 1703936 | tf_op jit(solution)/shard_map/all_to_all | solution.py:154
  113.8 23.2 %all-to-all-done = f32[32,4,1664]{2,1,0:T(4,128)S(1)} async-done(((f32[32,4,1664]{2,1,0:T(4,128)}), f32[32,4,1664]{2,1,0:T(4,128)S(1)}, u32[]{:S(2)}, u32[]{:S(2)}) %all-to-all-start) | async-done | bytes 852000 | tf_op jit(solution)/shard_map/all_to_all | solution.py:154
  137.0 0.3 reshape.52
  137.5 1.4 convolution_add_fusion
  (47 shorter events, 3.1 us)
Async XLA Ops:
  6.5 3.2 %copy-start = (f32[8,2,18432]{2,1,0:T(2,128)S(1)}, f32[8,2,18432]{2,1,0:T(2,128)}, u32[]{:S(2)}) copy-start(f32[8,2,18432]{2,1,0:T(2,128)} %param.6) | copy-start | bytes 3538948
  6.5 43.2 %all-gather.5.cloned.1.call-start = ((), (), s32[]{:S(2)}) async-start(), calls=%async_computation.2 | async-start | bytes 3244032 | tf_op jit(solution)/shard_map/all_gather | solution.py:127
  10.9 73.9 %all-gather.3.cloned.1.call-start = ((), (), s32[]{:S(2)}) async-start(), calls=%async_computation.1 | async-start | bytes 2064384 | tf_op jit(solution)/shard_map/all_gather | solution.py:127
  13.4 4.5 %copy-start.4 = (s32[96]{0:T(128)S(1)}, s32[96]{0:T(128)}, u32[]{:S(2)}) copy-start(s32[96]{0:T(128)} %param.11) | copy-start | bytes 1156
  13.4 4.6 %copy-start.2 = (s32[96,1]{0,1:T(1,128)S(1)}, s32[96,1]{0,1:T(1,128)}, u32[]{:S(2)}) copy-start(s32[96,1]{0,1:T(1,128)} %param.10) | copy-start | bytes 1156
  17.6 1.7 %copy-start.5 = (s32[96]{0:T(128)S(1)}, s32[96]{0:T(128)}, u32[]{:S(2)}) copy-start(s32[96]{0:T(128)} %param.9) | copy-start | bytes 1156
  17.6 1.7 %copy-start.3 = (s32[2,96]{1,0:T(2,128)S(1)}, s32[2,96]{1,0:T(2,128)}, u32[]{:S(2)}) copy-start(s32[2,96]{1,0:T(2,128)} %param.8) | copy-start | bytes 2308
  108.8 28.7 %copy-start.1 = (f32[96,1601]{1,0:T(8,128)S(1)}, f32[96,1601]{1,0:T(8,128)}, u32[]{:S(2)}) copy-start(f32[96,1601]{1,0:T(8,128)} %param.7) | copy-start | bytes 1844356
  110.0 27.0 %all-to-all-start = ((f32[32,4,1664]{2,1,0:T(4,128)}), f32[32,4,1664]{2,1,0:T(4,128)S(1)}, u32[]{:S(2)}, u32[]{:S(2)}) async-start(f32[32,4,1664]{2,1,0:T(4,128)} %reshape.51), calls=%async_computation | async-start | bytes 1703936 | tf_op jit(solution)/shard_map/all_to_all | solution.py:154
Sparse Core Ops, SparseCore 0:
  11.0 38.6 all-gather.4
  51.3 26.0 all-gather.2

commit v7 on v6

--- a/solution.py
+++ b/solution.py
@@ -106,8 +106,11 @@
     members = lax.axis_size("sta")
     devices = groups * members
     capacity = max(2, (4 * pair_count + 3 * devices - 1) // (3 * devices))
-    group_sta = spectra.shape[0] * members
-    sta_ids = lax.iota(jnp.int32, group_sta)[None, :]
+    per = spectra.shape[0]
+    group_sta = per * members
+    me = lax.axis_index("sta")
+    source = jnp.mod(me - lax.iota(jnp.int32, members), members)
+    sta_ids = (source[:, None] * per + lax.iota(jnp.int32, per)[None, :]).reshape(1, group_sta)
     pick0 = (pair_sta[0][:, None] == sta_ids).astype(jnp.bfloat16)
     pick1 = (pair_sta[1][:, None] == sta_ids).astype(jnp.bfloat16)
     assert lag_count % 2 == 1
@@ -124,7 +127,11 @@
         begin, end = bounds[c], bounds[c + 1]
         width = end - begin
         piece = whiten(spectra[:, :, begin:end])
-        gathered = lax.all_gather(piece, "sta", axis=0, tiled=True)
+        parts = [piece]
+        for k in range(1, members):
+            shift = [(j, (j + k) % members) for j in range(members)]
+            parts.append(lax.ppermute(piece, "sta", shift))
+        gathered = jnp.concatenate(parts, axis=0)
         if c:
             gathered, corr = lax.optimization_barrier((gathered, corr))
         flat = gathered.reshape(group_sta, 2 * width)

time: 146 us -> 214 us (1.47)
  starting transfers between devices: 4.01 us -> 44.1 us
  waiting for transfers between devices: 53.6 us -> 77 us
  local copies, waits for them, and re-layouts: 8.19 us -> 22 us
  between operations: 13.7 us -> 0.34 us
  other arithmetic: 11.4 us -> 15.2 us
    ppermute x0 -> x14, waiting for transfers between devices: none -> 53.8 us  [local(): parts.append(lax.ppermute(piece, 'sta', shift))]
    ppermute x0 -> x14, starting transfers between devices: none -> 33.9 us  [local(): parts.append(lax.ppermute(piece, 'sta', shift))]
    all_gather x2 -> x0, waiting for transfers between devices: 30.4 us -> none  [local(): gathered = lax.all_gather(piece, 'sta', axis=0, tiled=True)]
    unnamed x16 -> x34, local copies, waits for them, and re-layouts: 5.04 us -> 13.4 us
    all_to_all x1, starting transfers between devices: 3.78 us -> 10.2 us  [local(): lax.all_to_all(send_rows.reshape(devices, capacity, corr.shape[1]), ('grp...]
    unnamed x0 -> x2, other arithmetic: none -> 2.47 us
  transfers between devices with their start and end apart: 3 -> 15, of which waited for: 2 -> 11; matrix products, arithmetic and copies ran while one was open for 12% -> 13% of each run, Pallas kernels for 18% -> 0%
where the time goes in v7:
time: 214 us; the launch traced here: 213 us
  waiting for transfers between devices  77 us (36%)
  starting transfers between devices  44.1 us (21%)
  Pallas kernels  42.6 us (20%)
  local copies, waits for them, and re-layouts  22 us (10%)
  other arithmetic  15.2 us (7%)
  matrix products  12 us (6%)
    ppermute x14, waiting for transfers between devices, local(): parts.append(lax.ppermute(piece, 'sta', shift))  53.8 us
    pallas_call x2, Pallas kernels, correlate(): pl.pallas_call(table_kernel, grid=(blocks,), in_specs=[pl.BlockSpec((pair...  42.6 us
    ppermute x14, starting transfers between devices, local(): parts.append(lax.ppermute(piece, 'sta', shift))  33.9 us
    all_to_all x1, waiting for transfers between devices, local(): lax.all_to_all(send_rows.reshape(devices, capacity, corr.shape[1]), ('grp...  23.2 us
    unnamed x34, local copies, waits for them, and re-layouts  13.4 us
    all_to_all x1, starting transfers between devices, local(): lax.all_to_all(send_rows.reshape(devices, capacity, corr.shape[1]), ('grp...  10.2 us
    sin x2, other arithmetic, angle_table(): return (jnp.cos(theta), jnp.sin(theta))  6.32 us
    dot_general x2, matrix products, local(): second = jnp.dot(pick1, flat, preferred_element_type=jnp.bfloat16)  5.84 us
  transfers between devices with their start and end apart: 15, of which 11 were waited for; matrix products, arithmetic and copies ran while one was open for 13% of the time, Pallas kernels for 0%

profile of v7, /device:TPU:0, one launch (start us, length us, event | category | flops | bytes accessed | tf_op | source)
XLA Modules:
  0.0 213.4 jit_solution(11162208897375748580)
XLA Ops:
  0.0 2.1 %multiply_reduce_fusion = f32[8,11264]{1,0:T(8,128)S(1)} fusion(f32[8,2,18432]{2,1,0:T(2,128)} %param.6), kind=kLoop, calls=%fused_computation.12 | loop fusion | flops 270336 | bytes 1081344 | tf_op jit(solution)/shard_map/reduce_sum | solution.py:16
  5.0 2.6 %collective-permute-start.8 = (bf16[8,2,11264]{2,1,0:T(2,128)(2,1)}, bf16[8,2,11264]{2,1,0:T(2,128)(2,1)}, u32[]{:S(2)}, u32[]{:S(2)}) collective-permute-start(bf16[8,2,11264]{2,1,0:T(2,128)(2,1)} %get-tuple-element.10), channel_id=1, source_target_pairs={{0,2},{1,3},{2,4},{3,5},{4,6},{5,7},{6,0},{7,1},{8,10},{9,11},{10,... | collective-permute-start | bytes 1081352 | tf_op jit(solution)/shard_map/ppermute | solution.py:133
  7.6 2.6 %collective-permute-start.9 = (bf16[8,2,11264]{2,1,0:T(2,128)(2,1)}, bf16[8,2,11264]{2,1,0:T(2,128)(2,1)}, u32[]{:S(2)}, u32[]{:S(2)}) collective-permute-start(bf16[8,2,11264]{2,1,0:T(2,128)(2,1)} %get-tuple-element.10), channel_id=1, source_target_pairs={{0,3},{1,4},{2,5},{3,6},{4,7},{5,0},{6,1},{7,2},{8,11},{9,12},{10,... | collective-permute-start | bytes 1081352 | tf_op jit(solution)/shard_map/ppermute | solution.py:133
  14.5 5.4 %fusion.4 = (f32[288,896]{1,0:T(8,128)S(1)}, f32[288,896]{1,0:T(8,128)}) fusion(s32[288]{0:T(512)S(1)} %iota_multiply_fusion), kind=kLoop, calls=%fused_computation.7 | loop fusion | flops 2322432 | bytes 2065536 | tf_op jit(solution)/shard_map/sin | solution.py:24
  27.4 12.8 %collective-permute-done = bf16[8,2,7168]{2,1,0:T(2,128)(2,1)} collective-permute-done((bf16[8,2,7168]{2,1,0:T(2,128)(2,1)}, bf16[8,2,7168]{2,1,0:T(2,128)(2,1)}, u32[]{:S(2)}, u32[]{:S(2)}) %collective-permute-start) | collective-permute-done | bytes 229408 | tf_op jit(solution)/shard_map/ppermute | solution.py:133
  42.2 6.1 %collective-permute-done.1 = bf16[8,2,7168]{2,1,0:T(2,128)(2,1)S(1)} collective-permute-done((bf16[8,2,7168]{2,1,0:T(2,128)(2,1)}, bf16[8,2,7168]{2,1,0:T(2,128)(2,1)S(1)}, u32[]{:S(2)}, u32[]{:S(2)}) %collective-permute-start.1) | collective-permute-done | bytes 229408 | tf_op jit(solution)/shard_map/ppermute | solution.py:133
  48.3 7.6 %collective-permute-start.2 = (bf16[8,2,7168]{2,1,0:T(2,128)(2,1)}, bf16[8,2,7168]{2,1,0:T(2,128)(2,1)S(1)}, u32[]{:S(2)}, u32[]{:S(2)}) collective-permute-start(bf16[8,2,7168]{2,1,0:T(2,128)(2,1)} %get-tuple-element.12), channel_id=1, source_target_pairs={{0,3},{1,4},{2,5},{3,6},{4,7},{5,0},{6,1},{7,2},{8,11},{9,12},{10,... | collective-permute-start | bytes 688136 | tf_op jit(solution)/shard_map/ppermute | solution.py:133
  56.8 3.0 %collective-permute-done.2 = bf16[8,2,7168]{2,1,0:T(2,128)(2,1)S(1)} collective-permute-done((bf16[8,2,7168]{2,1,0:T(2,128)(2,1)}, bf16[8,2,7168]{2,1,0:T(2,128)(2,1)S(1)}, u32[]{:S(2)}, u32[]{:S(2)}) %collective-permute-start.2) | collective-permute-done | bytes 229408 | tf_op jit(solution)/shard_map/ppermute | solution.py:133
  59.8 6.1 %collective-permute-start.3 = (bf16[8,2,7168]{2,1,0:T(2,128)(2,1)}, bf16[8,2,7168]{2,1,0:T(2,128)(2,1)S(1)}, u32[]{:S(2)}, u32[]{:S(2)}) collective-permute-start(bf16[8,2,7168]{2,1,0:T(2,128)(2,1)} %get-tuple-element.12), channel_id=1, source_target_pairs={{0,4},{1,5},{2,6},{3,7},{4,0},{5,1},{6,2},{7,3},{8,12},{9,13},{10,... | collective-permute-start | bytes 688136 | tf_op jit(solution)/shard_map/ppermute | solution.py:133
  66.7 10.1 %collective-permute-done.3 = bf16[8,2,7168]{2,1,0:T(2,128)(2,1)S(1)} collective-permute-done((bf16[8,2,7168]{2,1,0:T(2,128)(2,1)}, bf16[8,2,7168]{2,1,0:T(2,128)(2,1)S(1)}, u32[]{:S(2)}, u32[]{:S(2)}) %collective-permute-start.3) | collective-permute-done | bytes 229408 | tf_op jit(solution)/shard_map/ppermute | solution.py:133
  77.7 4.9 %collective-permute-done.4 = bf16[8,2,7168]{2,1,0:T(2,128)(2,1)S(1)} collective-permute-done((bf16[8,2,7168]{2,1,0:T(2,128)(2,1)}, bf16[8,2,7168]{2,1,0:T(2,128)(2,1)S(1)}, u32[]{:S(2)}, u32[]{:S(2)}) %collective-permute-start.4) | collective-permute-done | bytes 229408 | tf_op jit(solution)/shard_map/ppermute | solution.py:133
  82.6 4.8 %collective-permute-start.5 = (bf16[8,2,7168]{2,1,0:T(2,128)(2,1)}, bf16[8,2,7168]{2,1,0:T(2,128)(2,1)S(1)}, u32[]{:S(2)}, u32[]{:S(2)}) collective-permute-start(bf16[8,2,7168]{2,1,0:T(2,128)(2,1)} %get-tuple-element.12), channel_id=1, source_target_pairs={{0,6},{1,7},{2,0},{3,1},{4,2},{5,3},{6,4},{7,5},{8,14},{9,15},{10,... | collective-permute-start | bytes 688136 | tf_op jit(solution)/shard_map/ppermute | solution.py:133
  88.3 4.7 %collective-permute-done.5 = bf16[8,2,7168]{2,1,0:T(2,128)(2,1)S(1)} collective-permute-done((bf16[8,2,7168]{2,1,0:T(2,128)(2,1)}, bf16[8,2,7168]{2,1,0:T(2,128)(2,1)S(1)}, u32[]{:S(2)}, u32[]{:S(2)}) %collective-permute-start.5) | collective-permute-done | bytes 229408 | tf_op jit(solution)/shard_map/ppermute | solution.py:133
  93.0 4.3 %collective-permute-start.6 = (bf16[8,2,7168]{2,1,0:T(2,128)(2,1)}, bf16[8,2,7168]{2,1,0:T(2,128)(2,1)S(1)}, u32[]{:S(2)}, u32[]{:S(2)}) collective-permute-start(bf16[8,2,7168]{2,1,0:T(2,128)(2,1)} %get-tuple-element.12), channel_id=1, source_target_pairs={{0,7},{1,0},{2,1},{3,2},{4,3},{5,4},{6,5},{7,6},{8,15},{9,8},{10,9... | collective-permute-start | bytes 688136 | tf_op jit(solution)/shard_map/ppermute | solution.py:133
  98.2 3.0 %collective-permute-done.6 = bf16[8,2,7168]{2,1,0:T(2,128)(2,1)S(1)} collective-permute-done((bf16[8,2,7168]{2,1,0:T(2,128)(2,1)}, bf16[8,2,7168]{2,1,0:T(2,128)(2,1)S(1)}, u32[]{:S(2)}, u32[]{:S(2)}) %collective-permute-start.6) | collective-permute-done | bytes 229408 | tf_op jit(solution)/shard_map/ppermute | solution.py:133
  103.4 3.8 %collective-permute-start.13 = (bf16[8,2,11264]{2,1,0:T(2,128)(2,1)}, bf16[8,2,11264]{2,1,0:T(2,128)(2,1)S(1)}, u32[]{:S(2)}, u32[]{:S(2)}) collective-permute-start(bf16[8,2,11264]{2,1,0:T(2,128)(2,1)} %get-tuple-element.10), channel_id=1, source_target_pairs={{0,7},{1,0},{2,1},{3,2},{4,3},{5,4},{6,5},{7,6},{8,15},{9,8},{10,9... | collective-permute-start | bytes 1081352 | tf_op jit(solution)/shard_map/ppermute | solution.py:133
  111.7 7.3 %collective-permute-done.12 = bf16[8,2,11264]{2,1,0:T(2,128)(2,1)S(1)} collective-permute-done((bf16[8,2,11264]{2,1,0:T(2,128)(2,1)}, bf16[8,2,11264]{2,1,0:T(2,128)(2,1)S(1)}, u32[]{:S(2)}, u32[]{:S(2)}) %collective-permute-start.12) | collective-permute-done | bytes 360480 | tf_op jit(solution)/shard_map/ppermute | solution.py:133
  121.6 3.4 %fusion.17.b0_ref.b1_ref = bf16[96,22528]{1,0:T(8,128)(2,1)} fusion(bf16[64,22528]{1,0:T(8,128)(2,1)S(1)} %bitcast.23, s32[64]{0:T(128)S(1)} %add.91, s32[96]{0:T(128)S(1)} %get-tuple-element.18), kind=kOutput, calls=%fused_computation.29 | convolution fusion | flops 276830208 | bytes 7209600 | tf_op jit(solution)/shard_map/dot_general | solution.py:139
  125.0 3.3 %fusion.21.a0_ref.a1_ref = bf16[96,22528]{1,0:T(8,128)(2,1)} fusion(bf16[64,22528]{1,0:T(8,128)(2,1)S(1)} %bitcast.24, s32[64]{0:T(128)S(1)} %add.91, s32[96]{0:T(128)S(1)} %get-tuple-element.19), kind=kOutput, calls=%fused_computation.33 | convolution fusion | flops 276830208 | bytes 7209600 | tf_op jit(solution)/shard_map/dot_general | solution.py:138
  128.4 25.8 %shard_map.64.acc_ref = f32[96,1792]{1,0:T(8,128)S(1)} custom-call(bf16[96,22528]{1,0:T(8,128)(2,1)} %fusion.21.a0_ref.a1_ref, bf16[96,22528]{1,0:T(8,128)(2,1)} %fusion.21.a0_ref.a1_ref, bf16[96,22528]{1,0:T(8,128)(2,1)} %fusion.17.b0_ref.b1_ref, bf16[96,22528]{1,0:T(8,128)(2,1)} %fusion.17.b0_ref.b1_ref, ...), custom_call_target="tpu_custom_call", output_to_operand_aliasing={{}: (8, {})} | custom-call | flops 3976462336 | bytes 8994816 | tf_op jit(solution)/shard_map/pallas_call | solution.py:67
  154.6 2.5 %fusion.15.b0_ref.b1_ref = bf16[96,14336]{1,0:T(8,128)(2,1)} fusion(bf16[64,14336]{1,0:T(8,128)(2,1)S(1)} %bitcast.25, s32[64]{0:T(128)S(1)} %add.91, s32[96]{0:T(128)S(1)} %get-tuple-element.18), kind=kOutput, calls=%fused_computation.27 | convolution fusion | flops 176166912 | bytes 4588160 | tf_op jit(solution)/shard_map/dot_general | solution.py:139
  158.0 16.8 %shard_map.65 = f32[96,1792]{1,0:T(8,128)S(1)} custom-call(bf16[96,14336]{1,0:T(8,128)(2,1)S(1)} %fusion.19.a0_ref.a1_ref, bf16[96,14336]{1,0:T(8,128)(2,1)S(1)} %fusion.19.a0_ref.a1_ref, bf16[96,14336]{1,0:T(8,128)(2,1)} %fusion.15.b0_ref.b1_ref, bf16[96,14336]{1,0:T(8,128)(2,1)} %fusion.15.b0_ref.b1_ref, ...), custom_call_target="tpu_custom_call", output_to_operand_aliasing={{}: (8, {})} | custom-call | flops 2530476032 | bytes 5849088 | tf_op jit(solution)/shard_map/pallas_call | solution.py:67
  178.0 10.2 %all-to-all-start = ((f32[32,4,1664]{2,1,0:T(4,128)}), f32[32,4,1664]{2,1,0:T(4,128)S(1)}, u32[]{:S(2)}, u32[]{:S(2)}) async-start(f32[32,4,1664]{2,1,0:T(4,128)} %reshape.83), calls=%async_computation | async-start | bytes 1703936 | tf_op jit(solution)/shard_map/all_to_all | solution.py:161
  188.3 23.2 %all-to-all-done = f32[32,4,1664]{2,1,0:T(4,128)S(1)} async-done(((f32[32,4,1664]{2,1,0:T(4,128)}), f32[32,4,1664]{2,1,0:T(4,128)S(1)}, u32[]{:S(2)}, u32[]{:S(2)}) %all-to-all-start) | async-done | bytes 852000 | tf_op jit(solution)/shard_map/all_to_all | solution.py:161
  (92 shorter events, 36.5 us)
Async XLA Ops:
  0.0 3.2 %copy-start = (f32[8,2,18432]{2,1,0:T(2,128)S(1)}, f32[8,2,18432]{2,1,0:T(2,128)}, u32[]{:S(2)}) copy-start(f32[8,2,18432]{2,1,0:T(2,128)} %param.6) | copy-start | bytes 3538948
  4.5 97.6 %collective-permute-start.7 = (bf16[8,2,11264]{2,1,0:T(2,128)(2,1)}, bf16[8,2,11264]{2,1,0:T(2,128)(2,1)}, u32[]{:S(2)}, u32[]{:S(2)}) collective-permute-start(bf16[8,2,11264]{2,1,0:T(2,128)(2,1)} %get-tuple-element.10), channel_id=1, source_target_pairs={{0,1},{1,2},{2,3},{3,4},{4,5},{5,6},{6,7},{7,0},{8,9},{9,10},{10,1... | collective-permute-start | bytes 1081352 | tf_op jit(solution)/shard_map/ppermute | solution.py:133
  5.0 98.3 %collective-permute-start.8 = (bf16[8,2,11264]{2,1,0:T(2,128)(2,1)}, bf16[8,2,11264]{2,1,0:T(2,128)(2,1)}, u32[]{:S(2)}, u32[]{:S(2)}) collective-permute-start(bf16[8,2,11264]{2,1,0:T(2,128)(2,1)} %get-tuple-element.10), channel_id=1, source_target_pairs={{0,2},{1,3},{2,4},{3,5},{4,6},{5,7},{6,0},{7,1},{8,10},{9,11},{10,... | collective-permute-start | bytes 1081352 | tf_op jit(solution)/shard_map/ppermute | solution.py:133
  7.6 100.9 %collective-permute-start.9 = (bf16[8,2,11264]{2,1,0:T(2,128)(2,1)}, bf16[8,2,11264]{2,1,0:T(2,128)(2,1)}, u32[]{:S(2)}, u32[]{:S(2)}) collective-permute-start(bf16[8,2,11264]{2,1,0:T(2,128)(2,1)} %get-tuple-element.10), channel_id=1, source_target_pairs={{0,3},{1,4},{2,5},{3,6},{4,7},{5,0},{6,1},{7,2},{8,11},{9,12},{10,... | collective-permute-start | bytes 1081352 | tf_op jit(solution)/shard_map/ppermute | solution.py:133
  10.2 99.6 %collective-permute-start.10 = (bf16[8,2,11264]{2,1,0:T(2,128)(2,1)}, bf16[8,2,11264]{2,1,0:T(2,128)(2,1)}, u32[]{:S(2)}, u32[]{:S(2)}) collective-permute-start(bf16[8,2,11264]{2,1,0:T(2,128)(2,1)} %get-tuple-element.10), channel_id=1, source_target_pairs={{0,4},{1,5},{2,6},{3,7},{4,0},{5,1},{6,2},{7,3},{8,12},{9,13},{10,... | collective-permute-start | bytes 1081352 | tf_op jit(solution)/shard_map/ppermute | solution.py:133
  12.0 7.9 %copy-start.7 = (s32[96]{0:T(128)S(1)}, s32[96]{0:T(128)}, u32[]{:S(2)}) copy-start(s32[96]{0:T(128)} %param.9) | copy-start | bytes 1156
  12.0 8.5 %copy-start.8 = (s32[96]{0:T(128)S(1)}, s32[96]{0:T(128)}, u32[]{:S(2)}) copy-start(s32[96]{0:T(128)} %param.11) | copy-start | bytes 1156
  12.0 9.0 %copy-start.4 = (s32[96,1]{0,1:T(1,128)S(1)}, s32[96,1]{0,1:T(1,128)}, u32[]{:S(2)}) copy-start(s32[96,1]{0,1:T(1,128)} %param.10) | copy-start | bytes 1156
  13.9 26.3 %collective-permute-start = (bf16[8,2,7168]{2,1,0:T(2,128)(2,1)}, bf16[8,2,7168]{2,1,0:T(2,128)(2,1)}, u32[]{:S(2)}, u32[]{:S(2)}) collective-permute-start(bf16[8,2,7168]{2,1,0:T(2,128)(2,1)} %get-tuple-element.12), channel_id=1, source_target_pairs={{0,1},{1,2},{2,3},{3,4},{4,5},{5,6},{6,7},{7,0},{8,9},{9,10},{10,1... | collective-permute-start | bytes 688136 | tf_op jit(solution)/shard_map/ppermute | solution.py:133
  26.6 75.5 %copy-start.1 = (bf16[64,2,11264]{2,1,0:T(2,128)(2,1)S(1)}, bf16[64,2,11264]{2,1,0:T(2,128)(2,1)}, u32[]{:S(2)}) copy-start(bf16[64,2,11264]{2,1,0:T(2,128)(2,1)} %get-tuple-element.9) | copy-start | bytes 8650756
  40.2 8.1 %collective-permute-start.1 = (bf16[8,2,7168]{2,1,0:T(2,128)(2,1)}, bf16[8,2,7168]{2,1,0:T(2,128)(2,1)S(1)}, u32[]{:S(2)}, u32[]{:S(2)}) collective-permute-start(bf16[8,2,7168]{2,1,0:T(2,128)(2,1)} %get-tuple-element.12), channel_id=1, source_target_pairs={{0,2},{1,3},{2,4},{3,5},{4,6},{5,7},{6,0},{7,1},{8,10},{9,11},{10,... | collective-permute-start | bytes 688136 | tf_op jit(solution)/shard_map/ppermute | solution.py:133
  48.3 11.4 %collective-permute-start.2 = (bf16[8,2,7168]{2,1,0:T(2,128)(2,1)}, bf16[8,2,7168]{2,1,0:T(2,128)(2,1)S(1)}, u32[]{:S(2)}, u32[]{:S(2)}) collective-permute-start(bf16[8,2,7168]{2,1,0:T(2,128)(2,1)} %get-tuple-element.12), channel_id=1, source_target_pairs={{0,3},{1,4},{2,5},{3,6},{4,7},{5,0},{6,1},{7,2},{8,11},{9,12},{10,... | collective-permute-start | bytes 688136 | tf_op jit(solution)/shard_map/ppermute | solution.py:133
  59.8 17.0 %collective-permute-start.3 = (bf16[8,2,7168]{2,1,0:T(2,128)(2,1)}, bf16[8,2,7168]{2,1,0:T(2,128)(2,1)S(1)}, u32[]{:S(2)}, u32[]{:S(2)}) collective-permute-start(bf16[8,2,7168]{2,1,0:T(2,128)(2,1)} %get-tuple-element.12), channel_id=1, source_target_pairs={{0,4},{1,5},{2,6},{3,7},{4,0},{5,1},{6,2},{7,3},{8,12},{9,13},{10,... | collective-permute-start | bytes 688136 | tf_op jit(solution)/shard_map/ppermute | solution.py:133
  76.8 5.8 %collective-permute-start.4 = (bf16[8,2,7168]{2,1,0:T(2,128)(2,1)}, bf16[8,2,7168]{2,1,0:T(2,128)(2,1)S(1)}, u32[]{:S(2)}, u32[]{:S(2)}) collective-permute-start(bf16[8,2,7168]{2,1,0:T(2,128)(2,1)} %get-tuple-element.12), channel_id=1, source_target_pairs={{0,5},{1,6},{2,7},{3,0},{4,1},{5,2},{6,3},{7,4},{8,13},{9,14},{10,... | collective-permute-start | bytes 688136 | tf_op jit(solution)/shard_map/ppermute | solution.py:133
  82.6 10.4 %collective-permute-start.5 = (bf16[8,2,7168]{2,1,0:T(2,128)(2,1)}, bf16[8,2,7168]{2,1,0:T(2,128)(2,1)S(1)}, u32[]{:S(2)}, u32[]{:S(2)}) collective-permute-start(bf16[8,2,7168]{2,1,0:T(2,128)(2,1)} %get-tuple-element.12), channel_id=1, source_target_pairs={{0,6},{1,7},{2,0},{3,1},{4,2},{5,3},{6,4},{7,5},{8,14},{9,15},{10,... | collective-permute-start | bytes 688136 | tf_op jit(solution)/shard_map/ppermute | solution.py:133
  93.0 8.2 %collective-permute-start.6 = (bf16[8,2,7168]{2,1,0:T(2,128)(2,1)}, bf16[8,2,7168]{2,1,0:T(2,128)(2,1)S(1)}, u32[]{:S(2)}, u32[]{:S(2)}) collective-permute-start(bf16[8,2,7168]{2,1,0:T(2,128)(2,1)} %get-tuple-element.12), channel_id=1, source_target_pairs={{0,7},{1,0},{2,1},{3,2},{4,3},{5,4},{6,5},{7,6},{8,15},{9,8},{10,9... | collective-permute-start | bytes 688136 | tf_op jit(solution)/shard_map/ppermute | solution.py:133
  101.2 10.2 %collective-permute-start.11 = (bf16[8,2,11264]{2,1,0:T(2,128)(2,1)}, bf16[8,2,11264]{2,1,0:T(2,128)(2,1)S(1)}, u32[]{:S(2)}, u32[]{:S(2)}) collective-permute-start(bf16[8,2,11264]{2,1,0:T(2,128)(2,1)} %get-tuple-element.10), channel_id=1, source_target_pairs={{0,5},{1,6},{2,7},{3,0},{4,1},{5,2},{6,3},{7,4},{8,13},{9,14},{10,... | collective-permute-start | bytes 1081352 | tf_op jit(solution)/shard_map/ppermute | solution.py:133
  102.1 16.9 %collective-permute-start.12 = (bf16[8,2,11264]{2,1,0:T(2,128)(2,1)}, bf16[8,2,11264]{2,1,0:T(2,128)(2,1)S(1)}, u32[]{:S(2)}, u32[]{:S(2)}) collective-permute-start(bf16[8,2,11264]{2,1,0:T(2,128)(2,1)} %get-tuple-element.10), channel_id=1, source_target_pairs={{0,6},{1,7},{2,0},{3,1},{4,2},{5,3},{6,4},{7,5},{8,14},{9,15},{10,... | collective-permute-start | bytes 1081352 | tf_op jit(solution)/shard_map/ppermute | solution.py:133
  103.4 17.4 %collective-permute-start.13 = (bf16[8,2,11264]{2,1,0:T(2,128)(2,1)}, bf16[8,2,11264]{2,1,0:T(2,128)(2,1)S(1)}, u32[]{:S(2)}, u32[]{:S(2)}) collective-permute-start(bf16[8,2,11264]{2,1,0:T(2,128)(2,1)} %get-tuple-element.10), channel_id=1, source_target_pairs={{0,7},{1,0},{2,1},{3,2},{4,3},{5,4},{6,5},{7,6},{8,15},{9,8},{10,9... | collective-permute-start | bytes 1081352 | tf_op jit(solution)/shard_map/ppermute | solution.py:133
  128.4 25.8 %copy-start.2 = (bf16[64,2,7168]{2,1,0:T(2,128)(2,1)S(1)}, bf16[64,2,7168]{2,1,0:T(2,128)(2,1)}, u32[]{:S(2)}) copy-start(bf16[64,2,7168]{2,1,0:T(2,128)(2,1)} %constant_dynamic-update-slice_fusion) | copy-start | bytes 5505028
  174.8 1.1 copy-start.5
  174.9 1.3 copy-start.6
  176.8 35.2 %copy-start.3 = (f32[96,1601]{1,0:T(8,128)S(1)}, f32[96,1601]{1,0:T(8,128)}, u32[]{:S(2)}) copy-start(f32[96,1601]{1,0:T(8,128)} %param.7) | copy-start | bytes 1844356
  178.0 33.5 %all-to-all-start = ((f32[32,4,1664]{2,1,0:T(4,128)}), f32[32,4,1664]{2,1,0:T(4,128)S(1)}, u32[]{:S(2)}, u32[]{:S(2)}) async-start(f32[32,4,1664]{2,1,0:T(4,128)} %reshape.83), calls=%async_computation | async-start | bytes 1703936 | tf_op jit(solution)/shard_map/all_to_all | solution.py:161

commit v8 on v6

--- a/solution.py
+++ b/solution.py
@@ -56,11 +56,11 @@
     out_ref[:, half:] += jnp.dot(imag, stab[...], preferred_element_type=jnp.float32)
 
 
-def correlate(first, second, tables, acc):
+def correlate(both, tables, acc):
     cos_hi, sin_hi, cos_lo, sin_lo = tables
-    pair_count = first.shape[0]
+    pair_count = both.shape[0] // 2
     lag_pad = cos_lo.shape[1]
-    width = first.shape[1] // 2
+    width = both.shape[1] // 2
     hi_rows = FBLOCK // LOW
     assert width % FBLOCK == 0
     blocks = width // FBLOCK
@@ -70,8 +70,8 @@
         in_specs=[
             pl.BlockSpec((pair_count, FBLOCK), lambda i: (0, i)),
             pl.BlockSpec((pair_count, FBLOCK), lambda i: (0, i + blocks)),
-            pl.BlockSpec((pair_count, FBLOCK), lambda i: (0, i)),
-            pl.BlockSpec((pair_count, FBLOCK), lambda i: (0, i + blocks)),
+            pl.BlockSpec((pair_count, FBLOCK), lambda i: (1, i)),
+            pl.BlockSpec((pair_count, FBLOCK), lambda i: (1, i + blocks)),
             pl.BlockSpec((hi_rows, lag_pad), lambda i: (i, 0)),
             pl.BlockSpec((hi_rows, lag_pad), lambda i: (i, 0)),
             pl.BlockSpec((LOW, lag_pad), lambda i: (0, 0)),
@@ -93,7 +93,7 @@
             bytes_accessed=4 * pair_count * width * 2 + 4 * pair_count * lag_pad,
         ),
         input_output_aliases={8: 0},
-    )(first, first, second, second, cos_hi, sin_hi, cos_lo, sin_lo, acc)
+    )(both, both, both, both, cos_hi, sin_hi, cos_lo, sin_lo, acc)
     return out
 
 
@@ -110,6 +110,7 @@
     sta_ids = lax.iota(jnp.int32, group_sta)[None, :]
     pick0 = (pair_sta[0][:, None] == sta_ids).astype(jnp.bfloat16)
     pick1 = (pair_sta[1][:, None] == sta_ids).astype(jnp.bfloat16)
+    picks = jnp.concatenate([pick0, pick1], axis=0)
     assert lag_count % 2 == 1
     side = (lag_count - 1) // 2
     lag_pad = -(-(side + 1) // 128) * 128
@@ -123,16 +124,14 @@
     for c in range(len(bounds) - 1):
         begin, end = bounds[c], bounds[c + 1]
         width = end - begin
-        piece = whiten(spectra[:, :, begin:end])
-        gathered = lax.all_gather(piece, "sta", axis=0, tiled=True)
+        piece = whiten(spectra[:, :, begin:end]).reshape(spectra.shape[0], 2 * width)
+        flat = lax.all_gather(piece, "sta", axis=0, tiled=True)
         if c:
-            gathered, corr = lax.optimization_barrier((gathered, corr))
-        flat = gathered.reshape(group_sta, 2 * width)
-        first = jnp.dot(pick0, flat, preferred_element_type=jnp.bfloat16)
-        second = jnp.dot(pick1, flat, preferred_element_type=jnp.bfloat16)
+            flat, corr = lax.optimization_barrier((flat, corr))
+        both = jnp.dot(picks, flat, preferred_element_type=jnp.bfloat16)
         rows = slice(begin // LOW, end // LOW)
         tables = (hi_all[0][rows], hi_all[1][rows], lo_all[0], lo_all[1])
-        corr = correlate(first, second, tables, corr)
+        corr = correlate(both, tables, corr)
     even = corr[:, : side + 1]
     odd = corr[:, lag_pad : lag_pad + side + 1]
     corr = jnp.concatenate([(even + odd)[:, :0:-1], even - odd], axis=1)

time: 146 us -> 145 us (level)
  matrix products: 12 us -> 14.9 us
  local copies, waits for them, and re-layouts: 8.19 us -> 6.13 us
    dot_general x4 -> x2, matrix products: 10 us -> 12.9 us  [local(): both = jnp.dot(picks, flat, preferred_element_type=jnp.bfloat16)]
    unnamed x16, local copies, waits for them, and re-layouts: 5.04 us -> 2.98 us
    convert_element_type x2 -> x0, other arithmetic: 2.06 us -> none  [whiten(): (split * lax.rsqrt(power + 1e-06)).reshape(shape).astype(jnp.bfloat16)]
  transfers between devices with their start and end apart: 3 -> 3, of which waited for: 2 -> 2; matrix products, arithmetic and copies ran while one was open for 12% -> 11% of each run, Pallas kernels for 18% -> 18%
where the time goes in v8:
time: 145 us
  waiting for transfers between devices  53.1 us (37%)
  Pallas kernels  43 us (30%)
  matrix products  14.9 us (10%)
  between operations  13.7 us (9%)
  other arithmetic  9.98 us (7%)
  local copies, waits for them, and re-layouts  6.13 us (4%)
  starting transfers between devices  3.85 us (3%)
    pallas_call x2, Pallas kernels, correlate(): pl.pallas_call(table_kernel, grid=(blocks,), in_specs=[pl.BlockSpec((pair...  43 us
    all_gather x2, waiting for transfers between devices, local(): flat = lax.all_gather(piece, 'sta', axis=0, tiled=True)  29.8 us
    all_to_all x1, waiting for transfers between devices, local(): lax.all_to_all(send_rows.reshape(devices, capacity, corr.shape[1]), ('grp...  23.2 us
    dot_general x2, matrix products, local(): both = jnp.dot(picks, flat, preferred_element_type=jnp.bfloat16)  12.9 us
    sin x2, other arithmetic, angle_table(): return (jnp.cos(theta), jnp.sin(theta))  5.18 us
    all_to_all x1, starting transfers between devices, local(): lax.all_to_all(send_rows.reshape(devices, capacity, corr.shape[1]), ('grp...  3.63 us
    reduce_sum x4, other arithmetic, whiten(): power = jnp.mean(split * split, axis=(1, 3), keepdims=True)  3.18 us
    unnamed x16, local copies, waits for them, and re-layouts  2.98 us
  transfers between devices with their start and end apart: 3, of which 2 were waited for; matrix products, arithmetic and copies ran while one was open for 11% of the time, Pallas kernels for 18%

profile of v8, /device:TPU:0, one launch (start us, length us, event | category | flops | bytes accessed | tf_op | source)
XLA Modules:
  0.0 144.6 jit_solution(17035742622119537695)
XLA Ops:
  6.5 2.0 %multiply_reduce_fusion = f32[8,11264]{1,0:T(8,128)S(1)} fusion(f32[8,2,18432]{2,1,0:T(2,128)} %param.6), kind=kLoop, calls=%fused_computation.12 | loop fusion | flops 270336 | bytes 1081344 | tf_op jit(solution)/shard_map/reduce_sum | solution.py:16
  8.8 0.3 reduce_sum.50
  9.1 0.3 mul.169
  9.9 0.4 fusion.8
  10.2 0.8 copy.14
  11.3 0.6 multiply_reduce_fusion.1
  12.6 0.2 fusion.11
  12.8 0.7 copy.13
  13.6 4.2 %fusion.4 = (f32[288,896]{1,0:T(8,128)S(1)}, f32[288,896]{1,0:T(8,128)S(1)}) fusion(s32[288]{0:T(512)S(1)} %iota_multiply_fusion), kind=kLoop, calls=%fused_computation.7 | loop fusion | flops 2322432 | bytes 2065536 | tf_op jit(solution)/shard_map/sin | solution.py:24
  18.1 0.4 copy-done.4
  19.0 0.9 fusion.14
  20.1 29.8 %all-gather.5.cloned.1.call-done = bf16[64,22528]{1,0:T(8,128)(2,1)} async-done(((bf16[8,22528]{1,0:T(8,128)(2,1)}), bf16[64,22528]{1,0:T(8,128)(2,1)}) %all-gather.5.cloned.1.call-update) | async-done | bytes 2883600 | tf_op jit(solution)/shard_map/all_gather | solution.py:128
  49.9 7.5 %fusion.20.a0_ref.a1_ref.b0_ref.b1_ref = bf16[192,22528]{1,0:T(8,128)(2,1)} fusion(bf16[64,22528]{1,0:T(8,128)(2,1)} %all-gather.5.cloned.1.call-done, pred[96,64]{1,0:T(32,128)(4,1)S(1)} %get-tuple-element.16, pred[96,64]{1,0:T(32,128)(4,1)S(1)} %get-tuple-element.17), kind=kOutput, calls=%fused_computation.38 | convolution fusion | flops 553660416 | bytes 11546624 | tf_op jit(solution)/shard_map/dot_general | solution.py:131
  57.4 26.1 %shard_map.64.acc_ref = f32[96,1792]{1,0:T(8,128)S(1)} custom-call(bf16[192,22528]{1,0:T(8,128)(2,1)} %fusion.20.a0_ref.a1_ref.b0_ref.b1_ref, bf16[192,22528]{1,0:T(8,128)(2,1)} %fusion.20.a0_ref.a1_ref.b0_ref.b1_ref, bf16[192,22528]{1,0:T(8,128)(2,1)} %fusion.20.a0_ref.a1_ref.b0_ref.b1_ref, ...), custom_call_target="tpu_custom_call", output_to_operand_aliasing={{}: (8, {})} | custom-call | flops 3976462336 | bytes 8994816 | tf_op jit(solution)/shard_map/pallas_call | solution.py:67
  83.5 5.5 %fusion.21.a0_ref.a1_ref.b0_ref.b1_ref = bf16[192,14336]{1,0:T(8,128)(2,1)} fusion(bf16[64,14336]{1,0:T(8,128)(2,1)} %all-gather.3.cloned.1.call-done, pred[96,64]{1,0:T(32,128)(4,1)S(1)} %get-tuple-element.16, pred[96,64]{1,0:T(32,128)(4,1)S(1)} %get-tuple-element.17), kind=kOutput, calls=%fused_computation.39 | convolution fusion | flops 352333824 | bytes 7352320 | tf_op jit(solution)/shard_map/dot_general | solution.py:131
  89.0 16.9 %shard_map.65 = f32[96,1792]{1,0:T(8,128)S(1)} custom-call(bf16[192,14336]{1,0:T(8,128)(2,1)} %fusion.21.a0_ref.a1_ref.b0_ref.b1_ref, bf16[192,14336]{1,0:T(8,128)(2,1)} %fusion.21.a0_ref.a1_ref.b0_ref.b1_ref, bf16[192,14336]{1,0:T(8,128)(2,1)} %fusion.21.a0_ref.a1_ref.b0_ref.b1_ref, ...), custom_call_target="tpu_custom_call", output_to_operand_aliasing={{}: (8, {})} | custom-call | flops 2530476032 | bytes 5849088 | tf_op jit(solution)/shard_map/pallas_call | solution.py:67
  106.0 0.2 slice_add_fusion
  106.2 0.6 reverse
  107.3 0.6 fusion.18
  107.9 1.2 reshape.51
  109.1 3.6 %all-to-all-start = ((f32[32,4,1664]{2,1,0:T(4,128)}), f32[32,4,1664]{2,1,0:T(4,128)S(1)}, u32[]{:S(2)}, u32[]{:S(2)}) async-start(f32[32,4,1664]{2,1,0:T(4,128)} %reshape.51), calls=%async_computation | async-start | bytes 1703936 | tf_op jit(solution)/shard_map/all_to_all | solution.py:153
  112.7 23.2 %all-to-all-done = f32[32,4,1664]{2,1,0:T(4,128)S(1)} async-done(((f32[32,4,1664]{2,1,0:T(4,128)}), f32[32,4,1664]{2,1,0:T(4,128)S(1)}, u32[]{:S(2)}, u32[]{:S(2)}) %all-to-all-start) | async-done | bytes 852000 | tf_op jit(solution)/shard_map/all_to_all | solution.py:153
  136.0 0.3 reshape.52
  136.4 1.4 convolution_add_fusion
  (46 shorter events, 3.1 us)
Async XLA Ops:
  6.5 43.4 %all-gather.5.cloned.1.call-start = ((), (), s32[]{:S(2)}) async-start(), calls=%async_computation.2 | async-start | bytes 3244032 | tf_op jit(solution)/shard_map/all_gather | solution.py:128
  8.6 1.3 copy-start
  11.1 72.5 %all-gather.3.cloned.1.call-start = ((), (), s32[]{:S(2)}) async-start(), calls=%async_computation.1 | async-start | bytes 2064384 | tf_op jit(solution)/shard_map/all_gather | solution.py:128
  17.8 0.7 copy-start.4
  17.9 0.8 copy-start.2
  17.9 2.0 %copy-start.5 = (s32[96]{0:T(128)S(1)}, s32[96]{0:T(128)}, u32[]{:S(2)}) copy-start(s32[96]{0:T(128)} %param.9) | copy-start | bytes 1156
  17.9 2.1 %copy-start.3 = (s32[2,96]{1,0:T(2,128)S(1)}, s32[2,96]{1,0:T(2,128)}, u32[]{:S(2)}) copy-start(s32[2,96]{1,0:T(2,128)} %param.8) | copy-start | bytes 2308
  109.1 27.4 %copy-start.1 = (f32[96,1601]{1,0:T(8,128)S(1)}, f32[96,1601]{1,0:T(8,128)}, u32[]{:S(2)}) copy-start(f32[96,1601]{1,0:T(8,128)} %param.7) | copy-start | bytes 1844356
  109.1 26.9 %all-to-all-start = ((f32[32,4,1664]{2,1,0:T(4,128)}), f32[32,4,1664]{2,1,0:T(4,128)S(1)}, u32[]{:S(2)}, u32[]{:S(2)}) async-start(f32[32,4,1664]{2,1,0:T(4,128)} %reshape.51), calls=%async_computation | async-start | bytes 1703936 | tf_op jit(solution)/shard_map/all_to_all | solution.py:153
Sparse Core Ops, SparseCore 0:
  11.2 38.6 all-gather.4
  51.5 25.9 all-gather.2

commit v9 on v8

--- a/solution.py
+++ b/solution.py
@@ -25,7 +25,7 @@
 
 
 LOW = 64
-FBLOCK = 1024
+FBLOCK = 2048
 
 
 def table_kernel(a0_ref, a1_ref, b0_ref, b1_ref, chi_ref, shi_ref, clo_ref, slo_ref, acc_ref, out_ref, ctab, stab):
@@ -118,7 +118,7 @@
     lo_all = angle_table(lax.iota(jnp.int32, LOW), lag_pad, total_bins)
     blocks = total_bins // FBLOCK
     assert total_bins % FBLOCK == 0
-    lead = max(1, min(blocks - 1, (blocks * 31 + 25) // 50))
+    lead = max(1, min(blocks - 1, (blocks * 57 + 50) // 100))
     bounds = [0, lead * FBLOCK, total_bins] if blocks > 1 else [0, total_bins]
     corr = jnp.zeros((pair_count, 2 * lag_pad), jnp.float32)
     for c in range(len(bounds) - 1):

time: 145 us -> 142 us (0.979)
  waiting for transfers between devices: 53.1 us -> 50.4 us
    all_gather x2, waiting for transfers between devices: 29.8 us -> 27.2 us  [local(): flat = lax.all_gather(piece, 'sta', axis=0, tiled=True)]
  transfers between devices with their start and end apart: 3 -> 3, of which waited for: 2 -> 2; matrix products, arithmetic and copies ran while one was open for 11% -> 11% of each run, Pallas kernels for 18% -> 17%
where the time goes in v9:
time: 142 us; the launch traced here: 141 us
  waiting for transfers between devices  50.4 us (35%)
  Pallas kernels  42.1 us (30%)
  matrix products  15 us (11%)
  between operations  13.7 us (10%)
  other arithmetic  10.1 us (7%)
  local copies, waits for them, and re-layouts  6.24 us (4%)
  starting transfers between devices  3.92 us (3%)
    pallas_call x2, Pallas kernels, correlate(): pl.pallas_call(table_kernel, grid=(blocks,), in_specs=[pl.BlockSpec((pair...  42.1 us
    all_gather x2, waiting for transfers between devices, local(): flat = lax.all_gather(piece, 'sta', axis=0, tiled=True)  27.2 us
    all_to_all x1, waiting for transfers between devices, local(): lax.all_to_all(send_rows.reshape(devices, capacity, corr.shape[1]), ('grp...  23.2 us
    dot_general x2, matrix products, local(): both = jnp.dot(picks, flat, preferred_element_type=jnp.bfloat16)  13 us
    sin x2, other arithmetic, angle_table(): return (jnp.cos(theta), jnp.sin(theta))  5.18 us
    all_to_all x1, starting transfers between devices, local(): lax.all_to_all(send_rows.reshape(devices, capacity, corr.shape[1]), ('grp...  3.69 us
    reduce_sum x4, other arithmetic, whiten(): power = jnp.mean(split * split, axis=(1, 3), keepdims=True)  3.25 us
    unnamed x16, local copies, waits for them, and re-layouts  2.9 us
  transfers between devices with their start and end apart: 3, of which 2 were waited for; matrix products, arithmetic and copies ran while one was open for 11% of the time, Pallas kernels for 17%

profile of v9, /device:TPU:0, one launch (start us, length us, event | category | flops | bytes accessed | tf_op | source)
XLA Modules:
  0.0 141.5 jit_solution(13240970347287675225)
XLA Ops:
  6.5 2.0 %multiply_reduce_fusion = f32[8,10240]{1,0:T(8,128)S(1)} fusion(f32[8,2,18432]{2,1,0:T(2,128)} %param.6), kind=kLoop, calls=%fused_computation.12 | loop fusion | flops 245760 | bytes 983040 | tf_op jit(solution)/shard_map/reduce_sum | solution.py:16
  8.6 0.2 reduce_sum.49
  8.8 0.3 reduce_sum.50
  9.7 0.3 fusion.8
  10.0 0.8 copy.14
  11.1 0.7 multiply_reduce_fusion.1
  12.6 0.3 fusion.9
  12.9 0.9 copy.13
  13.8 4.2 %fusion.4 = (f32[288,896]{1,0:T(8,128)S(1)}, f32[288,896]{1,0:T(8,128)S(1)}) fusion(s32[288]{0:T(512)S(1)} %iota_multiply_fusion), kind=kLoop, calls=%fused_computation.7 | loop fusion | flops 2322432 | bytes 2065536 | tf_op jit(solution)/shard_map/sin | solution.py:24
  18.3 0.4 copy-done.4
  19.2 0.9 fusion.14
  20.3 27.1 %all-gather.5.cloned.1.call-done = bf16[64,20480]{1,0:T(8,128)(2,1)} async-done(((bf16[8,20480]{1,0:T(8,128)(2,1)}), bf16[64,20480]{1,0:T(8,128)(2,1)}) %all-gather.5.cloned.1.call-update) | async-done | bytes 2621456 | tf_op jit(solution)/shard_map/all_gather | solution.py:128
  47.4 7.0 %fusion.20.a0_ref.a1_ref.b0_ref.b1_ref = bf16[192,20480]{1,0:T(8,128)(2,1)} fusion(bf16[64,20480]{1,0:T(8,128)(2,1)} %all-gather.5.cloned.1.call-done, pred[96,64]{1,0:T(32,128)(4,1)S(1)} %get-tuple-element.16, pred[96,64]{1,0:T(32,128)(4,1)S(1)} %get-tuple-element.17), kind=kOutput, calls=%fused_computation.38 | convolution fusion | flops 503328768 | bytes 10498048 | tf_op jit(solution)/shard_map/dot_general | solution.py:131
  54.5 23.4 %shard_map.64.acc_ref = f32[96,1792]{1,0:T(8,128)S(1)} custom-call(bf16[192,20480]{1,0:T(8,128)(2,1)} %fusion.20.a0_ref.a1_ref.b0_ref.b1_ref, bf16[192,20480]{1,0:T(8,128)(2,1)} %fusion.20.a0_ref.a1_ref.b0_ref.b1_ref, bf16[192,20480]{1,0:T(8,128)(2,1)} %fusion.20.a0_ref.a1_ref.b0_ref.b1_ref, ...), custom_call_target="tpu_custom_call", output_to_operand_aliasing={{}: (8, {})} | custom-call | flops 3614965760 | bytes 8208384 | tf_op jit(solution)/shard_map/pallas_call | solution.py:67
  77.9 6.0 %fusion.21.a0_ref.a1_ref.b0_ref.b1_ref = bf16[192,16384]{1,0:T(8,128)(2,1)} fusion(bf16[64,16384]{1,0:T(8,128)(2,1)} %all-gather.3.cloned.1.call-done, pred[96,64]{1,0:T(32,128)(4,1)S(1)} %get-tuple-element.16, pred[96,64]{1,0:T(32,128)(4,1)S(1)} %get-tuple-element.17), kind=kOutput, calls=%fused_computation.39 | convolution fusion | flops 402665472 | bytes 8400896 | tf_op jit(solution)/shard_map/dot_general | solution.py:131
  83.9 18.7 %shard_map.65 = f32[96,1792]{1,0:T(8,128)S(1)} custom-call(bf16[192,16384]{1,0:T(8,128)(2,1)} %fusion.21.a0_ref.a1_ref.b0_ref.b1_ref, bf16[192,16384]{1,0:T(8,128)(2,1)} %fusion.21.a0_ref.a1_ref.b0_ref.b1_ref, bf16[192,16384]{1,0:T(8,128)(2,1)} %fusion.21.a0_ref.a1_ref.b0_ref.b1_ref, ...), custom_call_target="tpu_custom_call", output_to_operand_aliasing={{}: (8, {})} | custom-call | flops 2891972608 | bytes 6635520 | tf_op jit(solution)/shard_map/pallas_call | solution.py:67
  102.8 0.2 slice_add_fusion
  103.0 0.6 reverse
  104.1 0.6 fusion.18
  104.7 1.2 reshape.51
  105.9 3.7 %all-to-all-start = ((f32[32,4,1664]{2,1,0:T(4,128)}), f32[32,4,1664]{2,1,0:T(4,128)S(1)}, u32[]{:S(2)}, u32[]{:S(2)}) async-start(f32[32,4,1664]{2,1,0:T(4,128)} %reshape.51), calls=%async_computation | async-start | bytes 1703936 | tf_op jit(solution)/shard_map/all_to_all | solution.py:153
  109.6 23.2 %all-to-all-done = f32[32,4,1664]{2,1,0:T(4,128)S(1)} async-done(((f32[32,4,1664]{2,1,0:T(4,128)}), f32[32,4,1664]{2,1,0:T(4,128)S(1)}, u32[]{:S(2)}, u32[]{:S(2)}) %all-to-all-start) | async-done | bytes 852000 | tf_op jit(solution)/shard_map/all_to_all | solution.py:153
  132.8 0.3 reshape.52
  133.3 1.4 convolution_add_fusion
  (46 shorter events, 3.1 us)
Async XLA Ops:
  6.5 3.1 %copy-start = (f32[8,2,18432]{2,1,0:T(2,128)S(1)}, f32[8,2,18432]{2,1,0:T(2,128)}, u32[]{:S(2)}) copy-start(f32[8,2,18432]{2,1,0:T(2,128)} %param.6) | copy-start | bytes 3538948
  6.5 40.9 %all-gather.5.cloned.1.call-start = ((), (), s32[]{:S(2)}) async-start(), calls=%async_computation.2 | async-start | bytes 2949120 | tf_op jit(solution)/shard_map/all_gather | solution.py:128
  10.9 67.0 %all-gather.3.cloned.1.call-start = ((), (), s32[]{:S(2)}) async-start(), calls=%async_computation.1 | async-start | bytes 2359296 | tf_op jit(solution)/shard_map/all_gather | solution.py:128
  18.0 0.7 copy-start.4
  18.0 0.8 copy-start.2
  18.1 2.1 %copy-start.5 = (s32[96]{0:T(128)S(1)}, s32[96]{0:T(128)}, u32[]{:S(2)}) copy-start(s32[96]{0:T(128)} %param.9) | copy-start | bytes 1156
  18.1 2.1 %copy-start.3 = (s32[2,96]{1,0:T(2,128)S(1)}, s32[2,96]{1,0:T(2,128)}, u32[]{:S(2)}) copy-start(s32[2,96]{1,0:T(2,128)} %param.8) | copy-start | bytes 2308
  105.9 27.4 %copy-start.1 = (f32[96,1601]{1,0:T(8,128)S(1)}, f32[96,1601]{1,0:T(8,128)}, u32[]{:S(2)}) copy-start(f32[96,1601]{1,0:T(8,128)} %param.7) | copy-start | bytes 1844356
  105.9 27.0 %all-to-all-start = ((f32[32,4,1664]{2,1,0:T(4,128)}), f32[32,4,1664]{2,1,0:T(4,128)S(1)}, u32[]{:S(2)}, u32[]{:S(2)}) async-start(f32[32,4,1664]{2,1,0:T(4,128)} %reshape.51), calls=%async_computation | async-start | bytes 1703936 | tf_op jit(solution)/shard_map/all_to_all | solution.py:153
Sparse Core Ops, SparseCore 0:
  11.0 36.4 all-gather.4
  49.0 28.2 all-gather.2

commit v10 on v9

--- a/solution.py
+++ b/solution.py
@@ -28,15 +28,19 @@
 FBLOCK = 2048
 
 
-def table_kernel(a0_ref, a1_ref, b0_ref, b1_ref, chi_ref, shi_ref, clo_ref, slo_ref, acc_ref, out_ref, ctab, stab):
+def table_kernel(pick_ref, g0_ref, g1_ref, chi_ref, shi_ref, clo_ref, slo_ref, acc_ref, out_ref, ctab, stab):
     @pl.when(pl.program_id(0) == 0)
     def _():
         out_ref[...] = acc_ref[...]
 
-    a0 = a0_ref[...].astype(jnp.float32)
-    a1 = a1_ref[...].astype(jnp.float32)
-    b0 = b0_ref[...].astype(jnp.float32)
-    b1 = b1_ref[...].astype(jnp.float32)
+    pairs = out_ref.shape[0]
+    picks = pick_ref[...]
+    rows0 = jnp.dot(picks, g0_ref[...], preferred_element_type=jnp.float32)
+    rows1 = jnp.dot(picks, g1_ref[...], preferred_element_type=jnp.float32)
+    a0 = rows0[:pairs]
+    b0 = rows0[pairs:]
+    a1 = rows1[:pairs]
+    b1 = rows1[pairs:]
     real = (a0 * b0 + a1 * b1).astype(jnp.bfloat16)
     imag = (a1 * b0 - a0 * b1).astype(jnp.bfloat16)
 
@@ -56,11 +60,12 @@
     out_ref[:, half:] += jnp.dot(imag, stab[...], preferred_element_type=jnp.float32)
 
 
-def correlate(both, tables, acc):
+def correlate(picks, flat, tables, acc):
     cos_hi, sin_hi, cos_lo, sin_lo = tables
-    pair_count = both.shape[0] // 2
+    pair_count = picks.shape[0] // 2
+    group_sta = flat.shape[0]
     lag_pad = cos_lo.shape[1]
-    width = both.shape[1] // 2
+    width = flat.shape[1] // 2
     hi_rows = FBLOCK // LOW
     assert width % FBLOCK == 0
     blocks = width // FBLOCK
@@ -68,10 +73,9 @@
         table_kernel,
         grid=(blocks,),
         in_specs=[
-            pl.BlockSpec((pair_count, FBLOCK), lambda i: (0, i)),
-            pl.BlockSpec((pair_count, FBLOCK), lambda i: (0, i + blocks)),
-            pl.BlockSpec((pair_count, FBLOCK), lambda i: (1, i)),
-            pl.BlockSpec((pair_count, FBLOCK), lambda i: (1, i + blocks)),
+            pl.BlockSpec((2 * pair_count, group_sta), lambda i: (0, 0)),
+            pl.BlockSpec((group_sta, FBLOCK), lambda i: (0, i)),
+            pl.BlockSpec((group_sta, FBLOCK), lambda i: (0, i + blocks)),
             pl.BlockSpec((hi_rows, lag_pad), lambda i: (i, 0)),
             pl.BlockSpec((hi_rows, lag_pad), lambda i: (i, 0)),
             pl.BlockSpec((LOW, lag_pad), lambda i: (0, 0)),
@@ -92,8 +96,8 @@
             transcendentals=0,
             bytes_accessed=4 * pair_count * width * 2 + 4 * pair_count * lag_pad,
         ),
-        input_output_aliases={8: 0},
-    )(both, both, both, both, cos_hi, sin_hi, cos_lo, sin_lo, acc)
+        input_output_aliases={7: 0},
+    )(picks, flat, flat, cos_hi, sin_hi, cos_lo, sin_lo, acc)
     return out
 
 
@@ -128,10 +132,9 @@
         flat = lax.all_gather(piece, "sta", axis=0, tiled=True)
         if c:
             flat, corr = lax.optimization_barrier((flat, corr))
-        both = jnp.dot(picks, flat, preferred_element_type=jnp.bfloat16)
         rows = slice(begin // LOW, end // LOW)
         tables = (hi_all[0][rows], hi_all[1][rows], lo_all[0], lo_all[1])
-        corr = correlate(both, tables, corr)
+        corr = correlate(picks, flat, tables, corr)
     even = corr[:, : side + 1]
     odd = corr[:, lag_pad : lag_pad + side + 1]
     corr = jnp.concatenate([(even + odd)[:, :0:-1], even - odd], axis=1)

time: 142 us -> 135 us (0.951)
  matrix products: 15 us -> 1.96 us
  waiting for transfers between devices: 50.4 us -> 57.8 us
  Pallas kernels: 42.1 us -> 37.4 us
  local copies, waits for them, and re-layouts: 6.24 us -> 10.1 us
    dot_general x2 -> x0, matrix products: 13 us -> none  [local(): both = jnp.dot(picks, flat, preferred_element_type=jnp.bfloat16)]
    all_gather x2, waiting for transfers between devices: 27.2 us -> 34.5 us  [local(): flat = lax.all_gather(piece, 'sta', axis=0, tiled=True)]
    pallas_call x2, Pallas kernels: 42.1 us -> 37.4 us  [correlate(): pl.pallas_call(table_kernel, grid=(blocks,), in_specs=[pl.BlockSpec((2 *...]
    unnamed x16 -> x20, local copies, waits for them, and re-layouts: 2.9 us -> 6.74 us
  transfers between devices with their start and end apart: 3 -> 3, of which waited for: 2 -> 3; matrix products, arithmetic and copies ran while one was open for 11% -> 6% of each run, Pallas kernels for 17% -> 15%
where the time goes in v10:
time: 135 us
  waiting for transfers between devices  57.8 us (43%)
  Pallas kernels  37.4 us (28%)
  between operations  13.7 us (10%)
  local copies, waits for them, and re-layouts  10.1 us (7%)
  other arithmetic  9.98 us (7%)
  starting transfers between devices  4.05 us (3%)
  matrix products  1.96 us (1%)
    pallas_call x2, Pallas kernels, correlate(): pl.pallas_call(table_kernel, grid=(blocks,), in_specs=[pl.BlockSpec((2 *...  37.4 us
    all_gather x2, waiting for transfers between devices, local(): flat = lax.all_gather(piece, 'sta', axis=0, tiled=True)  34.5 us
    all_to_all x1, waiting for transfers between devices, local(): lax.all_to_all(send_rows.reshape(devices, capacity, corr.shape[1]), ('grp...  23.2 us
    unnamed x20, local copies, waits for them, and re-layouts  6.74 us
    sin x2, other arithmetic, angle_table(): return (jnp.cos(theta), jnp.sin(theta))  5.18 us
    all_to_all x1, starting transfers between devices, local(): lax.all_to_all(send_rows.reshape(devices, capacity, corr.shape[1]), ('grp...  4 us
    reduce_sum x4, other arithmetic, whiten(): power = jnp.mean(split * split, axis=(1, 3), keepdims=True)  3.15 us
  transfers between devices with their start and end apart: 3, of which 3 were waited for; matrix products, arithmetic and copies ran while one was open for 6% of the time, Pallas kernels for 15%

profile of v10, /device:TPU:0, one launch (start us, length us, event | category | flops | bytes accessed | tf_op | source)
XLA Modules:
  0.0 135.0 jit_solution(15858679049103524433)
XLA Ops:
  6.5 1.9 %multiply_reduce_fusion = f32[8,10240]{1,0:T(8,128)S(1)} fusion(f32[8,2,18432]{2,1,0:T(2,128)} %param.6), kind=kLoop, calls=%fused_computation.12 | loop fusion | flops 245760 | bytes 983040 | tf_op jit(solution)/shard_map/reduce_sum | solution.py:16
  8.7 0.3 reduce_sum.50
  9.6 0.4 copy-done.2
  10.0 0.3 fusion.8
  10.4 0.8 copy.14
  11.2 0.7 multiply_reduce_fusion.1
  12.8 0.3 fusion.9
  13.1 0.9 copy.13
  13.9 4.2 %fusion.4 = (f32[288,896]{1,0:T(8,128)S(1)}, f32[288,896]{1,0:T(8,128)S(1)}) fusion(s32[288]{0:T(512)S(1)} %iota_multiply_fusion), kind=kLoop, calls=%fused_computation.7 | loop fusion | flops 2322432 | bytes 2065536 | tf_op jit(solution)/shard_map/sin | solution.py:24
  18.4 0.5 copy-done.6
  19.6 0.9 fusion.14
  20.6 27.2 %all-gather.5.cloned.1.call-done.g0_ref.g1_ref = bf16[64,20480]{1,0:T(8,128)(2,1)} async-done(((bf16[8,20480]{1,0:T(8,128)(2,1)}), bf16[64,20480]{1,0:T(8,128)(2,1)}) %all-gather.5.cloned.1.call-update) | async-done | bytes 2621456 | tf_op jit(solution)/shard_map/all_gather | solution.py:132
  47.9 1.7 %copy-done = bf16[64,20480]{1,0:T(8,128)(2,1)S(1)} copy-done((bf16[64,20480]{1,0:T(8,128)(2,1)S(1)}, bf16[64,20480]{1,0:T(8,128)(2,1)}, u32[]{:S(2)}) %copy-start) | copy-done | bytes 2621464
  49.6 20.8 %shard_map.64.acc_ref = f32[96,1792]{1,0:T(8,128)S(1)} custom-call(bf16[192,64]{1,0:T(8,128)(2,1)S(1)} %add_convert_fusion.pick_ref, bf16[64,20480]{1,0:T(8,128)(2,1)S(1)} %copy-done, bf16[64,20480]{1,0:T(8,128)(2,1)S(1)} %copy-done, f32[160,896]{1,0:T(8,128)S(1)} %slice.52.chi_ref, f32[160,896]{1,0:T(8,128)S(1)} %slice.53.shi_ref, ...), custom_call_target="tpu_custom_call", output_to_operand_aliasing={{}: (7, {})} | custom-call | flops 3614965760 | bytes 8208384 | tf_op jit(solution)/shard_map/pallas_call | solution.py:72
  70.4 7.3 %all-gather.3.cloned.1.call-done.g0_ref.g1_ref = bf16[64,16384]{1,0:T(8,128)(2,1)} async-done(((bf16[8,16384]{1,0:T(8,128)(2,1)}), bf16[64,16384]{1,0:T(8,128)(2,1)}) %all-gather.3.cloned.1.call-update) | async-done | bytes 2097168 | tf_op jit(solution)/shard_map/all_gather | solution.py:132
  77.7 1.6 %copy-done.1 = bf16[64,16384]{1,0:T(8,128)(2,1)S(1)} copy-done((bf16[64,16384]{1,0:T(8,128)(2,1)S(1)}, bf16[64,16384]{1,0:T(8,128)(2,1)}, u32[]{:S(2)}) %copy-start.1) | copy-done | bytes 2097176
  79.3 16.6 %shard_map.65 = f32[96,1792]{1,0:T(8,128)S(1)} custom-call(bf16[192,64]{1,0:T(8,128)(2,1)S(1)} %add_convert_fusion.pick_ref, bf16[64,16384]{1,0:T(8,128)(2,1)S(1)} %copy-done.1, bf16[64,16384]{1,0:T(8,128)(2,1)S(1)} %copy-done.1, f32[128,896]{1,0:T(8,128)S(1)} %slice.54.chi_ref, f32[128,896]{1,0:T(8,128)S(1)} %slice.55.shi_ref, ...), custom_call_target="tpu_custom_call", output_to_operand_aliasing={{}: (7, {})} | custom-call | flops 2891972608 | bytes 6635520 | tf_op jit(solution)/shard_map/pallas_call | solution.py:72
  96.3 0.6 reverse
  97.3 0.6 fusion.18
  98.0 1.2 reshape.51
  99.1 4.0 %all-to-all-start = ((f32[32,4,1664]{2,1,0:T(4,128)}), f32[32,4,1664]{2,1,0:T(4,128)S(1)}, u32[]{:S(2)}, u32[]{:S(2)}) async-start(f32[32,4,1664]{2,1,0:T(4,128)} %reshape.51), calls=%async_computation | async-start | bytes 1703936 | tf_op jit(solution)/shard_map/all_to_all | solution.py:156
  103.1 23.2 %all-to-all-done = f32[32,4,1664]{2,1,0:T(4,128)S(1)} async-done(((f32[32,4,1664]{2,1,0:T(4,128)}), f32[32,4,1664]{2,1,0:T(4,128)S(1)}, u32[]{:S(2)}, u32[]{:S(2)}) %all-to-all-start) | async-done | bytes 852000 | tf_op jit(solution)/shard_map/all_to_all | solution.py:156
  126.4 0.3 reshape.52
  126.9 1.4 %convolution_add_fusion = f32[96,1601]{1,0:T(8,128)} fusion(f32[96,1601]{1,0:T(8,128)S(1)} %copy-done.3, f32[128,1664]{1,0:T(8,128)S(1)} %reshape.52, f32[128]{0:T(128)S(1)} %slice_reduce_fusion, f32[96]{0:T(128)S(1)} %iota_convert_fusion), kind=kOutput, calls=%fused_computation | convolution fusion | flops 236243040 | bytes 2082432 | tf_op jit(solution)/shard_map/dot_general | solution.py:168
  (49 shorter events, 3.4 us)
Async XLA Ops:
  6.5 41.3 %all-gather.5.cloned.1.call-start = ((), (), s32[]{:S(2)}) async-start(), calls=%async_computation.2 | async-start | bytes 2949120 | tf_op jit(solution)/shard_map/all_gather | solution.py:132
  8.7 1.3 copy-start.2
  11.2 66.5 %all-gather.3.cloned.1.call-start = ((), (), s32[]{:S(2)}) async-start(), calls=%async_computation.1 | async-start | bytes 2359296 | tf_op jit(solution)/shard_map/all_gather | solution.py:132
  18.3 0.7 copy-start.6
  18.3 0.8 copy-start.4
  18.3 1.0 copy-start.5
  18.3 2.2 %copy-start.7 = (s32[96]{0:T(128)S(1)}, s32[96]{0:T(128)}, u32[]{:S(2)}) copy-start(s32[96]{0:T(128)} %param.9) | copy-start | bytes 1156
  47.9 1.7 %copy-start = (bf16[64,20480]{1,0:T(8,128)(2,1)S(1)}, bf16[64,20480]{1,0:T(8,128)(2,1)}, u32[]{:S(2)}) copy-start(bf16[64,20480]{1,0:T(8,128)(2,1)} %all-gather.5.cloned.1.call-done.g0_ref.g1_ref) | copy-start | bytes 7864324
  77.7 1.6 %copy-start.1 = (bf16[64,16384]{1,0:T(8,128)(2,1)S(1)}, bf16[64,16384]{1,0:T(8,128)(2,1)}, u32[]{:S(2)}) copy-start(bf16[64,16384]{1,0:T(8,128)(2,1)} %all-gather.3.cloned.1.call-done.g0_ref.g1_ref) | copy-start | bytes 6291460
  99.1 27.3 %all-to-all-start = ((f32[32,4,1664]{2,1,0:T(4,128)}), f32[32,4,1664]{2,1,0:T(4,128)S(1)}, u32[]{:S(2)}, u32[]{:S(2)}) async-start(f32[32,4,1664]{2,1,0:T(4,128)} %reshape.51), calls=%async_computation | async-start | bytes 1703936 | tf_op jit(solution)/shard_map/all_to_all | solution.py:156
  103.1 23.7 %copy-start.3 = (f32[96,1601]{1,0:T(8,128)S(1)}, f32[96,1601]{1,0:T(8,128)}, u32[]{:S(2)}) copy-start(f32[96,1601]{1,0:T(8,128)} %param.7) | copy-start | bytes 1844356
Sparse Core Ops, SparseCore 0:
  11.3 36.4 all-gather.4
  49.4 28.2 all-gather.2

commit v11 on v10

--- a/solution.py
+++ b/solution.py
@@ -122,7 +122,7 @@
     lo_all = angle_table(lax.iota(jnp.int32, LOW), lag_pad, total_bins)
     blocks = total_bins // FBLOCK
     assert total_bins % FBLOCK == 0
-    lead = max(1, min(blocks - 1, (blocks * 57 + 50) // 100))
+    lead = max(1, min(blocks - 1, (2 * blocks + 1) // 3))
     bounds = [0, lead * FBLOCK, total_bins] if blocks > 1 else [0, total_bins]
     corr = jnp.zeros((pair_count, 2 * lag_pad), jnp.float32)
     for c in range(len(bounds) - 1):

time: 135 us -> 133 us (0.985)
  waiting for transfers between devices: 57.8 us -> 55.5 us
    all_gather x2, waiting for transfers between devices: 34.5 us -> 32.2 us  [local(): flat = lax.all_gather(piece, 'sta', axis=0, tiled=True)]
  transfers between devices with their start and end apart: 3 -> 3, of which waited for: 3 -> 2; matrix products, arithmetic and copies ran while one was open for 6% -> 6% of each run, Pallas kernels for 15% -> 19%
where the time goes in v11:
time: 133 us
  waiting for transfers between devices  55.5 us (42%)
  Pallas kernels  37.4 us (28%)
  between operations  13.8 us (10%)
  local copies, waits for them, and re-layouts  10.3 us (8%)
  other arithmetic  10 us (8%)
  starting transfers between devices  3.51 us (3%)
  matrix products  1.96 us (1%)
    pallas_call x2, Pallas kernels, correlate(): pl.pallas_call(table_kernel, grid=(blocks,), in_specs=[pl.BlockSpec((2 *...  37.4 us
    all_gather x2, waiting for transfers between devices, local(): flat = lax.all_gather(piece, 'sta', axis=0, tiled=True)  32.2 us
    all_to_all x1, waiting for transfers between devices, local(): lax.all_to_all(send_rows.reshape(devices, capacity, corr.shape[1]), ('grp...  23.2 us
    unnamed x20, local copies, waits for them, and re-layouts  7.01 us
    sin x2, other arithmetic, angle_table(): return (jnp.cos(theta), jnp.sin(theta))  5.18 us
    all_to_all x1, starting transfers between devices, local(): lax.all_to_all(send_rows.reshape(devices, capacity, corr.shape[1]), ('grp...  3.46 us
    reduce_sum x4, other arithmetic, whiten(): power = jnp.mean(split * split, axis=(1, 3), keepdims=True)  3.21 us
  transfers between devices with their start and end apart: 3, of which 2 were waited for; matrix products, arithmetic and copies ran while one was open for 6% of the time, Pallas kernels for 19%

profile of v11, /device:TPU:0, one launch (start us, length us, event | category | flops | bytes accessed | tf_op | source)
XLA Modules:
  0.0 132.6 jit_solution(6251729294419438392)
XLA Ops:
  6.5 2.2 %multiply_reduce_fusion = f32[8,12288]{1,0:T(8,128)S(1)} fusion(f32[8,2,18432]{2,1,0:T(2,128)} %param.6), kind=kLoop, calls=%fused_computation.12 | loop fusion | flops 294912 | bytes 1179648 | tf_op jit(solution)/shard_map/reduce_sum | solution.py:16
  8.7 0.3 reduce_sum.49
  9.0 0.3 reduce_sum.50
  9.7 0.3 mul.170
  9.9 0.7 copy-done.2
  10.6 0.4 fusion.8
  11.1 1.0 copy.14
  12.1 0.5 multiply_reduce_fusion.1
  13.5 0.7 copy.13
  14.3 4.2 %fusion.4 = (f32[288,896]{1,0:T(8,128)S(1)}, f32[288,896]{1,0:T(8,128)S(1)}) fusion(s32[288]{0:T(512)S(1)} %iota_multiply_fusion), kind=kLoop, calls=%fused_computation.7 | loop fusion | flops 2322432 | bytes 2065536 | tf_op jit(solution)/shard_map/sin | solution.py:24
  18.8 0.5 copy-done.6
  20.0 0.9 fusion.13
  20.9 32.2 %all-gather.5.cloned.1.call-done.g0_ref.g1_ref = bf16[64,24576]{1,0:T(8,128)(2,1)} async-done(((bf16[8,24576]{1,0:T(8,128)(2,1)}), bf16[64,24576]{1,0:T(8,128)(2,1)}) %all-gather.5.cloned.1.call-update) | async-done | bytes 3145744 | tf_op jit(solution)/shard_map/all_gather | solution.py:132
  53.2 1.9 %copy-done = bf16[64,24576]{1,0:T(8,128)(2,1)S(1)} copy-done((bf16[64,24576]{1,0:T(8,128)(2,1)S(1)}, bf16[64,24576]{1,0:T(8,128)(2,1)}, u32[]{:S(2)}) %copy-start) | copy-done | bytes 3145752
  55.1 24.9 %shard_map.64.acc_ref = f32[96,1792]{1,0:T(8,128)S(1)} custom-call(bf16[192,64]{1,0:T(8,128)(2,1)S(1)} %add_convert_fusion.pick_ref, bf16[64,24576]{1,0:T(8,128)(2,1)S(1)} %copy-done, bf16[64,24576]{1,0:T(8,128)(2,1)S(1)} %copy-done, f32[192,896]{1,0:T(8,128)S(1)} %slice.52.chi_ref, f32[192,896]{1,0:T(8,128)S(1)} %slice.53.shi_ref, ...), custom_call_target="tpu_custom_call", output_to_operand_aliasing={{}: (7, {})} | custom-call | flops 4337958912 | bytes 9781248 | tf_op jit(solution)/shard_map/pallas_call | solution.py:72
  80.0 1.4 %copy-done.1 = bf16[64,12288]{1,0:T(8,128)(2,1)S(1)} copy-done((bf16[64,12288]{1,0:T(8,128)(2,1)S(1)}, bf16[64,12288]{1,0:T(8,128)(2,1)}, u32[]{:S(2)}) %copy-start.1) | copy-done | bytes 1572888
  81.4 12.5 %shard_map.65 = f32[96,1792]{1,0:T(8,128)S(1)} custom-call(bf16[192,64]{1,0:T(8,128)(2,1)S(1)} %add_convert_fusion.pick_ref, bf16[64,12288]{1,0:T(8,128)(2,1)S(1)} %copy-done.1, bf16[64,12288]{1,0:T(8,128)(2,1)S(1)} %copy-done.1, f32[96,896]{1,0:T(8,128)S(1)} %slice.54.chi_ref, f32[96,896]{1,0:T(8,128)S(1)} %slice.55.shi_ref, ...), custom_call_target="tpu_custom_call", output_to_operand_aliasing={{}: (7, {})} | custom-call | flops 2168979456 | bytes 5062656 | tf_op jit(solution)/shard_map/pallas_call | solution.py:72
  94.3 0.6 reverse
  95.4 0.6 fusion.18
  96.0 1.2 reshape.51
  97.2 3.5 %all-to-all-start = ((f32[32,4,1664]{2,1,0:T(4,128)}), f32[32,4,1664]{2,1,0:T(4,128)S(1)}, u32[]{:S(2)}, u32[]{:S(2)}) async-start(f32[32,4,1664]{2,1,0:T(4,128)} %reshape.51), calls=%async_computation | async-start | bytes 1703936 | tf_op jit(solution)/shard_map/all_to_all | solution.py:156
  100.6 23.2 %all-to-all-done = f32[32,4,1664]{2,1,0:T(4,128)S(1)} async-done(((f32[32,4,1664]{2,1,0:T(4,128)}), f32[32,4,1664]{2,1,0:T(4,128)S(1)}, u32[]{:S(2)}, u32[]{:S(2)}) %all-to-all-start) | async-done | bytes 852000 | tf_op jit(solution)/shard_map/all_to_all | solution.py:156
  123.9 0.3 reshape.52
  124.4 1.4 %convolution_add_fusion = f32[96,1601]{1,0:T(8,128)} fusion(f32[96,1601]{1,0:T(8,128)S(1)} %copy-done.3, f32[128,1664]{1,0:T(8,128)S(1)} %reshape.52, f32[128]{0:T(128)S(1)} %slice_reduce_fusion, f32[96]{0:T(128)S(1)} %iota_convert_fusion), kind=kOutput, calls=%fused_computation | convolution fusion | flops 236243040 | bytes 2082432 | tf_op jit(solution)/shard_map/dot_general | solution.py:168
  (49 shorter events, 3.0 us)
Async XLA Ops:
  6.5 46.6 %all-gather.5.cloned.1.call-start = ((), (), s32[]{:S(2)}) async-start(), calls=%async_computation.2 | async-start | bytes 3538944 | tf_op jit(solution)/shard_map/all_gather | solution.py:132
  9.4 1.3 copy-start.2
  12.1 68.0 %all-gather.3.cloned.1.call-start = ((), (), s32[]{:S(2)}) async-start(), calls=%async_computation.1 | async-start | bytes 1769472 | tf_op jit(solution)/shard_map/all_gather | solution.py:132
  18.6 0.7 copy-start.6
  18.7 0.8 copy-start.4
  18.7 1.0 copy-start.5
  18.7 2.2 %copy-start.7 = (s32[96]{0:T(128)S(1)}, s32[96]{0:T(128)}, u32[]{:S(2)}) copy-start(s32[96]{0:T(128)} %param.9) | copy-start | bytes 1156
  53.2 1.9 %copy-start = (bf16[64,24576]{1,0:T(8,128)(2,1)S(1)}, bf16[64,24576]{1,0:T(8,128)(2,1)}, u32[]{:S(2)}) copy-start(bf16[64,24576]{1,0:T(8,128)(2,1)} %all-gather.5.cloned.1.call-done.g0_ref.g1_ref) | copy-start | bytes 9437188
  80.0 1.4 %copy-start.1 = (bf16[64,12288]{1,0:T(8,128)(2,1)S(1)}, bf16[64,12288]{1,0:T(8,128)(2,1)}, u32[]{:S(2)}) copy-start(bf16[64,12288]{1,0:T(8,128)(2,1)} %all-gather.3.cloned.1.call-done.g0_ref.g1_ref) | copy-start | bytes 4718596
  97.2 26.7 %all-to-all-start = ((f32[32,4,1664]{2,1,0:T(4,128)}), f32[32,4,1664]{2,1,0:T(4,128)S(1)}, u32[]{:S(2)}, u32[]{:S(2)}) async-start(f32[32,4,1664]{2,1,0:T(4,128)} %reshape.51), calls=%async_computation | async-start | bytes 1703936 | tf_op jit(solution)/shard_map/all_to_all | solution.py:156
  100.6 23.7 %copy-start.3 = (f32[96,1601]{1,0:T(8,128)S(1)}, f32[96,1601]{1,0:T(8,128)}, u32[]{:S(2)}) copy-start(f32[96,1601]{1,0:T(8,128)} %param.7) | copy-start | bytes 1844356
Sparse Core Ops, SparseCore 0:
  12.2 40.9 all-gather.4
  54.8 24.1 all-gather.2

commit v12 on v11

--- a/solution.py
+++ b/solution.py
@@ -58,6 +58,100 @@
     half = ctab.shape[1]
     out_ref[:, :half] += jnp.dot(real, ctab[...], preferred_element_type=jnp.float32)
     out_ref[:, half:] += jnp.dot(imag, stab[...], preferred_element_type=jnp.float32)
+
+
+def fill_kernel(chi_ref, shi_ref, clo_ref, slo_ref, ctab, stab):
+    def fill(j, carry):
+        clo = clo_ref[...]
+        slo = slo_ref[...]
+        ch = chi_ref[pl.ds(j, 1), :]
+        sh = shi_ref[pl.ds(j, 1), :]
+        rows = pl.ds(pl.multiple_of(j * LOW, LOW), LOW)
+        ctab[rows, :] = (ch * clo - sh * slo).astype(jnp.bfloat16)
+        stab[rows, :] = (sh * clo + ch * slo).astype(jnp.bfloat16)
+        return carry
+
+    lax.fori_loop(0, FBLOCK // LOW, fill, 0)
+
+
+def stored_kernel(pick_ref, g0_ref, g1_ref, ctab, stab, acc_ref, out_ref):
+    @pl.when(pl.program_id(0) == 0)
+    def _():
+        out_ref[...] = acc_ref[...]
+
+    pairs = out_ref.shape[0]
+    picks = pick_ref[...]
+    rows0 = jnp.dot(picks, g0_ref[...], preferred_element_type=jnp.float32)
+    rows1 = jnp.dot(picks, g1_ref[...], preferred_element_type=jnp.float32)
+    a0 = rows0[:pairs]
+    b0 = rows0[pairs:]
+    a1 = rows1[:pairs]
+    b1 = rows1[pairs:]
+    real = (a0 * b0 + a1 * b1).astype(jnp.bfloat16)
+    imag = (a1 * b0 - a0 * b1).astype(jnp.bfloat16)
+    half = ctab.shape[1]
+    out_ref[:, :half] += jnp.dot(real, ctab[...], preferred_element_type=jnp.float32)
+    out_ref[:, half:] += jnp.dot(imag, stab[...], preferred_element_type=jnp.float32)
+
+
+def fill_tables(tables):
+    cos_hi, sin_hi, cos_lo, sin_lo = tables
+    lag_pad = cos_lo.shape[1]
+    hi_rows = FBLOCK // LOW
+    width = cos_hi.shape[0] * LOW
+    blocks = width // FBLOCK
+    spec = pl.BlockSpec((FBLOCK, lag_pad), lambda i: (i, 0))
+    return pl.pallas_call(
+        fill_kernel,
+        grid=(blocks,),
+        in_specs=[
+            pl.BlockSpec((hi_rows, lag_pad), lambda i: (i, 0)),
+            pl.BlockSpec((hi_rows, lag_pad), lambda i: (i, 0)),
+            pl.BlockSpec((LOW, lag_pad), lambda i: (0, 0)),
+            pl.BlockSpec((LOW, lag_pad), lambda i: (0, 0)),
+        ],
+        out_specs=[spec, spec],
+        out_shape=[jax.ShapeDtypeStruct((width, lag_pad), jnp.bfloat16)] * 2,
+        compiler_params=pltpu.CompilerParams(
+            dimension_semantics=("arbitrary",), vmem_limit_bytes=48 * 1024 * 1024
+        ),
+        cost_estimate=pl.CostEstimate(
+            flops=10 * width * lag_pad, transcendentals=0, bytes_accessed=4 * width * lag_pad
+        ),
+    )(cos_hi, sin_hi, cos_lo, sin_lo)
+
+
+def correlate_stored(picks, flat, stored, acc):
+    ctab, stab = stored
+    pair_count = picks.shape[0] // 2
+    group_sta = flat.shape[0]
+    lag_pad = ctab.shape[1]
+    width = flat.shape[1] // 2
+    assert width % FBLOCK == 0 and ctab.shape[0] == width
+    blocks = width // FBLOCK
+    return pl.pallas_call(
+        stored_kernel,
+        grid=(blocks,),
+        in_specs=[
+            pl.BlockSpec((2 * pair_count, group_sta), lambda i: (0, 0)),
+            pl.BlockSpec((group_sta, FBLOCK), lambda i: (0, i)),
+            pl.BlockSpec((group_sta, FBLOCK), lambda i: (0, i + blocks)),
+            pl.BlockSpec((FBLOCK, lag_pad), lambda i: (i, 0)),
+            pl.BlockSpec((FBLOCK, lag_pad), lambda i: (i, 0)),
+            pl.BlockSpec((pair_count, 2 * lag_pad), lambda i: (0, 0)),
+        ],
+        out_specs=pl.BlockSpec((pair_count, 2 * lag_pad), lambda i: (0, 0)),
+        out_shape=jax.ShapeDtypeStruct((pair_count, 2 * lag_pad), jnp.float32),
+        compiler_params=pltpu.CompilerParams(
+            dimension_semantics=("arbitrary",), vmem_limit_bytes=48 * 1024 * 1024
+        ),
+        cost_estimate=pl.CostEstimate(
+            flops=2 * 2 * pair_count * width * lag_pad,
+            transcendentals=0,
+            bytes_accessed=4 * width * lag_pad + 4 * pair_count * lag_pad,
+        ),
+        input_output_aliases={5: 0},
+    )(picks, flat, flat, ctab, stab, acc)
 
 
 def correlate(picks, flat, tables, acc):
@@ -122,9 +216,11 @@
     lo_all = angle_table(lax.iota(jnp.int32, LOW), lag_pad, total_bins)
     blocks = total_bins // FBLOCK
     assert total_bins % FBLOCK == 0
-    lead = max(1, min(blocks - 1, (2 * blocks + 1) // 3))
+    lead = max(1, min(blocks - 1, (7 * blocks + 4) // 9))
     bounds = [0, lead * FBLOCK, total_bins] if blocks > 1 else [0, total_bins]
     corr = jnp.zeros((pair_count, 2 * lag_pad), jnp.float32)
+    lead_rows = slice(0, bounds[1] // LOW)
+    stored = fill_tables((hi_all[0][lead_rows], hi_all[1][lead_rows], lo_all[0], lo_all[1]))
     for c in range(len(bounds) - 1):
         begin, end = bounds[c], bounds[c + 1]
         width = end - begin
@@ -134,7 +230,10 @@
             flat, corr = lax.optimization_barrier((flat, corr))
         rows = slice(begin // LOW, end // LOW)
         tables = (hi_all[0][rows], hi_all[1][rows], lo_all[0], lo_all[1])
-        corr = correlate(picks, flat, tables, corr)
+        if c == 0:
+            corr = correlate_stored(picks, flat, stored, corr)
+        else:
+            corr = correlate(picks, flat, tables, corr)
     even = corr[:, : side + 1]
     odd = corr[:, lag_pad : lag_pad + side + 1]
     corr = jnp.concatenate([(even + odd)[:, :0:-1], even - odd], axis=1)

time: 133 us -> 130 us (0.977)
  waiting for transfers between devices: 55.5 us -> 39.9 us
  Pallas kernels: 37.4 us -> 49.8 us
    pallas_call x0 -> x2, Pallas kernels: none -> 41.5 us  [the longest x1 21.1 us: fill_tables(): pl.pallas_call(fill_kernel, grid=(blocks,), in_specs=[pl.BlockSpec((hi_ro...]
    pallas_call x2 -> x1, Pallas kernels: 37.4 us -> 8.39 us  [correlate(): pl.pallas_call(table_kernel, grid=(blocks,), in_specs=[pl.BlockSpec((2 *...]
    all_gather x2, waiting for transfers between devices: 32.2 us -> 16.6 us  [local(): flat = lax.all_gather(piece, 'sta', axis=0, tiled=True)]
  transfers between devices with their start and end apart: 3 -> 3, of which waited for: 2 -> 3; matrix products, arithmetic and copies ran while one was open for 6% -> 6% of each run, Pallas kernels for 19% -> 32%
where the time goes in v12:
time: 130 us; the launch traced here: 129 us
  Pallas kernels  49.8 us (38%)
  waiting for transfers between devices  39.9 us (31%)
  between operations  13.7 us (11%)
  other arithmetic  10 us (8%)
  local copies, waits for them, and re-layouts  9.65 us (7%)
  starting transfers between devices  4.24 us (3%)
  matrix products  1.97 us (2%)
    all_to_all x1, waiting for transfers between devices, local(): lax.all_to_all(send_rows.reshape(devices, capacity, corr.shape[1]), ('grp...  23.2 us
    pallas_call x1, Pallas kernels, fill_tables(): pl.pallas_call(fill_kernel, grid=(blocks,), in_specs=[pl.BlockSpec((hi_ro...  21.1 us
    pallas_call x1, Pallas kernels, correlate_stored(): pl.pallas_call(stored_kernel, grid=(blocks,), in_specs=[pl.BlockSpec((2 *...  20.4 us
    all_gather x2, waiting for transfers between devices, local(): flat = lax.all_gather(piece, 'sta', axis=0, tiled=True)  16.6 us
    pallas_call x1, Pallas kernels, correlate(): pl.pallas_call(table_kernel, grid=(blocks,), in_specs=[pl.BlockSpec((2 *...  8.39 us
    unnamed x20, local copies, waits for them, and re-layouts  6.3 us
    sin x2, other arithmetic, angle_table(): return (jnp.cos(theta), jnp.sin(theta))  5.17 us
    all_to_all x1, starting transfers between devices, local(): lax.all_to_all(send_rows.reshape(devices, capacity, corr.shape[1]), ('grp...  4.2 us
  transfers between devices with their start and end apart: 3, of which 3 were waited for; matrix products, arithmetic and copies ran while one was open for 6% of the time, Pallas kernels for 32%

profile of v12, /device:TPU:0, one launch (start us, length us, event | category | flops | bytes accessed | tf_op | source)
XLA Modules:
  0.0 129.3 jit_solution(1655839180946170706)
XLA Ops:
  6.5 2.4 %multiply_reduce_fusion = f32[8,14336]{1,0:T(8,128)S(1)} fusion(f32[8,2,18432]{2,1,0:T(2,128)} %param.6), kind=kLoop, calls=%fused_computation.11 | loop fusion | flops 344064 | bytes 1376256 | tf_op jit(solution)/shard_map/reduce_sum | solution.py:16
  8.9 0.4 reduce_sum.49
  9.3 0.3 reduce_sum.50
  9.7 0.3 mul.169
  10.0 0.3 mul.170
  10.3 0.6 copy-done.2
  10.9 0.5 fusion.8
  11.4 0.9 copy.15
  12.4 0.3 multiply_reduce_fusion.1
  13.4 0.7 copy.14
  14.2 4.2 %fusion.4 = (f32[288,896]{1,0:T(8,128)S(1)}, f32[288,896]{1,0:T(8,128)S(1)}) fusion(s32[288]{0:T(512)S(1)} %iota_multiply_fusion), kind=kLoop, calls=%fused_computation.7 | loop fusion | flops 2322432 | bytes 2065536 | tf_op jit(solution)/shard_map/sin | solution.py:24
  18.9 0.9 fusion.13
  19.9 21.1 %shard_map.64 = (bf16[14336,896]{1,0:T(8,128)(2,1)}, bf16[14336,896]{1,0:T(8,128)(2,1)}) custom-call(f32[224,896]{1,0:T(8,128)S(1)} %slice.52.chi_ref, f32[224,896]{1,0:T(8,128)S(1)} %slice.53.shi_ref, f32[64,896]{1,0:T(8,128)S(1)} %get-tuple-element.23.clo_ref, f32[64,896]{1,0:T(8,128)S(1)} %get-tuple-element.22.slo_ref), custom_call_target="tpu_custom_call" | custom-call | flops 128450560 | bytes 51380224 | tf_op jit(solution)/shard_map/pallas_call | solution.py:104
  41.3 16.4 %all-gather.5.cloned.1.call-done.g0_ref.g1_ref = bf16[64,28672]{1,0:T(8,128)(2,1)} async-done(((bf16[8,28672]{1,0:T(8,128)(2,1)}), bf16[64,28672]{1,0:T(8,128)(2,1)}) %all-gather.5.cloned.1.call-update) | async-done | bytes 3670032 | tf_op jit(solution)/shard_map/all_gather | solution.py:228
  57.8 2.0 %copy-done = bf16[64,28672]{1,0:T(8,128)(2,1)S(1)} copy-done((bf16[64,28672]{1,0:T(8,128)(2,1)S(1)}, bf16[64,28672]{1,0:T(8,128)(2,1)}, u32[]{:S(2)}) %copy-start) | copy-done | bytes 3670040
  59.8 20.4 %shard_map.65.acc_ref = f32[96,1792]{1,0:T(8,128)S(1)} custom-call(bf16[192,64]{1,0:T(8,128)(2,1)S(1)} %add_convert_fusion.pick_ref, bf16[64,28672]{1,0:T(8,128)(2,1)S(1)} %copy-done, bf16[64,28672]{1,0:T(8,128)(2,1)S(1)} %copy-done, bf16[14336,896]{1,0:T(8,128)(2,1)} %get-tuple-element.9.ctab, ...), custom_call_target="tpu_custom_call", output_to_operand_aliasing={{}: (5, {})} | custom-call | flops 4932501504 | bytes 51724288 | tf_op jit(solution)/shard_map/pallas_call | solution.py:132
  80.4 1.2 copy-done.1
  81.6 8.4 %shard_map.66 = f32[96,1792]{1,0:T(8,128)S(1)} custom-call(bf16[192,64]{1,0:T(8,128)(2,1)S(1)} %add_convert_fusion.pick_ref, bf16[64,8192]{1,0:T(8,128)(2,1)S(1)} %copy-done.1, bf16[64,8192]{1,0:T(8,128)(2,1)S(1)} %copy-done.1, f32[64,896]{1,0:T(8,128)S(1)} %slice.54.chi_ref, f32[64,896]{1,0:T(8,128)S(1)} %slice.55.shi_ref, ...), custom_call_target="tpu_custom_call", output_to_operand_aliasing={{}: (7, {})} | custom-call | flops 1445986304 | bytes 3489792 | tf_op jit(solution)/shard_map/pallas_call | solution.py:166
  90.4 0.6 reverse
  91.4 0.6 fusion.18
  92.0 1.2 reshape.51
  93.2 4.2 %all-to-all-start = ((f32[32,4,1664]{2,1,0:T(4,128)}), f32[32,4,1664]{2,1,0:T(4,128)S(1)}, u32[]{:S(2)}, u32[]{:S(2)}) async-start(f32[32,4,1664]{2,1,0:T(4,128)} %reshape.51), calls=%async_computation | async-start | bytes 1703936 | tf_op jit(solution)/shard_map/all_to_all | solution.py:255
  97.4 23.2 %all-to-all-done = f32[32,4,1664]{2,1,0:T(4,128)S(1)} async-done(((f32[32,4,1664]{2,1,0:T(4,128)}), f32[32,4,1664]{2,1,0:T(4,128)S(1)}, u32[]{:S(2)}, u32[]{:S(2)}) %all-to-all-start) | async-done | bytes 852000 | tf_op jit(solution)/shard_map/all_to_all | solution.py:255
  121.2 1.4 %convolution_add_fusion = f32[96,1601]{1,0:T(8,128)} fusion(f32[96,1601]{1,0:T(8,128)S(1)} %copy-done.3, f32[128,1664]{1,0:T(8,128)S(1)} %reshape.52, f32[128]{0:T(128)S(1)} %slice_reduce_fusion, f32[96]{0:T(128)S(1)} %iota_convert_fusion), kind=kOutput, calls=%fused_computation | convolution fusion | flops 236243040 | bytes 2082432 | tf_op jit(solution)/shard_map/dot_general | solution.py:267
  (50 shorter events, 3.0 us)
Async XLA Ops:
  6.5 51.2 %all-gather.5.cloned.1.call-start = ((), (), s32[]{:S(2)}) async-start(), calls=%async_computation.2 | async-start | bytes 4128768 | tf_op jit(solution)/shard_map/all_gather | solution.py:228
  9.6 1.3 copy-start.2
  12.3 68.1 %all-gather.3.cloned.1.call-start = ((), (), s32[]{:S(2)}) async-start(), calls=%async_computation.1 | async-start | bytes 1179648 | tf_op jit(solution)/shard_map/all_gather | solution.py:228
  13.4 5.0 %copy-start.4 = (s32[96,1]{0,1:T(1,128)S(1)}, s32[96,1]{0,1:T(1,128)}, u32[]{:S(2)}) copy-start(s32[96,1]{0,1:T(1,128)} %param.10) | copy-start | bytes 1156
  14.1 4.4 %copy-start.6 = (s32[96]{0:T(128)S(1)}, s32[96]{0:T(128)}, u32[]{:S(2)}) copy-start(s32[96]{0:T(128)} %param.11) | copy-start | bytes 1156
  18.9 22.0 %copy-start.5 = (s32[2,96]{1,0:T(2,128)S(1)}, s32[2,96]{1,0:T(2,128)}, u32[]{:S(2)}) copy-start(s32[2,96]{1,0:T(2,128)} %param.8) | copy-start | bytes 2308
  19.9 21.4 %copy-start.7 = (s32[96]{0:T(128)S(1)}, s32[96]{0:T(128)}, u32[]{:S(2)}) copy-start(s32[96]{0:T(128)} %param.9) | copy-start | bytes 1156
  57.8 2.0 %copy-start = (bf16[64,28672]{1,0:T(8,128)(2,1)S(1)}, bf16[64,28672]{1,0:T(8,128)(2,1)}, u32[]{:S(2)}) copy-start(bf16[64,28672]{1,0:T(8,128)(2,1)} %all-gather.5.cloned.1.call-done.g0_ref.g1_ref) | copy-start | bytes 11010052
  80.4 1.2 copy-start.1
  93.2 27.5 %all-to-all-start = ((f32[32,4,1664]{2,1,0:T(4,128)}), f32[32,4,1664]{2,1,0:T(4,128)S(1)}, u32[]{:S(2)}, u32[]{:S(2)}) async-start(f32[32,4,1664]{2,1,0:T(4,128)} %reshape.51), calls=%async_computation | async-start | bytes 1703936 | tf_op jit(solution)/shard_map/all_to_all | solution.py:255
  97.4 23.7 %copy-start.3 = (f32[96,1601]{1,0:T(8,128)S(1)}, f32[96,1601]{1,0:T(8,128)}, u32[]{:S(2)}) copy-start(f32[96,1601]{1,0:T(8,128)} %param.7) | copy-start | bytes 1844356
Sparse Core Ops, SparseCore 0:
  12.4 45.2 all-gather.4
  59.3 21.0 all-gather.2

commit v13 on v12

--- a/solution.py
+++ b/solution.py
@@ -121,14 +121,15 @@
     )(cos_hi, sin_hi, cos_lo, sin_lo)
 
 
-def correlate_stored(picks, flat, stored, acc):
+def correlate_stored(picks, flat, stored, acc, begin):
     ctab, stab = stored
     pair_count = picks.shape[0] // 2
     group_sta = flat.shape[0]
     lag_pad = ctab.shape[1]
     width = flat.shape[1] // 2
-    assert width % FBLOCK == 0 and ctab.shape[0] == width
+    assert width % FBLOCK == 0 and begin % FBLOCK == 0
     blocks = width // FBLOCK
+    skip = begin // FBLOCK
     return pl.pallas_call(
         stored_kernel,
         grid=(blocks,),
@@ -136,8 +137,8 @@
             pl.BlockSpec((2 * pair_count, group_sta), lambda i: (0, 0)),
             pl.BlockSpec((group_sta, FBLOCK), lambda i: (0, i)),
             pl.BlockSpec((group_sta, FBLOCK), lambda i: (0, i + blocks)),
-            pl.BlockSpec((FBLOCK, lag_pad), lambda i: (i, 0)),
-            pl.BlockSpec((FBLOCK, lag_pad), lambda i: (i, 0)),
+            pl.BlockSpec((FBLOCK, lag_pad), lambda i: (i + skip, 0)),
+            pl.BlockSpec((FBLOCK, lag_pad), lambda i: (i + skip, 0)),
             pl.BlockSpec((pair_count, 2 * lag_pad), lambda i: (0, 0)),
         ],
         out_specs=pl.BlockSpec((pair_count, 2 * lag_pad), lambda i: (0, 0)),
@@ -219,8 +220,7 @@
     lead = max(1, min(blocks - 1, (7 * blocks + 4) // 9))
     bounds = [0, lead * FBLOCK, total_bins] if blocks > 1 else [0, total_bins]
     corr = jnp.zeros((pair_count, 2 * lag_pad), jnp.float32)
-    lead_rows = slice(0, bounds[1] // LOW)
-    stored = fill_tables((hi_all[0][lead_rows], hi_all[1][lead_rows], lo_all[0], lo_all[1]))
+    stored = fill_tables((hi_all[0], hi_all[1], lo_all[0], lo_all[1]))
     for c in range(len(bounds) - 1):
         begin, end = bounds[c], bounds[c + 1]
         width = end - begin
@@ -228,12 +228,7 @@
         flat = lax.all_gather(piece, "sta", axis=0, tiled=True)
         if c:
             flat, corr = lax.optimization_barrier((flat, corr))
-        rows = slice(begin // LOW, end // LOW)
-        tables = (hi_all[0][rows], hi_all[1][rows], lo_all[0], lo_all[1])
-        if c == 0:
-            corr = correlate_stored(picks, flat, stored, corr)
-        else:
-            corr = correlate(picks, flat, tables, corr)
+        corr = correlate_stored(picks, flat, stored, corr, begin)
     even = corr[:, : side + 1]
     odd = corr[:, lag_pad : lag_pad + side + 1]
     corr = jnp.concatenate([(even + odd)[:, :0:-1], even - odd], axis=1)

time: 130 us -> 129 us (level)
  waiting for transfers between devices: 39.9 us -> 35 us
  Pallas kernels: 49.8 us -> 53.5 us
    pallas_call x1 -> x0, Pallas kernels: 8.39 us -> none  [correlate(): pl.pallas_call(table_kernel, grid=(blocks,), in_specs=[pl.BlockSpec((2 *...]
    pallas_call x1 -> x2, Pallas kernels: 20.4 us -> 27.5 us  [correlate_stored(): pl.pallas_call(stored_kernel, grid=(blocks,), in_specs=[pl.BlockSpec((2 *...]
    all_gather x2, waiting for transfers between devices: 16.6 us -> 11.7 us  [local(): flat = lax.all_gather(piece, 'sta', axis=0, tiled=True)]
    pallas_call x1, Pallas kernels: 21.1 us -> 26 us  [fill_tables(): pl.pallas_call(fill_kernel, grid=(blocks,), in_specs=[pl.BlockSpec((hi_ro...]
  transfers between devices with their start and end apart: 3 -> 3, of which waited for: 3 -> 3; matrix products, arithmetic and copies ran while one was open for 6% -> 6% of each run, Pallas kernels for 32% -> 36%
where the time goes in v13:
time: 129 us; the launch traced here: 128 us
  Pallas kernels  53.5 us (41%)
  waiting for transfers between devices  35 us (27%)
  between operations  13.7 us (11%)
  other arithmetic  10 us (8%)
  local copies, waits for them, and re-layouts  9.51 us (7%)
  starting transfers between devices  4.55 us (4%)
  matrix products  1.97 us (2%)
    pallas_call x2, Pallas kernels, correlate_stored(): pl.pallas_call(stored_kernel, grid=(blocks,), in_specs=[pl.BlockSpec((2 *...  27.5 us
    pallas_call x1, Pallas kernels, fill_tables(): pl.pallas_call(fill_kernel, grid=(blocks,), in_specs=[pl.BlockSpec((hi_ro...  26 us
    all_to_all x1, waiting for transfers between devices, local(): lax.all_to_all(send_rows.reshape(devices, capacity, corr.shape[1]), ('grp...  23.2 us
    all_gather x2, waiting for transfers between devices, local(): flat = lax.all_gather(piece, 'sta', axis=0, tiled=True)  11.7 us
    unnamed x20, local copies, waits for them, and re-layouts  6.29 us
    sin x2, other arithmetic, angle_table(): return (jnp.cos(theta), jnp.sin(theta))  5.17 us
    all_to_all x1, starting transfers between devices, local(): lax.all_to_all(send_rows.reshape(devices, capacity, corr.shape[1]), ('grp...  4.32 us
    reduce_sum x4, other arithmetic, whiten(): power = jnp.mean(split * split, axis=(1, 3), keepdims=True)  3.19 us
  transfers between devices with their start and end apart: 3, of which 3 were waited for; matrix products, arithmetic and copies ran while one was open for 6% of the time, Pallas kernels for 36%

profile of v13, /device:TPU:0, one launch (start us, length us, event | category | flops | bytes accessed | tf_op | source)
XLA Modules:
  0.0 128.2 jit_solution(1870199416804860808)
XLA Ops:
  6.5 2.4 %multiply_reduce_fusion = f32[8,14336]{1,0:T(8,128)S(1)} fusion(f32[8,2,18432]{2,1,0:T(2,128)} %param.6), kind=kLoop, calls=%fused_computation.11 | loop fusion | flops 344064 | bytes 1376256 | tf_op jit(solution)/shard_map/reduce_sum | solution.py:16
  8.9 0.4 reduce_sum.49
  9.3 0.3 reduce_sum.50
  9.7 0.3 mul.133
  10.0 0.3 mul.134
  10.3 0.6 copy-done.2
  10.9 0.5 fusion.8
  11.4 0.9 copy.15
  12.5 0.3 multiply_reduce_fusion.1
  13.6 0.7 copy.14
  14.3 0.9 fusion.13
  15.6 4.2 %fusion.4 = (f32[288,896]{1,0:T(8,128)S(1)}, f32[288,896]{1,0:T(8,128)S(1)}) fusion(s32[288]{0:T(512)S(1)} %iota_multiply_fusion), kind=kLoop, calls=%fused_computation.7 | loop fusion | flops 2322432 | bytes 2065536 | tf_op jit(solution)/shard_map/sin | solution.py:24
  19.9 26.0 %shard_map.64 = (bf16[18432,896]{1,0:T(8,128)(2,1)}, bf16[18432,896]{1,0:T(8,128)(2,1)}) custom-call(f32[288,896]{1,0:T(8,128)S(1)} %get-tuple-element.17.chi_ref, f32[288,896]{1,0:T(8,128)S(1)} %get-tuple-element.16.shi_ref, f32[64,896]{1,0:T(8,128)S(1)} %get-tuple-element.23.clo_ref, f32[64,896]{1,0:T(8,128)S(1)} %get-tuple-element.22.slo_ref), custom_call_target="tpu_custom_call" | custom-call | flops 165150720 | bytes 66060288 | tf_op jit(solution)/shard_map/pallas_call | solution.py:104
  46.2 11.5 %all-gather.5.cloned.1.call-done.g0_ref.g1_ref = bf16[64,28672]{1,0:T(8,128)(2,1)} async-done(((bf16[8,28672]{1,0:T(8,128)(2,1)}), bf16[64,28672]{1,0:T(8,128)(2,1)}) %all-gather.5.cloned.1.call-update) | async-done | bytes 3670032 | tf_op jit(solution)/shard_map/all_gather | solution.py:228
  57.8 2.0 %copy-done = bf16[64,28672]{1,0:T(8,128)(2,1)S(1)} copy-done((bf16[64,28672]{1,0:T(8,128)(2,1)S(1)}, bf16[64,28672]{1,0:T(8,128)(2,1)}, u32[]{:S(2)}) %copy-start) | copy-done | bytes 3670040
  59.8 20.4 %shard_map.65.acc_ref = f32[96,1792]{1,0:T(8,128)S(1)} custom-call(bf16[192,64]{1,0:T(8,128)(2,1)S(1)} %add_convert_fusion.pick_ref, bf16[64,28672]{1,0:T(8,128)(2,1)S(1)} %copy-done, bf16[64,28672]{1,0:T(8,128)(2,1)S(1)} %copy-done, bf16[18432,896]{1,0:T(8,128)(2,1)} %get-tuple-element.9.ctab, ...), custom_call_target="tpu_custom_call", output_to_operand_aliasing={{}: (5, {})} | custom-call | flops 4932501504 | bytes 51724288 | tf_op jit(solution)/shard_map/pallas_call | solution.py:133
  80.4 1.2 copy-done.1
  81.6 7.1 %shard_map.66 = f32[96,1792]{1,0:T(8,128)S(1)} custom-call(bf16[192,64]{1,0:T(8,128)(2,1)S(1)} %add_convert_fusion.pick_ref, bf16[64,8192]{1,0:T(8,128)(2,1)S(1)} %copy-done.1, bf16[64,8192]{1,0:T(8,128)(2,1)S(1)} %copy-done.1, bf16[18432,896]{1,0:T(8,128)(2,1)} %get-tuple-element.9.ctab, ...), custom_call_target="tpu_custom_call", output_to_operand_aliasing={{}: (5, {})} | custom-call | flops 1409286144 | bytes 15024128 | tf_op jit(solution)/shard_map/pallas_call | solution.py:133
  89.1 0.6 reverse
  90.2 0.6 fusion.18
  90.8 1.2 reshape.51
  91.9 4.3 %all-to-all-start = ((f32[32,4,1664]{2,1,0:T(4,128)}), f32[32,4,1664]{2,1,0:T(4,128)S(1)}, u32[]{:S(2)}, u32[]{:S(2)}) async-start(f32[32,4,1664]{2,1,0:T(4,128)} %reshape.51), calls=%async_computation | async-start | bytes 1703936 | tf_op jit(solution)/shard_map/all_to_all | solution.py:250
  96.3 23.2 %all-to-all-done = f32[32,4,1664]{2,1,0:T(4,128)S(1)} async-done(((f32[32,4,1664]{2,1,0:T(4,128)}), f32[32,4,1664]{2,1,0:T(4,128)S(1)}, u32[]{:S(2)}, u32[]{:S(2)}) %all-to-all-start) | async-done | bytes 852000 | tf_op jit(solution)/shard_map/all_to_all | solution.py:250
  120.0 1.4 %convolution_add_fusion = f32[96,1601]{1,0:T(8,128)} fusion(f32[96,1601]{1,0:T(8,128)S(1)} %copy-done.3, f32[128,1664]{1,0:T(8,128)S(1)} %reshape.52, f32[128]{0:T(128)S(1)} %slice_reduce_fusion, f32[96]{0:T(128)S(1)} %iota_convert_fusion), kind=kOutput, calls=%fused_computation | convolution fusion | flops 236243040 | bytes 2082432 | tf_op jit(solution)/shard_map/dot_general | solution.py:262
  (46 shorter events, 3.0 us)
Async XLA Ops:
  6.5 51.2 %all-gather.5.cloned.1.call-start = ((), (), s32[]{:S(2)}) async-start(), calls=%async_computation.2 | async-start | bytes 4128768 | tf_op jit(solution)/shard_map/all_gather | solution.py:228
  9.6 1.3 copy-start.2
  12.3 68.1 %all-gather.3.cloned.1.call-start = ((), (), s32[]{:S(2)}) async-start(), calls=%async_computation.1 | async-start | bytes 1179648 | tf_op jit(solution)/shard_map/all_gather | solution.py:228
  13.0 2.3 %copy-start.6 = (s32[96]{0:T(128)S(1)}, s32[96]{0:T(128)}, u32[]{:S(2)}) copy-start(s32[96]{0:T(128)} %param.11) | copy-start | bytes 1156
  13.0 2.4 %copy-start.4 = (s32[96,1]{0,1:T(1,128)S(1)}, s32[96,1]{0,1:T(1,128)}, u32[]{:S(2)}) copy-start(s32[96,1]{0,1:T(1,128)} %param.10) | copy-start | bytes 1156
  19.9 26.0 %copy-start.5 = (s32[2,96]{1,0:T(2,128)S(1)}, s32[2,96]{1,0:T(2,128)}, u32[]{:S(2)}) copy-start(s32[2,96]{1,0:T(2,128)} %param.8) | copy-start | bytes 2308
  19.9 26.3 %copy-start.7 = (s32[96]{0:T(128)S(1)}, s32[96]{0:T(128)}, u32[]{:S(2)}) copy-start(s32[96]{0:T(128)} %param.9) | copy-start | bytes 1156
  57.8 2.0 %copy-start = (bf16[64,28672]{1,0:T(8,128)(2,1)S(1)}, bf16[64,28672]{1,0:T(8,128)(2,1)}, u32[]{:S(2)}) copy-start(bf16[64,28672]{1,0:T(8,128)(2,1)} %all-gather.5.cloned.1.call-done.g0_ref.g1_ref) | copy-start | bytes 11010052
  80.4 1.2 copy-start.1
  91.9 27.6 %all-to-all-start = ((f32[32,4,1664]{2,1,0:T(4,128)}), f32[32,4,1664]{2,1,0:T(4,128)S(1)}, u32[]{:S(2)}, u32[]{:S(2)}) async-start(f32[32,4,1664]{2,1,0:T(4,128)} %reshape.51), calls=%async_computation | async-start | bytes 1703936 | tf_op jit(solution)/shard_map/all_to_all | solution.py:250
  96.3 23.7 %copy-start.3 = (f32[96,1601]{1,0:T(8,128)S(1)}, f32[96,1601]{1,0:T(8,128)}, u32[]{:S(2)}) copy-start(f32[96,1601]{1,0:T(8,128)} %param.7) | copy-start | bytes 1844356
Sparse Core Ops, SparseCore 0:
  12.4 45.2 all-gather.4
  59.3 21.0 all-gather.2

commit v14 on v13

--- a/solution.py
+++ b/solution.py
@@ -248,7 +248,7 @@
     )
     send_rows = jnp.dot(placing.T, corr, precision=lax.Precision.HIGHEST)
     got = lax.all_to_all(
-        send_rows.reshape(devices, capacity, corr.shape[1]),
+        send_rows.reshape(devices, capacity * corr.shape[1]),
         ("grp", "sta"),
         split_axis=0,
         concat_axis=0,

time: 129 us -> 132 us (1.023)
  other arithmetic: 10 us -> 12 us
    all_to_all x0 -> x1, other arithmetic: none -> 2.02 us  [local(): lax.all_to_all(send_rows.reshape(devices, capacity * corr.shape[1]), ('gr...]
    all_to_all x0 -> x1, local copies, waits for them, and re-layouts: none -> 1.75 us  [local(): lax.all_to_all(send_rows.reshape(devices, capacity * corr.shape[1]), ('gr...]
  transfers between devices with their start and end apart: 3 -> 3, of which waited for: 3 -> 3; matrix products, arithmetic and copies ran while one was open for 6% -> 6% of each run, Pallas kernels for 36% -> 35%
where the time goes in v14:
time: 132 us; the launch traced here: 131 us
  Pallas kernels  53.7 us (41%)
  waiting for transfers between devices  35 us (27%)
  between operations  13.7 us (10%)
  other arithmetic  12 us (9%)
  local copies, waits for them, and re-layouts  10.7 us (8%)
  starting transfers between devices  4.24 us (3%)
  matrix products  1.96 us (1%)
    pallas_call x2, Pallas kernels, correlate_stored(): pl.pallas_call(stored_kernel, grid=(blocks,), in_specs=[pl.BlockSpec((2 *...  27.5 us
    pallas_call x1, Pallas kernels, fill_tables(): pl.pallas_call(fill_kernel, grid=(blocks,), in_specs=[pl.BlockSpec((hi_ro...  26.2 us
    all_to_all x1, waiting for transfers between devices, local(): lax.all_to_all(send_rows.reshape(devices, capacity * corr.shape[1]), ('gr...  23.2 us
    all_gather x2, waiting for transfers between devices, local(): flat = lax.all_gather(piece, 'sta', axis=0, tiled=True)  11.7 us
    unnamed x20, local copies, waits for them, and re-layouts  6.94 us
    sin x2, other arithmetic, angle_table(): return (jnp.cos(theta), jnp.sin(theta))  5.17 us
    all_to_all x1, starting transfers between devices, local(): lax.all_to_all(send_rows.reshape(devices, capacity * corr.shape[1]), ('gr...  4.19 us
    reduce_sum x4, other arithmetic, whiten(): power = jnp.mean(split * split, axis=(1, 3), keepdims=True)  3.19 us
  transfers between devices with their start and end apart: 3, of which 3 were waited for; matrix products, arithmetic and copies ran while one was open for 6% of the time, Pallas kernels for 35%

profile of v14, /device:TPU:0, one launch (start us, length us, event | category | flops | bytes accessed | tf_op | source)
XLA Modules:
  0.0 131.3 jit_solution(9759871711056968655)
XLA Ops:
  6.5 2.4 %multiply_reduce_fusion = f32[8,14336]{1,0:T(8,128)S(1)} fusion(f32[8,2,18432]{2,1,0:T(2,128)} %param.6), kind=kLoop, calls=%fused_computation.11 | loop fusion | flops 344064 | bytes 1376256 | tf_op jit(solution)/shard_map/reduce_sum | solution.py:16
  8.9 0.4 reduce_sum.49
  9.3 0.3 reduce_sum.50
  10.3 0.6 copy-done.2
  10.9 0.5 fusion.8
  11.4 0.9 copy.17
  12.4 0.3 multiply_reduce_fusion.1
  13.4 0.7 copy.16
  14.1 0.9 fusion.13
  15.4 4.2 %fusion.4 = (f32[288,896]{1,0:T(8,128)S(1)}, f32[288,896]{1,0:T(8,128)S(1)}) fusion(s32[288]{0:T(512)S(1)} %iota_multiply_fusion), kind=kLoop, calls=%fused_computation.7 | loop fusion | flops 2322432 | bytes 2065536 | tf_op jit(solution)/shard_map/sin | solution.py:24
  19.7 26.2 %shard_map.64 = (bf16[18432,896]{1,0:T(8,128)(2,1)}, bf16[18432,896]{1,0:T(8,128)(2,1)}) custom-call(f32[288,896]{1,0:T(8,128)S(1)} %get-tuple-element.17.chi_ref, f32[288,896]{1,0:T(8,128)S(1)} %get-tuple-element.16.shi_ref, f32[64,896]{1,0:T(8,128)S(1)} %get-tuple-element.23.clo_ref, f32[64,896]{1,0:T(8,128)S(1)} %get-tuple-element.22.slo_ref), custom_call_target="tpu_custom_call" | custom-call | flops 165150720 | bytes 66060288 | tf_op jit(solution)/shard_map/pallas_call | solution.py:104
  46.2 11.5 %all-gather.5.cloned.1.call-done.g0_ref.g1_ref = bf16[64,28672]{1,0:T(8,128)(2,1)} async-done(((bf16[8,28672]{1,0:T(8,128)(2,1)}), bf16[64,28672]{1,0:T(8,128)(2,1)}) %all-gather.5.cloned.1.call-update) | async-done | bytes 3670032 | tf_op jit(solution)/shard_map/all_gather | solution.py:228
  57.8 2.0 %copy-done = bf16[64,28672]{1,0:T(8,128)(2,1)S(1)} copy-done((bf16[64,28672]{1,0:T(8,128)(2,1)S(1)}, bf16[64,28672]{1,0:T(8,128)(2,1)}, u32[]{:S(2)}) %copy-start) | copy-done | bytes 3670040
  59.8 20.4 %shard_map.65.acc_ref = f32[96,1792]{1,0:T(8,128)S(1)} custom-call(bf16[192,64]{1,0:T(8,128)(2,1)S(1)} %add_convert_fusion.pick_ref, bf16[64,28672]{1,0:T(8,128)(2,1)S(1)} %copy-done, bf16[64,28672]{1,0:T(8,128)(2,1)S(1)} %copy-done, bf16[18432,896]{1,0:T(8,128)(2,1)} %get-tuple-element.9.ctab, ...), custom_call_target="tpu_custom_call", output_to_operand_aliasing={{}: (5, {})} | custom-call | flops 4932501504 | bytes 51724288 | tf_op jit(solution)/shard_map/pallas_call | solution.py:133
  80.4 1.2 copy-done.1
  81.6 7.1 %shard_map.66 = f32[96,1792]{1,0:T(8,128)S(1)} custom-call(bf16[192,64]{1,0:T(8,128)(2,1)S(1)} %add_convert_fusion.pick_ref, bf16[64,8192]{1,0:T(8,128)(2,1)S(1)} %copy-done.1, bf16[64,8192]{1,0:T(8,128)(2,1)S(1)} %copy-done.1, bf16[18432,896]{1,0:T(8,128)(2,1)} %get-tuple-element.9.ctab, ...), custom_call_target="tpu_custom_call", output_to_operand_aliasing={{}: (5, {})} | custom-call | flops 1409286144 | bytes 15024128 | tf_op jit(solution)/shard_map/pallas_call | solution.py:133
  89.1 0.6 reverse
  90.2 0.6 fusion.18
  90.8 1.7 %all_to_all.8 = f32[32,1,6656]{2,1,0:T(1,128)} reshape(f32[128,1664]{1,0:T(8,128)S(1)} %fusion.18) | data formatting | bytes 1703936 | tf_op jit(solution)/shard_map/all_to_all | solution.py:250
  92.5 4.2 %all-to-all-start = ((f32[32,1,6656]{2,1,0:T(1,128)}), f32[32,1,6656]{2,1,0:T(1,128)S(1)}, u32[]{:S(2)}, u32[]{:S(2)}) async-start(f32[32,1,6656]{2,1,0:T(1,128)} %all_to_all.8), calls=%async_computation | async-start | bytes 1703936 | tf_op jit(solution)/shard_map/all_to_all | solution.py:250
  96.7 23.2 %all-to-all-done = f32[32,1,6656]{2,1,0:T(1,128)S(1)} async-done(((f32[32,1,6656]{2,1,0:T(1,128)}), f32[32,1,6656]{2,1,0:T(1,128)S(1)}, u32[]{:S(2)}, u32[]{:S(2)}) %all-to-all-start) | async-done | bytes 852000 | tf_op jit(solution)/shard_map/all_to_all | solution.py:250
  120.0 2.0 %reduce.4 = f32[32,6656]{1,0:T(8,128)S(1)} reduce(f32[32,1,6656]{2,1,0:T(1,128)S(1)} %all-to-all-done, f32[]{:T(128)} %constant.45), dimensions={1}, to_apply=%all_to_all.7.reduce_sub_computation | reduce | bytes 1703940 | tf_op jit(solution)/shard_map/all_to_all | solution.py:250
  122.4 0.7 copy-done.3
  123.1 1.3 %convolution_add_fusion = f32[96,1601]{1,0:T(8,128)} fusion(f32[96,1601]{1,0:T(8,128)S(1)} %copy-done.3, f32[128,1664]{1,0:T(8,128)S(1)} %reshape.53, f32[128]{0:T(128)S(1)} %slice_reduce_fusion, f32[96]{0:T(128)S(1)} %iota_convert_fusion), kind=kOutput, calls=%fused_computation | convolution fusion | flops 236243040 | bytes 2082432 | tf_op jit(solution)/shard_map/dot_general | solution.py:262
  (47 shorter events, 3.4 us)
Async XLA Ops:
  6.5 51.2 %all-gather.5.cloned.1.call-start = ((), (), s32[]{:S(2)}) async-start(), calls=%async_computation.2 | async-start | bytes 4128768 | tf_op jit(solution)/shard_map/all_gather | solution.py:228
  9.6 1.3 copy-start.2
  12.3 68.1 %all-gather.3.cloned.1.call-start = ((), (), s32[]{:S(2)}) async-start(), calls=%async_computation.1 | async-start | bytes 1179648 | tf_op jit(solution)/shard_map/all_gather | solution.py:228
  12.8 2.3 %copy-start.6 = (s32[96]{0:T(128)S(1)}, s32[96]{0:T(128)}, u32[]{:S(2)}) copy-start(s32[96]{0:T(128)} %param.11) | copy-start | bytes 1156
  12.8 2.4 %copy-start.4 = (s32[96,1]{0,1:T(1,128)S(1)}, s32[96,1]{0,1:T(1,128)}, u32[]{:S(2)}) copy-start(s32[96,1]{0,1:T(1,128)} %param.10) | copy-start | bytes 1156
  19.7 26.2 %copy-start.5 = (s32[2,96]{1,0:T(2,128)S(1)}, s32[2,96]{1,0:T(2,128)}, u32[]{:S(2)}) copy-start(s32[2,96]{1,0:T(2,128)} %param.8) | copy-start | bytes 2308
  19.7 26.5 %copy-start.7 = (s32[96]{0:T(128)S(1)}, s32[96]{0:T(128)}, u32[]{:S(2)}) copy-start(s32[96]{0:T(128)} %param.9) | copy-start | bytes 1156
  57.8 2.0 %copy-start = (bf16[64,28672]{1,0:T(8,128)(2,1)S(1)}, bf16[64,28672]{1,0:T(8,128)(2,1)}, u32[]{:S(2)}) copy-start(bf16[64,28672]{1,0:T(8,128)(2,1)} %all-gather.5.cloned.1.call-done.g0_ref.g1_ref) | copy-start | bytes 11010052
  80.4 1.2 copy-start.1
  92.5 27.5 %all-to-all-start = ((f32[32,1,6656]{2,1,0:T(1,128)}), f32[32,1,6656]{2,1,0:T(1,128)S(1)}, u32[]{:S(2)}, u32[]{:S(2)}) async-start(f32[32,1,6656]{2,1,0:T(1,128)} %all_to_all.8), calls=%async_computation | async-start | bytes 1703936 | tf_op jit(solution)/shard_map/all_to_all | solution.py:250
  122.0 1.1 copy-start.3
Sparse Core Ops, SparseCore 0:
  12.4 45.2 all-gather.4
  59.3 21.0 all-gather.2

commit v15 on v13

--- a/solution.py
+++ b/solution.py
@@ -224,7 +224,10 @@
     for c in range(len(bounds) - 1):
         begin, end = bounds[c], bounds[c + 1]
         width = end - begin
-        piece = whiten(spectra[:, :, begin:end]).reshape(spectra.shape[0], 2 * width)
+        raw = spectra[:, :, begin:end]
+        if c:
+            raw, _ = lax.optimization_barrier((raw, piece))
+        piece = whiten(raw).reshape(spectra.shape[0], 2 * width)
         flat = lax.all_gather(piece, "sta", axis=0, tiled=True)
         if c:
             flat, corr = lax.optimization_barrier((flat, corr))

time: 129 us -> 128 us (level)
  no operation moved by 1% of the time
where the time goes in v15:
time: 128 us
  Pallas kernels  53.5 us (42%)
  waiting for transfers between devices  35 us (27%)
  between operations  13.7 us (11%)
  other arithmetic  10.1 us (8%)
  local copies, waits for them, and re-layouts  8.91 us (7%)
  starting transfers between devices  4.43 us (3%)
  matrix products  1.97 us (2%)
    pallas_call x2, Pallas kernels, correlate_stored(): pl.pallas_call(stored_kernel, grid=(blocks,), in_specs=[pl.BlockSpec((2 *...  27.5 us
    pallas_call x1, Pallas kernels, fill_tables(): pl.pallas_call(fill_kernel, grid=(blocks,), in_specs=[pl.BlockSpec((hi_ro...  26 us
    all_to_all x1, waiting for transfers between devices, local(): lax.all_to_all(send_rows.reshape(devices, capacity, corr.shape[1]), ('grp...  23.2 us
    all_gather x2, waiting for transfers between devices, local(): flat = lax.all_gather(piece, 'sta', axis=0, tiled=True)  11.7 us
    unnamed x20, local copies, waits for them, and re-layouts  5.67 us
    sin x2, other arithmetic, angle_table(): return (jnp.cos(theta), jnp.sin(theta))  5.17 us
    all_to_all x1, starting transfers between devices, local(): lax.all_to_all(send_rows.reshape(devices, capacity, corr.shape[1]), ('grp...  4.2 us
    reduce_sum x4, other arithmetic, whiten(): power = jnp.mean(split * split, axis=(1, 3), keepdims=True)  3.28 us
  transfers between devices with their start and end apart: 3, of which 3 were waited for; matrix products, arithmetic and copies ran while one was open for 6% of the time, Pallas kernels for 36%

profile of v15, /device:TPU:0, one launch (start us, length us, event | category | flops | bytes accessed | tf_op | source)
XLA Modules:
  0.0 127.6 jit_solution(580412885071143448)
XLA Ops:
  6.5 2.5 %multiply_reduce_fusion = f32[8,14336]{1,0:T(8,128)S(1)} fusion(f32[8,2,18432]{2,1,0:T(2,128)} %param.6), kind=kLoop, calls=%fused_computation.11 | loop fusion | flops 344064 | bytes 1376256 | tf_op jit(solution)/shard_map/reduce_sum | solution.py:16
  9.0 0.4 reduce_sum.46
  9.4 0.3 reduce_sum.47
  9.7 0.3 mul.128
  10.0 0.3 mul.129
  10.4 0.5 fusion.8
  10.9 0.9 copy.14
  12.1 0.3 multiply_reduce_fusion.1
  13.1 0.7 copy.15
  13.9 0.9 fusion.13
  15.2 4.2 %fusion.4 = (f32[288,896]{1,0:T(8,128)S(1)}, f32[288,896]{1,0:T(8,128)S(1)}) fusion(s32[288]{0:T(512)S(1)} %iota_multiply_fusion), kind=kLoop, calls=%fused_computation.7 | loop fusion | flops 2322432 | bytes 2065536 | tf_op jit(solution)/shard_map/sin | solution.py:24
  19.4 26.0 %shard_map.64 = (bf16[18432,896]{1,0:T(8,128)(2,1)}, bf16[18432,896]{1,0:T(8,128)(2,1)}) custom-call(f32[288,896]{1,0:T(8,128)S(1)} %get-tuple-element.19.chi_ref, f32[288,896]{1,0:T(8,128)S(1)} %get-tuple-element.18.shi_ref, f32[64,896]{1,0:T(8,128)S(1)} %get-tuple-element.25.clo_ref, f32[64,896]{1,0:T(8,128)S(1)} %get-tuple-element.24.slo_ref), custom_call_target="tpu_custom_call" | custom-call | flops 165150720 | bytes 66060288 | tf_op jit(solution)/shard_map/pallas_call | solution.py:104
  45.7 11.5 %all-gather.5.cloned.1.call-done.g0_ref.g1_ref = bf16[64,28672]{1,0:T(8,128)(2,1)} async-done(((bf16[8,28672]{1,0:T(8,128)(2,1)}), bf16[64,28672]{1,0:T(8,128)(2,1)}) %all-gather.5.cloned.1.call-update) | async-done | bytes 3670032 | tf_op jit(solution)/shard_map/all_gather | solution.py:231
  57.3 2.0 %copy-done = bf16[64,28672]{1,0:T(8,128)(2,1)S(1)} copy-done((bf16[64,28672]{1,0:T(8,128)(2,1)S(1)}, bf16[64,28672]{1,0:T(8,128)(2,1)}, u32[]{:S(2)}) %copy-start) | copy-done | bytes 3670040
  59.3 20.4 %shard_map.65.acc_ref = f32[96,1792]{1,0:T(8,128)S(1)} custom-call(bf16[192,64]{1,0:T(8,128)(2,1)S(1)} %add_convert_fusion.pick_ref, bf16[64,28672]{1,0:T(8,128)(2,1)S(1)} %copy-done, bf16[64,28672]{1,0:T(8,128)(2,1)S(1)} %copy-done, bf16[18432,896]{1,0:T(8,128)(2,1)} %get-tuple-element.11.ctab, ...), custom_call_target="tpu_custom_call", output_to_operand_aliasing={{}: (5, {})} | custom-call | flops 4932501504 | bytes 51724288 | tf_op jit(solution)/shard_map/pallas_call | solution.py:133
  79.9 1.2 copy-done.1
  81.1 7.1 %shard_map.66 = f32[96,1792]{1,0:T(8,128)S(1)} custom-call(bf16[192,64]{1,0:T(8,128)(2,1)S(1)} %add_convert_fusion.pick_ref, bf16[64,8192]{1,0:T(8,128)(2,1)S(1)} %copy-done.1, bf16[64,8192]{1,0:T(8,128)(2,1)S(1)} %copy-done.1, bf16[18432,896]{1,0:T(8,128)(2,1)} %get-tuple-element.11.ctab, ...), custom_call_target="tpu_custom_call", output_to_operand_aliasing={{}: (5, {})} | custom-call | flops 1409286144 | bytes 15024128 | tf_op jit(solution)/shard_map/pallas_call | solution.py:133
  88.6 0.6 reverse
  89.7 0.6 fusion.18
  90.3 1.2 reshape.51
  91.4 4.2 %all-to-all-start = ((f32[32,4,1664]{2,1,0:T(4,128)}), f32[32,4,1664]{2,1,0:T(4,128)S(1)}, u32[]{:S(2)}, u32[]{:S(2)}) async-start(f32[32,4,1664]{2,1,0:T(4,128)} %reshape.51), calls=%async_computation | async-start | bytes 1703936 | tf_op jit(solution)/shard_map/all_to_all | solution.py:253
  95.7 23.2 %all-to-all-done = f32[32,4,1664]{2,1,0:T(4,128)S(1)} async-done(((f32[32,4,1664]{2,1,0:T(4,128)}), f32[32,4,1664]{2,1,0:T(4,128)S(1)}, u32[]{:S(2)}, u32[]{:S(2)}) %all-to-all-start) | async-done | bytes 852000 | tf_op jit(solution)/shard_map/all_to_all | solution.py:253
  118.9 0.3 reshape.52
  119.4 1.4 %convolution_add_fusion = f32[96,1601]{1,0:T(8,128)} fusion(f32[96,1601]{1,0:T(8,128)S(1)} %copy-done.3, f32[128,1664]{1,0:T(8,128)S(1)} %reshape.52, f32[128]{0:T(128)S(1)} %slice_reduce_fusion, f32[96]{0:T(128)S(1)} %iota_convert_fusion), kind=kOutput, calls=%fused_computation | convolution fusion | flops 236243040 | bytes 2082432 | tf_op jit(solution)/shard_map/dot_general | solution.py:265
  (47 shorter events, 2.7 us)
Async XLA Ops:
  6.5 3.8 %copy-start.2 = (f32[8,2,18432]{2,1,0:T(2,128)S(1)}, f32[8,2,18432]{2,1,0:T(2,128)}, u32[]{:S(2)}) copy-start(f32[8,2,18432]{2,1,0:T(2,128)} %param.6) | copy-start | bytes 3538948
  6.5 50.7 %all-gather.5.cloned.1.call-start = ((), (), s32[]{:S(2)}) async-start(), calls=%async_computation.2 | async-start | bytes 4128768 | tf_op jit(solution)/shard_map/all_gather | solution.py:231
  10.4 4.4 %copy-start.6 = (s32[96]{0:T(128)S(1)}, s32[96]{0:T(128)}, u32[]{:S(2)}) copy-start(s32[96]{0:T(128)} %param.11) | copy-start | bytes 1156
  10.4 4.5 %copy-start.4 = (s32[96,1]{0,1:T(1,128)S(1)}, s32[96,1]{0,1:T(1,128)}, u32[]{:S(2)}) copy-start(s32[96,1]{0,1:T(1,128)} %param.10) | copy-start | bytes 1156
  11.8 68.1 %all-gather.3.cloned.1.call-start = ((), (), s32[]{:S(2)}) async-start(), calls=%async_computation.1 | async-start | bytes 1179648 | tf_op jit(solution)/shard_map/all_gather | solution.py:231
  12.4 33.0 %copy-start.5 = (s32[2,96]{1,0:T(2,128)S(1)}, s32[2,96]{1,0:T(2,128)}, u32[]{:S(2)}) copy-start(s32[2,96]{1,0:T(2,128)} %param.8) | copy-start | bytes 2308
  12.5 33.1 %copy-start.7 = (s32[96]{0:T(128)S(1)}, s32[96]{0:T(128)}, u32[]{:S(2)}) copy-start(s32[96]{0:T(128)} %param.9) | copy-start | bytes 1156
  57.3 2.0 %copy-start = (bf16[64,28672]{1,0:T(8,128)(2,1)S(1)}, bf16[64,28672]{1,0:T(8,128)(2,1)}, u32[]{:S(2)}) copy-start(bf16[64,28672]{1,0:T(8,128)(2,1)} %all-gather.5.cloned.1.call-done.g0_ref.g1_ref) | copy-start | bytes 11010052
  79.9 1.2 copy-start.1
  89.7 29.7 %copy-start.3 = (f32[96,1601]{1,0:T(8,128)S(1)}, f32[96,1601]{1,0:T(8,128)}, u32[]{:S(2)}) copy-start(f32[96,1601]{1,0:T(8,128)} %param.7) | copy-start | bytes 1844356
  91.4 27.5 %all-to-all-start = ((f32[32,4,1664]{2,1,0:T(4,128)}), f32[32,4,1664]{2,1,0:T(4,128)S(1)}, u32[]{:S(2)}, u32[]{:S(2)}) async-start(f32[32,4,1664]{2,1,0:T(4,128)} %reshape.51), calls=%async_computation | async-start | bytes 1703936 | tf_op jit(solution)/shard_map/all_to_all | solution.py:253
Sparse Core Ops, SparseCore 0:
  11.9 45.2 all-gather.4
  58.8 21.0 all-gather.2

commit v16 on v15

--- a/solution.py
+++ b/solution.py
@@ -217,7 +217,7 @@
     lo_all = angle_table(lax.iota(jnp.int32, LOW), lag_pad, total_bins)
     blocks = total_bins // FBLOCK
     assert total_bins % FBLOCK == 0
-    lead = max(1, min(blocks - 1, (7 * blocks + 4) // 9))
+    lead = max(1, min(blocks - 1, (2 * blocks + 1) // 3))
     bounds = [0, lead * FBLOCK, total_bins] if blocks > 1 else [0, total_bins]
     corr = jnp.zeros((pair_count, 2 * lag_pad), jnp.float32)
     stored = fill_tables((hi_all[0], hi_all[1], lo_all[0], lo_all[1]))
@@ -228,7 +228,11 @@
         if c:
             raw, _ = lax.optimization_barrier((raw, piece))
         piece = whiten(raw).reshape(spectra.shape[0], 2 * width)
-        flat = lax.all_gather(piece, "sta", axis=0, tiled=True)
+        if c:
+            copies = jnp.broadcast_to(piece[None], (members,) + piece.shape)
+            flat = lax.all_to_all(copies, "sta", 0, 0, tiled=True).reshape(group_sta, 2 * width)
+        else:
+            flat = lax.all_gather(piece, "sta", axis=0, tiled=True)
         if c:
             flat, corr = lax.optimization_barrier((flat, corr))
         corr = correlate_stored(picks, flat, stored, corr, begin)

time: 128 us -> 150 us (1.17)
  waiting for transfers between devices: 35 us -> 52.7 us
  starting transfers between devices: 4.43 us -> 9.25 us
    all_gather x2 -> x1, waiting for transfers between devices: 11.7 us -> 29.5 us  [local(): flat = lax.all_gather(piece, 'sta', axis=0, tiled=True)]
    all_to_all x0 -> x1, starting transfers between devices: none -> 6.49 us  [local(): lax.all_to_all(copies, 'sta', 0, 0, tiled=True)]
    unnamed x20 -> x18, local copies, waits for them, and re-layouts: 5.67 us -> 4.04 us
  transfers between devices with their start and end apart: 3 -> 3, of which waited for: 3 -> 2; matrix products, arithmetic and copies ran while one was open for 6% -> 6% of each run, Pallas kernels for 36% -> 29%
where the time goes in v16:
time: 150 us
  Pallas kernels  53.5 us (36%)
  waiting for transfers between devices  52.7 us (35%)
  between operations  13.7 us (9%)
  other arithmetic  10 us (7%)
  starting transfers between devices  9.25 us (6%)
  local copies, waits for them, and re-layouts  8.52 us (6%)
  matrix products  1.97 us (1%)
    all_gather x1, waiting for transfers between devices, local(): flat = lax.all_gather(piece, 'sta', axis=0, tiled=True)  29.5 us
    pallas_call x2, Pallas kernels, correlate_stored(): pl.pallas_call(stored_kernel, grid=(blocks,), in_specs=[pl.BlockSpec((2 *...  27.6 us
    pallas_call x1, Pallas kernels, fill_tables(): pl.pallas_call(fill_kernel, grid=(blocks,), in_specs=[pl.BlockSpec((hi_ro...  26 us
    all_to_all x1, waiting for transfers between devices, local(): lax.all_to_all(send_rows.reshape(devices, capacity, corr.shape[1]), ('grp...  23.2 us
    all_to_all x1, starting transfers between devices, local(): lax.all_to_all(copies, 'sta', 0, 0, tiled=True)  6.49 us
    sin x2, other arithmetic, angle_table(): return (jnp.cos(theta), jnp.sin(theta))  5.17 us
    unnamed x18, local copies, waits for them, and re-layouts  4.04 us
    reduce_sum x4, other arithmetic, whiten(): power = jnp.mean(split * split, axis=(1, 3), keepdims=True)  3.2 us
  transfers between devices with their start and end apart: 3, of which 2 were waited for; matrix products, arithmetic and copies ran while one was open for 6% of the time, Pallas kernels for 29%

profile of v16, /device:TPU:0, one launch (start us, length us, event | category | flops | bytes accessed | tf_op | source)
XLA Modules:
  0.0 149.7 jit_solution(4644077999168294298)
XLA Ops:
  6.5 2.2 %multiply_reduce_fusion = f32[8,12288]{1,0:T(8,128)S(1)} fusion(f32[8,2,18432]{2,1,0:T(2,128)} %param.6), kind=kLoop, calls=%fused_computation.12 | loop fusion | flops 294912 | bytes 1179648 | tf_op jit(solution)/shard_map/reduce_sum | solution.py:16
  8.7 0.3 reduce_sum.46
  9.0 0.3 reduce_sum.47
  9.7 0.3 mul.129
  9.9 0.3 copy-done.1
  10.3 0.4 fusion.8
  10.7 1.0 copy.13
  11.7 0.5 multiply_reduce_fusion.1
  13.2 1.2 broadcast_in_dim.11
  14.5 6.5 %all-to-all-start = ((bf16[8,8,12288]{2,1,0:T(8,128)(2,1)}), bf16[8,8,12288]{2,1,0:T(8,128)(2,1)S(1)}, u32[]{:S(2)}, u32[]{:S(2)}) async-start(bf16[8,8,12288]{2,1,0:T(8,128)(2,1)} %broadcast_in_dim.11), calls=%async_computation | async-start | bytes 3145728 | tf_op jit(solution)/shard_map/all_to_all | solution.py:233
  21.3 0.9 fusion.13
  22.3 4.2 %fusion.4 = (f32[288,896]{1,0:T(8,128)S(1)}, f32[288,896]{1,0:T(8,128)S(1)}) fusion(s32[288]{0:T(512)S(1)} %iota_multiply_fusion), kind=kLoop, calls=%fused_computation.7 | loop fusion | flops 2322432 | bytes 2065536 | tf_op jit(solution)/shard_map/sin | solution.py:24
  26.5 26.0 %shard_map.64 = (bf16[18432,896]{1,0:T(8,128)(2,1)}, bf16[18432,896]{1,0:T(8,128)(2,1)}) custom-call(f32[288,896]{1,0:T(8,128)S(1)} %get-tuple-element.19.chi_ref, f32[288,896]{1,0:T(8,128)S(1)} %get-tuple-element.18.shi_ref, f32[64,896]{1,0:T(8,128)S(1)} %get-tuple-element.25.clo_ref, f32[64,896]{1,0:T(8,128)S(1)} %get-tuple-element.24.slo_ref), custom_call_target="tpu_custom_call" | custom-call | flops 165150720 | bytes 66060288 | tf_op jit(solution)/shard_map/pallas_call | solution.py:104
  52.8 29.5 %all-gather.2.cloned.1.call-done.g0_ref.g1_ref = bf16[64,24576]{1,0:T(8,128)(2,1)} async-done(((bf16[8,24576]{1,0:T(8,128)(2,1)}), bf16[64,24576]{1,0:T(8,128)(2,1)}) %all-gather.2.cloned.1.call-update) | async-done | bytes 3145744 | tf_op jit(solution)/shard_map/all_gather | solution.py:235
  82.4 1.9 %copy-done = bf16[64,24576]{1,0:T(8,128)(2,1)S(1)} copy-done((bf16[64,24576]{1,0:T(8,128)(2,1)S(1)}, bf16[64,24576]{1,0:T(8,128)(2,1)}, u32[]{:S(2)}) %copy-start) | copy-done | bytes 3145752
  84.2 17.5 %shard_map.65.acc_ref = f32[96,1792]{1,0:T(8,128)S(1)} custom-call(bf16[192,64]{1,0:T(8,128)(2,1)S(1)} %add_convert_fusion.pick_ref, bf16[64,24576]{1,0:T(8,128)(2,1)S(1)} %copy-done, bf16[64,24576]{1,0:T(8,128)(2,1)S(1)} %copy-done, bf16[18432,896]{1,0:T(8,128)(2,1)} %get-tuple-element.11.ctab, ...), custom_call_target="tpu_custom_call", output_to_operand_aliasing={{}: (5, {})} | custom-call | flops 4227858432 | bytes 44384256 | tf_op jit(solution)/shard_map/pallas_call | solution.py:133
  101.7 10.1 %shard_map.66 = f32[96,1792]{1,0:T(8,128)S(1)} custom-call(bf16[192,64]{1,0:T(8,128)(2,1)S(1)} %add_convert_fusion.pick_ref, bf16[64,12288]{1,0:T(8,128)(2,1)S(1)} %bitcast.22, bf16[64,12288]{1,0:T(8,128)(2,1)S(1)} %bitcast.23, bf16[18432,896]{1,0:T(8,128)(2,1)} %get-tuple-element.11.ctab, ...), custom_call_target="tpu_custom_call", output_to_operand_aliasing={{}: (5, {})} | custom-call | flops 2113929216 | bytes 22364160 | tf_op jit(solution)/shard_map/pallas_call | solution.py:133
  112.2 0.6 reverse
  113.2 0.6 fusion.18
  113.9 1.2 reshape.52
  115.0 2.8 %all-to-all-start.1 = ((f32[32,4,1664]{2,1,0:T(4,128)}), f32[32,4,1664]{2,1,0:T(4,128)S(1)}, u32[]{:S(2)}, u32[]{:S(2)}) async-start(f32[32,4,1664]{2,1,0:T(4,128)} %reshape.52), calls=%async_computation.1 | async-start | bytes 1703936 | tf_op jit(solution)/shard_map/all_to_all | solution.py:257
  117.8 23.2 %all-to-all-done.1 = f32[32,4,1664]{2,1,0:T(4,128)S(1)} async-done(((f32[32,4,1664]{2,1,0:T(4,128)}), f32[32,4,1664]{2,1,0:T(4,128)S(1)}, u32[]{:S(2)}, u32[]{:S(2)}) %all-to-all-start.1) | async-done | bytes 852000 | tf_op jit(solution)/shard_map/all_to_all | solution.py:257
  141.0 0.3 reshape.53
  141.5 1.4 convolution_add_fusion
  (45 shorter events, 2.9 us)
Async XLA Ops:
  6.5 75.8 %all-gather.2.cloned.1.call-start = ((), (), s32[]{:S(2)}) async-start(), calls=%async_computation.2 | async-start | bytes 3538944 | tf_op jit(solution)/shard_map/all_gather | solution.py:235
  9.0 1.3 copy-start.1
  14.5 6.5 %copy-start.5 = (s32[96]{0:T(128)S(1)}, s32[96]{0:T(128)}, u32[]{:S(2)}) copy-start(s32[96]{0:T(128)} %param.11) | copy-start | bytes 1156
  14.5 6.6 %copy-start.3 = (s32[96,1]{0,1:T(1,128)S(1)}, s32[96,1]{0,1:T(1,128)}, u32[]{:S(2)}) copy-start(s32[96,1]{0,1:T(1,128)} %param.10) | copy-start | bytes 1156
  14.5 87.2 %all-to-all-start = ((bf16[8,8,12288]{2,1,0:T(8,128)(2,1)}), bf16[8,8,12288]{2,1,0:T(8,128)(2,1)S(1)}, u32[]{:S(2)}, u32[]{:S(2)}) async-start(bf16[8,8,12288]{2,1,0:T(8,128)(2,1)} %broadcast_in_dim.11), calls=%async_computation | async-start | bytes 3145728 | tf_op jit(solution)/shard_map/all_to_all | solution.py:233
  26.5 26.0 %copy-start.4 = (s32[2,96]{1,0:T(2,128)S(1)}, s32[2,96]{1,0:T(2,128)}, u32[]{:S(2)}) copy-start(s32[2,96]{1,0:T(2,128)} %param.8) | copy-start | bytes 2308
  26.5 26.3 %copy-start.6 = (s32[96]{0:T(128)S(1)}, s32[96]{0:T(128)}, u32[]{:S(2)}) copy-start(s32[96]{0:T(128)} %param.9) | copy-start | bytes 1156
  82.3 1.9 %copy-start = (bf16[64,24576]{1,0:T(8,128)(2,1)S(1)}, bf16[64,24576]{1,0:T(8,128)(2,1)}, u32[]{:S(2)}) copy-start(bf16[64,24576]{1,0:T(8,128)(2,1)} %all-gather.2.cloned.1.call-done.g0_ref.g1_ref) | copy-start | bytes 9437188
  115.0 26.5 %copy-start.2 = (f32[96,1601]{1,0:T(8,128)S(1)}, f32[96,1601]{1,0:T(8,128)}, u32[]{:S(2)}) copy-start(f32[96,1601]{1,0:T(8,128)} %param.7) | copy-start | bytes 1844356
  115.0 26.0 %all-to-all-start.1 = ((f32[32,4,1664]{2,1,0:T(4,128)}), f32[32,4,1664]{2,1,0:T(4,128)S(1)}, u32[]{:S(2)}, u32[]{:S(2)}) async-start(f32[32,4,1664]{2,1,0:T(4,128)} %reshape.52), calls=%async_computation.1 | async-start | bytes 1703936 | tf_op jit(solution)/shard_map/all_to_all | solution.py:257
Sparse Core Ops, SparseCore 0:
  11.8 70.4 all-gather.1

commit v17 on v15

--- a/solution.py
+++ b/solution.py
@@ -121,24 +121,24 @@
     )(cos_hi, sin_hi, cos_lo, sin_lo)
 
 
-def correlate_stored(picks, flat, stored, acc, begin):
+def correlate_stored(picks, flat, stored, acc, begin, fblock):
     ctab, stab = stored
     pair_count = picks.shape[0] // 2
     group_sta = flat.shape[0]
     lag_pad = ctab.shape[1]
     width = flat.shape[1] // 2
-    assert width % FBLOCK == 0 and begin % FBLOCK == 0
-    blocks = width // FBLOCK
-    skip = begin // FBLOCK
+    assert width % fblock == 0 and begin % fblock == 0
+    blocks = width // fblock
+    skip = begin // fblock
     return pl.pallas_call(
         stored_kernel,
         grid=(blocks,),
         in_specs=[
             pl.BlockSpec((2 * pair_count, group_sta), lambda i: (0, 0)),
-            pl.BlockSpec((group_sta, FBLOCK), lambda i: (0, i)),
-            pl.BlockSpec((group_sta, FBLOCK), lambda i: (0, i + blocks)),
-            pl.BlockSpec((FBLOCK, lag_pad), lambda i: (i + skip, 0)),
-            pl.BlockSpec((FBLOCK, lag_pad), lambda i: (i + skip, 0)),
+            pl.BlockSpec((group_sta, fblock), lambda i: (0, i)),
+            pl.BlockSpec((group_sta, fblock), lambda i: (0, i + blocks)),
+            pl.BlockSpec((fblock, lag_pad), lambda i: (i + skip, 0)),
+            pl.BlockSpec((fblock, lag_pad), lambda i: (i + skip, 0)),
             pl.BlockSpec((pair_count, 2 * lag_pad), lambda i: (0, 0)),
         ],
         out_specs=pl.BlockSpec((pair_count, 2 * lag_pad), lambda i: (0, 0)),
@@ -231,7 +231,7 @@
         flat = lax.all_gather(piece, "sta", axis=0, tiled=True)
         if c:
             flat, corr = lax.optimization_barrier((flat, corr))
-        corr = correlate_stored(picks, flat, stored, corr, begin)
+        corr = correlate_stored(picks, flat, stored, corr, begin, FBLOCK if c == 0 else FBLOCK // 2)
     even = corr[:, : side + 1]
     odd = corr[:, lag_pad : lag_pad + side + 1]
     corr = jnp.concatenate([(even + odd)[:, :0:-1], even - odd], axis=1)

time: 128 us -> 128 us (level)
  no operation moved by 1% of the time
where the time goes in v17:
time: 128 us
  Pallas kernels  54 us (42%)
  waiting for transfers between devices  35 us (27%)
  between operations  13.7 us (11%)
  other arithmetic  10.1 us (8%)
  local copies, waits for them, and re-layouts  8.91 us (7%)
  starting transfers between devices  4.44 us (3%)
  matrix products  1.97 us (2%)
    pallas_call x2, Pallas kernels, correlate_stored(): pl.pallas_call(stored_kernel, grid=(blocks,), in_specs=[pl.BlockSpec((2 *...  28 us
    pallas_call x1, Pallas kernels, fill_tables(): pl.pallas_call(fill_kernel, grid=(blocks,), in_specs=[pl.BlockSpec((hi_ro...  26 us
    all_to_all x1, waiting for transfers between devices, local(): lax.all_to_all(send_rows.reshape(devices, capacity, corr.shape[1]), ('grp...  23.2 us
    all_gather x2, waiting for transfers between devices, local(): flat = lax.all_gather(piece, 'sta', axis=0, tiled=True)  11.7 us
    unnamed x20, local copies, waits for them, and re-layouts  5.67 us
    sin x2, other arithmetic, angle_table(): return (jnp.cos(theta), jnp.sin(theta))  5.17 us
    all_to_all x1, starting transfers between devices, local(): lax.all_to_all(send_rows.reshape(devices, capacity, corr.shape[1]), ('grp...  4.21 us
    reduce_sum x4, other arithmetic, whiten(): power = jnp.mean(split * split, axis=(1, 3), keepdims=True)  3.28 us
  transfers between devices with their start and end apart: 3, of which 3 were waited for; matrix products, arithmetic and copies ran while one was open for 6% of the time, Pallas kernels for 36%

profile of v17, /device:TPU:0, one launch (start us, length us, event | category | flops | bytes accessed | tf_op | source)
XLA Modules:
  0.0 128.1 jit_solution(4856784166343561255)
XLA Ops:
  6.5 2.5 %multiply_reduce_fusion = f32[8,14336]{1,0:T(8,128)S(1)} fusion(f32[8,2,18432]{2,1,0:T(2,128)} %param.6), kind=kLoop, calls=%fused_computation.11 | loop fusion | flops 344064 | bytes 1376256 | tf_op jit(solution)/shard_map/reduce_sum | solution.py:16
  9.0 0.4 reduce_sum.46
  9.4 0.3 reduce_sum.47
  9.7 0.3 mul.128
  10.0 0.3 mul.129
  10.4 0.5 fusion.8
  10.9 0.9 copy.14
  12.1 0.3 multiply_reduce_fusion.1
  13.1 0.7 copy.15
  13.9 0.9 fusion.13
  15.2 4.2 %fusion.4 = (f32[288,896]{1,0:T(8,128)S(1)}, f32[288,896]{1,0:T(8,128)S(1)}) fusion(s32[288]{0:T(512)S(1)} %iota_multiply_fusion), kind=kLoop, calls=%fused_computation.7 | loop fusion | flops 2322432 | bytes 2065536 | tf_op jit(solution)/shard_map/sin | solution.py:24
  19.4 26.0 %shard_map.64 = (bf16[18432,896]{1,0:T(8,128)(2,1)}, bf16[18432,896]{1,0:T(8,128)(2,1)}) custom-call(f32[288,896]{1,0:T(8,128)S(1)} %get-tuple-element.19.chi_ref, f32[288,896]{1,0:T(8,128)S(1)} %get-tuple-element.18.shi_ref, f32[64,896]{1,0:T(8,128)S(1)} %get-tuple-element.25.clo_ref, f32[64,896]{1,0:T(8,128)S(1)} %get-tuple-element.24.slo_ref), custom_call_target="tpu_custom_call" | custom-call | flops 165150720 | bytes 66060288 | tf_op jit(solution)/shard_map/pallas_call | solution.py:104
  45.7 11.5 %all-gather.5.cloned.1.call-done.g0_ref.g1_ref = bf16[64,28672]{1,0:T(8,128)(2,1)} async-done(((bf16[8,28672]{1,0:T(8,128)(2,1)}), bf16[64,28672]{1,0:T(8,128)(2,1)}) %all-gather.5.cloned.1.call-update) | async-done | bytes 3670032 | tf_op jit(solution)/shard_map/all_gather | solution.py:231
  57.3 2.0 %copy-done = bf16[64,28672]{1,0:T(8,128)(2,1)S(1)} copy-done((bf16[64,28672]{1,0:T(8,128)(2,1)S(1)}, bf16[64,28672]{1,0:T(8,128)(2,1)}, u32[]{:S(2)}) %copy-start) | copy-done | bytes 3670040
  59.3 20.4 %shard_map.65.acc_ref = f32[96,1792]{1,0:T(8,128)S(1)} custom-call(bf16[192,64]{1,0:T(8,128)(2,1)S(1)} %add_convert_fusion.pick_ref, bf16[64,28672]{1,0:T(8,128)(2,1)S(1)} %copy-done, bf16[64,28672]{1,0:T(8,128)(2,1)S(1)} %copy-done, bf16[18432,896]{1,0:T(8,128)(2,1)} %get-tuple-element.11.ctab, ...), custom_call_target="tpu_custom_call", output_to_operand_aliasing={{}: (5, {})} | custom-call | flops 4932501504 | bytes 51724288 | tf_op jit(solution)/shard_map/pallas_call | solution.py:133
  79.9 1.2 copy-done.1
  81.1 7.6 %shard_map.66 = f32[96,1792]{1,0:T(8,128)S(1)} custom-call(bf16[192,64]{1,0:T(8,128)(2,1)S(1)} %add_convert_fusion.pick_ref, bf16[64,8192]{1,0:T(8,128)(2,1)S(1)} %copy-done.1, bf16[64,8192]{1,0:T(8,128)(2,1)S(1)} %copy-done.1, bf16[18432,896]{1,0:T(8,128)(2,1)} %get-tuple-element.11.ctab, ...), custom_call_target="tpu_custom_call", output_to_operand_aliasing={{}: (5, {})} | custom-call | flops 1409286144 | bytes 15024128 | tf_op jit(solution)/shard_map/pallas_call | solution.py:133
  89.1 0.6 reverse
  90.2 0.6 fusion.18
  90.8 1.2 reshape.51
  91.9 4.2 %all-to-all-start = ((f32[32,4,1664]{2,1,0:T(4,128)}), f32[32,4,1664]{2,1,0:T(4,128)S(1)}, u32[]{:S(2)}, u32[]{:S(2)}) async-start(f32[32,4,1664]{2,1,0:T(4,128)} %reshape.51), calls=%async_computation | async-start | bytes 1703936 | tf_op jit(solution)/shard_map/all_to_all | solution.py:253
  96.2 23.2 %all-to-all-done = f32[32,4,1664]{2,1,0:T(4,128)S(1)} async-done(((f32[32,4,1664]{2,1,0:T(4,128)}), f32[32,4,1664]{2,1,0:T(4,128)S(1)}, u32[]{:S(2)}, u32[]{:S(2)}) %all-to-all-start) | async-done | bytes 852000 | tf_op jit(solution)/shard_map/all_to_all | solution.py:253
  119.4 0.3 reshape.52
  119.9 1.4 %convolution_add_fusion = f32[96,1601]{1,0:T(8,128)} fusion(f32[96,1601]{1,0:T(8,128)S(1)} %copy-done.3, f32[128,1664]{1,0:T(8,128)S(1)} %reshape.52, f32[128]{0:T(128)S(1)} %slice_reduce_fusion, f32[96]{0:T(128)S(1)} %iota_convert_fusion), kind=kOutput, calls=%fused_computation | convolution fusion | flops 236243040 | bytes 2082432 | tf_op jit(solution)/shard_map/dot_general | solution.py:265
  (47 shorter events, 2.7 us)
Async XLA Ops:
  6.5 3.8 %copy-start.2 = (f32[8,2,18432]{2,1,0:T(2,128)S(1)}, f32[8,2,18432]{2,1,0:T(2,128)}, u32[]{:S(2)}) copy-start(f32[8,2,18432]{2,1,0:T(2,128)} %param.6) | copy-start | bytes 3538948
  6.5 50.7 %all-gather.5.cloned.1.call-start = ((), (), s32[]{:S(2)}) async-start(), calls=%async_computation.2 | async-start | bytes 4128768 | tf_op jit(solution)/shard_map/all_gather | solution.py:231
  10.4 4.4 %copy-start.6 = (s32[96]{0:T(128)S(1)}, s32[96]{0:T(128)}, u32[]{:S(2)}) copy-start(s32[96]{0:T(128)} %param.11) | copy-start | bytes 1156
  10.4 4.5 %copy-start.4 = (s32[96,1]{0,1:T(1,128)S(1)}, s32[96,1]{0,1:T(1,128)}, u32[]{:S(2)}) copy-start(s32[96,1]{0,1:T(1,128)} %param.10) | copy-start | bytes 1156
  11.8 68.1 %all-gather.3.cloned.1.call-start = ((), (), s32[]{:S(2)}) async-start(), calls=%async_computation.1 | async-start | bytes 1179648 | tf_op jit(solution)/shard_map/all_gather | solution.py:231
  12.4 33.0 %copy-start.5 = (s32[2,96]{1,0:T(2,128)S(1)}, s32[2,96]{1,0:T(2,128)}, u32[]{:S(2)}) copy-start(s32[2,96]{1,0:T(2,128)} %param.8) | copy-start | bytes 2308
  12.5 33.1 %copy-start.7 = (s32[96]{0:T(128)S(1)}, s32[96]{0:T(128)}, u32[]{:S(2)}) copy-start(s32[96]{0:T(128)} %param.9) | copy-start | bytes 1156
  57.3 2.0 %copy-start = (bf16[64,28672]{1,0:T(8,128)(2,1)S(1)}, bf16[64,28672]{1,0:T(8,128)(2,1)}, u32[]{:S(2)}) copy-start(bf16[64,28672]{1,0:T(8,128)(2,1)} %all-gather.5.cloned.1.call-done.g0_ref.g1_ref) | copy-start | bytes 11010052
  79.9 1.2 copy-start.1
  90.1 29.7 %copy-start.3 = (f32[96,1601]{1,0:T(8,128)S(1)}, f32[96,1601]{1,0:T(8,128)}, u32[]{:S(2)}) copy-start(f32[96,1601]{1,0:T(8,128)} %param.7) | copy-start | bytes 1844356
  91.9 27.5 %all-to-all-start = ((f32[32,4,1664]{2,1,0:T(4,128)}), f32[32,4,1664]{2,1,0:T(4,128)S(1)}, u32[]{:S(2)}, u32[]{:S(2)}) async-start(f32[32,4,1664]{2,1,0:T(4,128)} %reshape.51), calls=%async_computation | async-start | bytes 1703936 | tf_op jit(solution)/shard_map/all_to_all | solution.py:253
Sparse Core Ops, SparseCore 0:
  11.9 45.2 all-gather.4
  58.8 21.0 all-gather.2
